TPU v7x, 32 devices: a whole 2x2x4 slice. The times are simulated.
32 devices in a mesh: clips: 2 (over y), seq: 4 (over z), pair: 4 (over x, core).
Axes of the slice: x: 2, y: 2, z: 4, core: 2. Of those that a mesh axis runs over, the one named last changes fastest.
Arguments:
- queries: bfloat16 [4096, 5120], P(('clips', 'seq', 'pair')), parts along dimension 0, may hold values from -34 to 34
- key_rows: bfloat16 [4096, 5120], P(('clips', 'seq', 'pair')), parts along dimension 0, may hold values from -6 to 6
- value_rows: bfloat16 [4096, 5120], P(('clips', 'seq', 'pair')), parts along dimension 0, may hold values from -6 to 6
- block_lists: int32 [40, 16, 2], replicated, may hold values from 0 to 15, as said below
- block_counts: int32 [40, 16], replicated, may hold values from 1 to 2, as said below
Outputs:
- attended: bfloat16 [4096, 5120], P(('clips', 'seq', 'pair')), parts along dimension 0
There are 2 independent parts, one for each index of `clips`. A program takes and returns all parts, laid end to end along the dimension named above; an argument that names none is the same for every part. Nothing has to cross between parts.
Inputs may be any that keep to these rules, and one draw needn't show every extreme that they name: `block_lists`: for each head and query block the entries are distinct and the first one is the query block itself; entries at positions block_counts[h, b] and beyond are not used. `block_counts`: some query block of some head has exactly 2 live key blocks.
All inputs are finite; a program needn't handle non-finite values.
Results may differ from a plain program's by a relative error of at most 0.0055.
Values may be sent and summed in bfloat16 or wider, within the bound.
No kernel may reach another device: no remote copies, remote signals or barrier semaphores. Data moves between devices by JAX's collectives and lax.ppermute only.
A program may use at most 128 MiB of HBM per device.

v0:
```python
import math

import jax
import jax.numpy as jnp
from jax import lax
from jax.sharding import PartitionSpec as P

HEADS = 40
HD = 128
BLOCK = 128


def body(queries, key_rows, value_rows, block_lists, block_counts):
    seq_count = lax.axis_size("seq")
    pair_count = lax.axis_size("pair")
    seq_place = lax.axis_index("seq")
    pair_place = lax.axis_index("pair")
    tok_rows = queries.shape[0]
    local_blocks = tok_rows // BLOCK
    block_total = block_lists.shape[1]
    slot_count = -(-HEADS // seq_count)
    padded_heads = slot_count * seq_count
    score_scale = 1.0 / math.sqrt(HD)
    head_grid = jnp.minimum(jnp.arange(padded_heads, dtype=jnp.int32), HEADS)

    def to_owner(rows_in):
        widened = jnp.pad(
            rows_in.reshape(tok_rows, HEADS, HD), ((0, 0), (0, padded_heads - HEADS), (0, 0))
        )
        return widened.reshape(tok_rows, slot_count, seq_count, HD)

    query_grid = to_owner(queries)
    key_grid = to_owner(key_rows)
    value_grid = to_owner(value_rows)
    query_own = lax.all_to_all(query_grid, "seq", split_axis=2, concat_axis=0, tiled=True)

    def widen_grid(grid_rows):
        copies = jnp.broadcast_to(
            grid_rows[:, :, :, None, :], (tok_rows, slot_count, seq_count, pair_count, HD)
        )
        return copies.reshape(tok_rows, slot_count, seq_count * pair_count, HD)

    key_own, value_own = (
        lax.all_to_all(
            widen_grid(key_grid), ("seq", "pair"), split_axis=2, concat_axis=0, tiled=True
        ),
        lax.all_to_all(
            widen_grid(value_grid), ("seq", "pair"), split_axis=2, concat_axis=0, tiled=True
        ),
    )
    own_count = seq_count * local_blocks
    local_index = jnp.arange(own_count, dtype=jnp.int32)
    own_blocks = (
        local_index // local_blocks * pair_count + pair_place
    ) * local_blocks + local_index % local_blocks

    def attend_slot(slot_idx, result):
        head_id = head_grid[slot_idx * seq_count + seq_place]
        head_live = head_id < HEADS
        head_safe = jnp.minimum(head_id, HEADS - 1)
        own_lists = jnp.take(block_lists[head_safe], own_blocks, axis=0)
        counts = jnp.where(head_live, jnp.take(block_counts[head_safe], own_blocks), 0)
        query_slot = lax.dynamic_index_in_dim(query_own, slot_idx, 1, False).reshape(
            own_count, BLOCK, HD
        )
        key_slot = lax.dynamic_index_in_dim(key_own, slot_idx, 1, False).reshape(
            block_total, BLOCK, HD
        )
        value_slot = lax.dynamic_index_in_dim(value_own, slot_idx, 1, False).reshape(
            block_total, BLOCK, HD
        )
        visit_count = jnp.max(counts)

        def visit_list(position, running):
            run_max, run_sum, run_acc = running
            picked = lax.dynamic_index_in_dim(own_lists, position, 1, False)
            key_block = jnp.take(key_slot, picked, axis=0)
            value_block = jnp.take(value_slot, picked, axis=0)
            scores = (
                jnp.einsum(
                    "qad,qbd->qab", query_slot, key_block, preferred_element_type=jnp.float32
                )
                * score_scale
            )
            live_rows = (position < counts)[:, None]
            new_max = jnp.where(live_rows, jnp.maximum(run_max, jnp.max(scores, axis=2)), run_max)
            raised = jnp.where(live_rows[:, :, None], jnp.exp(scores - new_max[:, :, None]), 0.0)
            shrink = jnp.exp(run_max - new_max)
            run_sum = run_sum * shrink + jnp.sum(raised, axis=2)
            run_acc = run_acc * shrink[:, :, None] + jnp.einsum(
                "qab,qbd->qad",
                raised.astype(jnp.bfloat16),
                value_block,
                preferred_element_type=jnp.float32,
            )
            return (new_max, run_sum, run_acc)

        start_state = (
            jnp.full((own_count, BLOCK), -1e30, jnp.float32),
            jnp.zeros((own_count, BLOCK), jnp.float32),
            jnp.zeros((own_count, BLOCK, HD), jnp.float32),
        )
        run_max, run_sum, run_acc = lax.fori_loop(0, visit_count, visit_list, start_state)
        mixed_out = (run_acc / jnp.where(run_sum > 0.0, run_sum, 1.0)[:, :, None]).astype(
            jnp.bfloat16
        )
        return lax.dynamic_update_index_in_dim(
            result, mixed_out.reshape(own_count * BLOCK, 1, HD), slot_idx, 1
        )

    result = jnp.zeros((own_count * BLOCK, slot_count, 1, HD), jnp.bfloat16)
    result = lax.fori_loop(0, slot_count, attend_slot, result)
    returned = lax.all_to_all(result, "seq", split_axis=0, concat_axis=2, tiled=True)
    return returned.reshape(tok_rows, padded_heads * HD)[:, : HEADS * HD]


def solution(mesh):
    placed = (
        P(("clips", "seq", "pair"), None),
        P(("clips", "seq", "pair"), None),
        P(("clips", "seq", "pair"), None),
        P(),
        P(),
    )
    return jax.shard_map(
        body,
        mesh=mesh,
        in_specs=placed,
        out_specs=P(("clips", "seq", "pair"), None),
        check_vma=False,
    )
```

profile of v0, /device:TPU:0, one launch (start us, length us, event | category | flops | bytes accessed | tf_op | source)
XLA Modules:
  0.0 453.7 jit_solution(4083131081481431631)
XLA Ops:
  0.0 1.8 copy.76
  1.8 1.5 copy.77
  3.2 6.3 %all-to-all-start.2 = ((bf16[128,10,4,128]{3,0,1,2:T(8,128)(2,1)}), bf16[128,10,4,128]{3,0,1,2:T(8,128)(2,1)S(1)}, u32[]{:S(2)}, u32[]{:S(2)}) async-start(bf16[128,10,4,128]{3,0,1,2:T(8,128)(2,1)} %copy.77), calls=%async_computation.2 | async-start | bytes 2621440 | tf_op jit(solution)/shard_map/all_to_all | solution.py:35
  9.5 2.8 broadcast_in_dim.88
  12.4 1.4 copy.74
  13.7 27.1 %all-to-all-done.2 = bf16[128,10,4,128]{3,0,1,2:T(8,128)(2,1)S(1)} async-done(((bf16[128,10,4,128]{3,0,1,2:T(8,128)(2,1)}), bf16[128,10,4,128]{3,0,1,2:T(8,128)(2,1)S(1)}, u32[]{:S(2)}, u32[]{:S(2)}) %all-to-all-start.2) | async-done | bytes 1310752 | tf_op jit(solution)/shard_map/all_to_all | solution.py:35
  40.9 5.0 %broadcast_in_dim.89 = bf16[128,10,4,4,128]{4,0,1,3,2:T(8,128)(2,1)} broadcast(bf16[128,10,4,128]{3,0,1,2:T(8,128)(2,1)} %copy.74), dimensions={0,1,2,4} | broadcast | bytes 6553600 | tf_op jit(solution)/shard_map/broadcast_in_dim | solution.py:38
  45.8 4.6 %all-to-all-start.1 = ((bf16[128,10,16,128]{3,0,1,2:T(8,128)(2,1)}), bf16[128,10,16,128]{3,0,1,2:T(8,128)(2,1)}, u32[]{:S(2)}, u32[]{:S(2)}) async-start(bf16[128,10,16,128]{3,0,1,2:T(8,128)(2,1)} %bitcast.74), calls=%async_computation.1 | async-start | bytes 10485760 | tf_op jit(solution)/shard_map/all_to_all | solution.py:47
  50.4 2.8 broadcast_in_dim.86
  53.3 1.4 copy.72
  54.6 91.7 %all-to-all-done.1 = bf16[128,10,16,128]{3,0,1,2:T(8,128)(2,1)} async-done(((bf16[128,10,16,128]{3,0,1,2:T(8,128)(2,1)}), bf16[128,10,16,128]{3,0,1,2:T(8,128)(2,1)}, u32[]{:S(2)}, u32[]{:S(2)}) %all-to-all-start.1) | async-done | bytes 5242912 | tf_op jit(solution)/shard_map/all_to_all | solution.py:47
  146.3 4.9 %broadcast_in_dim.87 = bf16[128,10,4,4,128]{4,0,1,3,2:T(8,128)(2,1)} broadcast(bf16[128,10,4,128]{3,0,1,2:T(8,128)(2,1)} %copy.72), dimensions={0,1,2,4} | broadcast | bytes 6553600 | tf_op jit(solution)/shard_map/broadcast_in_dim | solution.py:38
  151.2 24.0 %all-to-all-start = ((bf16[128,10,16,128]{3,0,1,2:T(8,128)(2,1)}), bf16[128,10,16,128]{3,0,1,2:T(8,128)(2,1)}, u32[]{:S(2)}, u32[]{:S(2)}) async-start(bf16[128,10,16,128]{3,0,1,2:T(8,128)(2,1)} %bitcast.73), calls=%async_computation | async-start | bytes 10485760 | tf_op jit(solution)/shard_map/all_to_all | solution.py:44
  175.5 6.9 %copy.75 = bf16[128,10,16,128]{3,0,2,1:T(8,128)(2,1)} copy(bf16[128,10,16,128]{3,0,1,2:T(8,128)(2,1)} %all-to-all-done.1) | data formatting | bytes 10485760 | tf_op jit(solution)/shard_map/all_to_all | solution.py:47
  182.4 88.7 %all-to-all-done = bf16[128,10,16,128]{3,0,1,2:T(8,128)(2,1)} async-done(((bf16[128,10,16,128]{3,0,1,2:T(8,128)(2,1)}), bf16[128,10,16,128]{3,0,1,2:T(8,128)(2,1)}, u32[]{:S(2)}, u32[]{:S(2)}) %all-to-all-start) | async-done | bytes 5242912 | tf_op jit(solution)/shard_map/all_to_all | solution.py:44
  271.2 6.9 %copy.73 = bf16[128,10,16,128]{3,0,2,1:T(8,128)(2,1)} copy(bf16[128,10,16,128]{3,0,1,2:T(8,128)(2,1)} %all-to-all-done) | data formatting | bytes 10485760 | tf_op jit(solution)/shard_map/all_to_all | solution.py:44
  278.1 105.0 %while.46 = (s32[]{:T(128)}, bf16[512,10,1,128]{3,0,2,1:T(8,128)(2,1)}, s32[]{:T(128)}, s32[40]{0:T(128)S(1)}, s32[40,16]{1,0:T(8,128)S(1)}, /*index=5*/s32[40,1...) while((s32[]{:T(128)}, ...), condition=%wide.region_6.8_spmd.clone, body=%wide.region_0.7_spmd.clone.sunk | while | flops 34476688 | bytes 5558466 | solution.py:112
  281.9 1.3 constant_dynamic-slice_fusion.7
  283.3 5.8 %while.47 = (s32[]{:T(128)}, f32[4,128]{1,0:T(4,128)S(1)}, f32[4,128]{1,0:T(4,128)S(1)}, f32[4,128,128]{2,1,0:T(8,128)S(1)}, s32[]{:T(128)}, /*index=5*/s32[4]{0...) while((s32[]{:T(128)}, f32[4,128]{1,0:T(4,128)S(1)}, ...), condition=%wide.region_5.6_spmd, body=%wide.region_2.5_spmd.sunk | while | flops 34343456 | bytes 2265379 | solution.py:103
  289.2 0.7 constant_dynamic-update-slice_fusion.2
  293.7 1.3 constant_dynamic-slice_fusion.7
  295.1 5.8 %while.47 = (s32[]{:T(128)}, f32[4,128]{1,0:T(4,128)S(1)}, f32[4,128]{1,0:T(4,128)S(1)}, f32[4,128,128]{2,1,0:T(8,128)S(1)}, s32[]{:T(128)}, /*index=5*/s32[4]{0...) while((s32[]{:T(128)}, f32[4,128]{1,0:T(4,128)S(1)}, ...), condition=%wide.region_5.6_spmd, body=%wide.region_2.5_spmd.sunk | while | flops 34343456 | bytes 2265379 | solution.py:103
  301.0 0.7 constant_dynamic-update-slice_fusion.2
  305.6 1.3 constant_dynamic-slice_fusion.7
  306.9 5.8 %while.47 = (s32[]{:T(128)}, f32[4,128]{1,0:T(4,128)S(1)}, f32[4,128]{1,0:T(4,128)S(1)}, f32[4,128,128]{2,1,0:T(8,128)S(1)}, s32[]{:T(128)}, /*index=5*/s32[4]{0...) while((s32[]{:T(128)}, f32[4,128]{1,0:T(4,128)S(1)}, ...), condition=%wide.region_5.6_spmd, body=%wide.region_2.5_spmd.sunk | while | flops 34343456 | bytes 2265379 | solution.py:103
  312.8 0.7 constant_dynamic-update-slice_fusion.2
  317.4 1.3 constant_dynamic-slice_fusion.7
  318.7 3.2 while.47
  322.0 0.7 constant_dynamic-update-slice_fusion.2
  326.6 1.3 constant_dynamic-slice_fusion.7
  327.9 3.2 while.47
  331.2 0.7 constant_dynamic-update-slice_fusion.2
  335.8 1.3 constant_dynamic-slice_fusion.7
  337.1 3.2 while.47
  340.4 0.7 constant_dynamic-update-slice_fusion.2
  344.9 1.3 constant_dynamic-slice_fusion.7
  346.3 3.2 while.47
  349.6 0.7 constant_dynamic-update-slice_fusion.2
  354.1 1.3 constant_dynamic-slice_fusion.7
  355.5 5.8 %while.47 = (s32[]{:T(128)}, f32[4,128]{1,0:T(4,128)S(1)}, f32[4,128]{1,0:T(4,128)S(1)}, f32[4,128,128]{2,1,0:T(8,128)S(1)}, s32[]{:T(128)}, /*index=5*/s32[4]{0...) while((s32[]{:T(128)}, f32[4,128]{1,0:T(4,128)S(1)}, ...), condition=%wide.region_5.6_spmd, body=%wide.region_2.5_spmd.sunk | while | flops 34343456 | bytes 2265379 | solution.py:103
  366.0 1.3 constant_dynamic-slice_fusion.7
  367.3 3.2 while.47
  375.1 1.3 constant_dynamic-slice_fusion.7
  376.5 5.8 %while.47 = (s32[]{:T(128)}, f32[4,128]{1,0:T(4,128)S(1)}, f32[4,128]{1,0:T(4,128)S(1)}, f32[4,128,128]{2,1,0:T(8,128)S(1)}, s32[]{:T(128)}, /*index=5*/s32[4]{0...) while((s32[]{:T(128)}, f32[4,128]{1,0:T(4,128)S(1)}, ...), condition=%wide.region_5.6_spmd, body=%wide.region_2.5_spmd.sunk | while | flops 34343456 | bytes 2265379 | solution.py:103
  383.1 2.3 copy.84
  385.4 65.7 %all_to_all.69 = bf16[512,10,1,128]{3,1,2,0:T(8,128)(2,1)S(1)} all-to-all(bf16[512,10,1,128]{3,1,2,0:T(8,128)(2,1)S(1)} %copy.84), channel_id=1, replica_groups=mesh['clips'=2,'seq'=4,'pair'=4] {'seq'}, dimensions={0} | all-to-all | bytes 2621440 | tf_op jit(solution)/shard_map/all_to_all | solution.py:113
  451.4 0.8 copy.86
  452.2 1.4 copy.87
  (343 shorter events, 61.1 us)
Async XLA Ops:
  3.2 37.7 %all-to-all-start.2 = ((bf16[128,10,4,128]{3,0,1,2:T(8,128)(2,1)}), bf16[128,10,4,128]{3,0,1,2:T(8,128)(2,1)S(1)}, u32[]{:S(2)}, u32[]{:S(2)}) async-start(bf16[128,10,4,128]{3,0,1,2:T(8,128)(2,1)} %copy.77), calls=%async_computation.2 | async-start | bytes 2621440 | tf_op jit(solution)/shard_map/all_to_all | solution.py:35
  45.8 100.5 %all-to-all-start.1 = ((bf16[128,10,16,128]{3,0,1,2:T(8,128)(2,1)}), bf16[128,10,16,128]{3,0,1,2:T(8,128)(2,1)}, u32[]{:S(2)}, u32[]{:S(2)}) async-start(bf16[128,10,16,128]{3,0,1,2:T(8,128)(2,1)} %bitcast.74), calls=%async_computation.1 | async-start | bytes 10485760 | tf_op jit(solution)/shard_map/all_to_all | solution.py:47
  151.2 24.0 %copy-start = (s32[40,16,2]{0,2,1:T(2,128)S(1)}, s32[40,16,2]{0,2,1:T(2,128)}, u32[]{:S(2)}) copy-start(s32[40,16,2]{0,2,1:T(2,128)} %param.14) | copy-start | bytes 15364
  151.2 24.1 %copy-start.1 = (s32[40,16]{0,1:T(8,128)S(1)}, s32[40,16]{0,1:T(8,128)}, u32[]{:S(2)}) copy-start(s32[40,16]{0,1:T(8,128)} %param.15) | copy-start | bytes 7684
  151.2 120.0 %all-to-all-start = ((bf16[128,10,16,128]{3,0,1,2:T(8,128)(2,1)}), bf16[128,10,16,128]{3,0,1,2:T(8,128)(2,1)}, u32[]{:S(2)}, u32[]{:S(2)}) async-start(bf16[128,10,16,128]{3,0,1,2:T(8,128)(2,1)} %bitcast.73), calls=%async_computation | async-start | bytes 10485760 | tf_op jit(solution)/shard_map/all_to_all | solution.py:44
where the time goes:
time: 459 us; the launch traced here: 454 us
  waiting for transfers between devices  208 us (45%)
  local copies, waits for them, and re-layouts  97.1 us (21%)
  blocking collectives  65.7 us (14%)
  starting transfers between devices  34.9 us (8%)
  loops' own time  27.1 us (6%)
  other arithmetic  12 us (3%)
  matrix products  9.13 us (2%)
    all_to_all x1, waiting for transfers between devices, body(): lax.all_to_all(widen_grid(value_grid), ('seq', 'pair'), split_axis=2, con...  91.7 us
    all_to_all x1, waiting for transfers between devices, body(): lax.all_to_all(widen_grid(key_grid), ('seq', 'pair'), split_axis=2, conca...  88.7 us
    all_to_all x1, blocking collectives, body(): lax.all_to_all(result, 'seq', split_axis=0, concat_axis=2, tiled=True)  65.7 us
    all_to_all x1, waiting for transfers between devices, body(): lax.all_to_all(query_grid, 'seq', split_axis=2, concat_axis=0, tiled=True)  27.1 us
    all_to_all x1, starting transfers between devices, body(): lax.all_to_all(widen_grid(key_grid), ('seq', 'pair'), split_axis=2, conca...  24 us
    broadcast_in_dim x6, local copies, waits for them, and re-layouts, widen_grid(): jnp.broadcast_to(grid_rows[:, :, :, None, :], (tok_rows, slot_count, seq_...  18.2 us
    another operation x10, loops' own time, attend_slot(): lax.fori_loop(0, visit_count, visit_list, start_state)  15 us
    dynamic_slice x10, local copies, waits for them, and re-layouts, attend_slot(): lax.dynamic_index_in_dim(value_own, slot_idx, 1, False)  12.7 us
  transfers between devices with their start and end apart: 3, of which 3 were waited for; matrix products, arithmetic and copies ran while one was open for 3% of the time, Pallas kernels for 0%

commit v1 on v0

v1 whole, which is shorter than its diff:
```python
import math

import jax
import jax.numpy as jnp
from jax import lax
from jax.sharding import Mesh
from jax.sharding import PartitionSpec as P

HEADS = 40
HD = 128
BLOCK = 128

ROWS = ("clips", "seq", "px", "pc")
GROUP = ("seq", "px")


def body(queries, key_rows, value_rows, block_lists, block_counts):
    seq_count = lax.axis_size("seq")
    px_count = lax.axis_size("px")
    pc_count = lax.axis_size("pc")
    group_count = seq_count * px_count
    group_place = lax.axis_index("seq") * px_count + lax.axis_index("px")
    pc_place = lax.axis_index("pc")
    tok_rows = queries.shape[0]
    local_blocks = tok_rows // BLOCK
    block_total = block_lists.shape[1]
    max_visits = block_lists.shape[2]
    heads_per = -(-HEADS // group_count)
    padded_heads = heads_per * group_count
    score_scale = 1.0 / math.sqrt(HD)

    def to_groups(rows_in):
        widened = rows_in.reshape(tok_rows, HEADS, HD)
        if padded_heads > HEADS:
            widened = jnp.pad(widened, ((0, 0), (0, padded_heads - HEADS), (0, 0)))
        return widened.reshape(tok_rows, group_count, heads_per * HD).transpose(1, 0, 2)

    def exchange(rows_in):
        return lax.all_to_all(to_groups(rows_in), GROUP, 0, 0, tiled=True)

    query_own = exchange(queries)
    key_part = exchange(key_rows)
    value_part = exchange(value_rows)
    key_all = lax.all_gather(key_part, "pc", axis=1)
    value_all = lax.all_gather(value_part, "pc", axis=1)

    own_count = group_count * local_blocks
    query_h = query_own.reshape(own_count, BLOCK, heads_per, HD).transpose(2, 0, 1, 3)
    key_h = key_all.reshape(block_total, BLOCK, heads_per, HD).transpose(2, 0, 1, 3)
    value_h = value_all.reshape(block_total, BLOCK, heads_per, HD).transpose(2, 0, 1, 3)

    local_index = jnp.arange(own_count, dtype=jnp.int32)
    own_blocks = (
        local_index // local_blocks * pc_count + pc_place
    ) * local_blocks + local_index % local_blocks
    head_ids = group_place * heads_per + jnp.arange(heads_per, dtype=jnp.int32)
    head_live = head_ids < HEADS
    head_safe = jnp.minimum(head_ids, HEADS - 1)
    own_lists = jnp.take(block_lists[head_safe], own_blocks, axis=1)
    counts = jnp.where(
        head_live[:, None], jnp.take(block_counts[head_safe], own_blocks, axis=1), 0
    )
    visit_count = jnp.max(counts)
    pick_key = jax.vmap(lambda blocks, idx: jnp.take(blocks, idx, axis=0))

    def visit_list(position, running):
        run_max, run_sum, run_acc = running
        picked = lax.dynamic_index_in_dim(own_lists, position, 2, False)
        key_block = pick_key(key_h, picked)
        value_block = pick_key(value_h, picked)
        scores = (
            jnp.einsum(
                "hqad,hqbd->hqab", query_h, key_block, preferred_element_type=jnp.float32
            )
            * score_scale
        )
        live_rows = (position < counts)[:, :, None]
        new_max = jnp.where(live_rows, jnp.maximum(run_max, jnp.max(scores, axis=3)), run_max)
        raised = jnp.where(live_rows[..., None], jnp.exp(scores - new_max[..., None]), 0.0)
        shrink = jnp.exp(run_max - new_max)
        run_sum = run_sum * shrink + jnp.sum(raised, axis=3)
        run_acc = run_acc * shrink[..., None] + jnp.einsum(
            "hqab,hqbd->hqad",
            raised.astype(jnp.bfloat16),
            value_block,
            preferred_element_type=jnp.float32,
        )
        return (new_max, run_sum, run_acc)

    start_state = (
        jnp.full((heads_per, own_count, BLOCK), -1e30, jnp.float32),
        jnp.zeros((heads_per, own_count, BLOCK), jnp.float32),
        jnp.zeros((heads_per, own_count, BLOCK, HD), jnp.float32),
    )
    del max_visits
    run_max, run_sum, run_acc = lax.fori_loop(0, visit_count, visit_list, start_state)
    mixed_out = (run_acc / jnp.where(run_sum > 0.0, run_sum, 1.0)[..., None]).astype(
        jnp.bfloat16
    )
    send_back = mixed_out.transpose(1, 2, 0, 3).reshape(group_count, tok_rows, heads_per * HD)
    returned = lax.all_to_all(send_back, GROUP, 0, 0, tiled=True)
    full = returned.transpose(1, 0, 2).reshape(tok_rows, padded_heads * HD)
    return full[:, : HEADS * HD]


def solution(mesh):
    sizes = dict(zip(mesh.axis_names, mesh.devices.shape))
    pair_count = sizes["pair"]
    pc_count = 2 if pair_count % 2 == 0 else 1
    view = Mesh(
        mesh.devices.reshape(
            sizes["clips"], sizes["seq"], pair_count // pc_count, pc_count
        ),
        ROWS,
    )
    rows = P(ROWS, None)
    return jax.shard_map(
        body,
        mesh=view,
        in_specs=(rows, rows, rows, P(), P()),
        out_specs=rows,
        check_vma=False,
    )
```

time: 459 us -> 219 us (0.48)
  waiting for transfers between devices: 208 us -> 27.3 us
  local copies, waits for them, and re-layouts: 97.1 us -> 51.6 us
  blocking collectives: 65.7 us -> 108 us
  starting transfers between devices: 34.9 us -> 3.61 us
  loops' own time: 27.1 us -> 2.24 us
  between operations: 0.1 us -> 13.6 us
  other arithmetic: 12 us -> 2.61 us
    all_to_all x3 -> x1, waiting for transfers between devices: 208 us -> 27.3 us  [exchange(): return lax.all_to_all(to_groups(rows_in), GROUP, 0, 0, tiled=True)]
    all_to_all x1 -> x3, blocking collectives: 65.7 us -> 108 us  [the longest x2 73.4 us: exchange(): return lax.all_to_all(to_groups(rows_in), GROUP, 0, 0, tiled=True)]
    all_to_all x3 -> x1, starting transfers between devices: 34.9 us -> 3.57 us  [exchange(): return lax.all_to_all(to_groups(rows_in), GROUP, 0, 0, tiled=True)]
    another operation x11 -> x1, loops' own time: 27.1 us -> 2.24 us  [body(): lax.fori_loop(0, visit_count, visit_list, start_state)]
    dynamic_slice x30 -> x4, local copies, waits for them, and re-layouts: 18.6 us -> 0.18 us  [visit_list(): picked = lax.dynamic_index_in_dim(own_lists, position, 2, False)]
    broadcast_in_dim x6 -> x2, local copies, waits for them, and re-layouts: 18.2 us -> 1.8 us  [the longest x1 1.8 us: body(): jnp.zeros((heads_per, own_count, BLOCK, HD), jnp.float32)]
    gather x50 -> x12, local copies, waits for them, and re-layouts: 29.2 us -> 13.5 us  [the longest x6 11 us: body(): pick_key = jax.vmap(lambda blocks, idx: jnp.take(blocks, idx, axis=0))]
    all_to_all x5 -> x0, local copies, waits for them, and re-layouts: 15.1 us -> none  [the longest x1 6.94 us: body(): lax.all_to_all(widen_grid(key_grid), ('seq', 'pair'), split_axis=2, conca...]
  transfers between devices with their start and end apart: 3 -> 3, of which waited for: 3 -> 1; matrix products, arithmetic and copies ran while one was open for 3% -> 8% of each run, Pallas kernels for 0% -> 0%
where the time goes in v1:
time: 219 us; the launch traced here: 218 us
  blocking collectives  108 us (49%)
  local copies, waits for them, and re-layouts  51.6 us (24%)
  waiting for transfers between devices  27.3 us (12%)
  between operations  13.6 us (6%)
  matrix products  9.02 us (4%)
  starting transfers between devices  3.61 us (2%)
  other arithmetic  2.61 us (1%)
  loops' own time  2.24 us (1%)
    all_to_all x2, blocking collectives, exchange(): return lax.all_to_all(to_groups(rows_in), GROUP, 0, 0, tiled=True)  73.4 us
    all_to_all x1, blocking collectives, body(): returned = lax.all_to_all(send_back, GROUP, 0, 0, tiled=True)  34.8 us
    all_to_all x1, waiting for transfers between devices, exchange(): return lax.all_to_all(to_groups(rows_in), GROUP, 0, 0, tiled=True)  27.3 us
    while x5, local copies, waits for them, and re-layouts, body(): lax.fori_loop(0, visit_count, visit_list, start_state)  13.1 us
    gather x6, local copies, waits for them, and re-layouts, body(): pick_key = jax.vmap(lambda blocks, idx: jnp.take(blocks, idx, axis=0))  11 us
    while x10, local copies, waits for them, and re-layouts  5.09 us
    dot_general x2, matrix products, visit_list(): jnp.einsum('hqad,hqbd->hqab', query_h, key_block, preferred_element_type=...  4.81 us
  transfers between devices with their start and end apart: 3, of which 1 were waited for; matrix products, arithmetic and copies ran while one was open for 8% of the time, Pallas kernels for 0%

profile of v1, /device:TPU:0, one launch (start us, length us, event | category | flops | bytes accessed | tf_op | source)
XLA Modules:
  0.0 218.2 jit_solution(1249656028758096972)
XLA Ops:
  6.5 1.8 copy.31
  8.3 38.7 %all_to_all.20 = bf16[8,128,640]{1,2,0:T(8,128)(2,1)} all-to-all(bf16[8,128,640]{1,2,0:T(8,128)(2,1)S(1)} %bitcast.83), channel_id=1, replica_groups=mesh['clips'=2,'seq'=4,'px'=2,'pc'=2] {'seq','px'}, dimensions={0} | all-to-all | bytes 2621440 | tf_op jit(solution)/shard_map/all_to_all | solution.py:39
  47.1 0.8 copy.34
  47.9 34.7 %all_to_all.21 = bf16[8,128,640]{1,2,0:T(8,128)(2,1)} all-to-all(bf16[8,128,640]{1,2,0:T(8,128)(2,1)S(1)} %bitcast.84), channel_id=1, replica_groups=mesh['clips'=2,'seq'=4,'px'=2,'pc'=2] {'seq','px'}, dimensions={0} | all-to-all | bytes 2621440 | tf_op jit(solution)/shard_map/all_to_all | solution.py:39
  82.6 1.4 copy.33
  84.1 3.6 %all-to-all-start.1 = ((bf16[8,128,640]{1,2,0:T(8,128)(2,1)}), bf16[8,128,640]{1,2,0:T(8,128)(2,1)S(1)}, u32[]{:S(2)}, u32[]{:S(2)}) async-start(bf16[8,128,640]{1,2,0:T(8,128)(2,1)} %bitcast.14), calls=%async_computation.1 | async-start | bytes 2621440 | tf_op jit(solution)/shard_map/all_to_all | solution.py:39
  87.8 0.6 gather_fusion.2
  88.3 0.1 copy.28
  88.4 0.6 gather_fusion.3
  89.0 0.8 fusion.21
  89.8 0.1 copy.36
  89.9 0.1 copy.29
  90.0 0.6 gather_fusion.4
  90.6 0.1 copy.30
  90.6 0.6 gather_fusion.5
  91.3 27.3 %all-to-all-done.1 = bf16[8,128,640]{1,2,0:T(8,128)(2,1)S(1)} async-done(((bf16[8,128,640]{1,2,0:T(8,128)(2,1)}), bf16[8,128,640]{1,2,0:T(8,128)(2,1)S(1)}, u32[]{:S(2)}, u32[]{:S(2)}) %all-to-all-start.1) | async-done | bytes 1310752 | tf_op jit(solution)/shard_map/all_to_all | solution.py:39
  118.6 1.4 copy.39
  120.0 3.2 %copy.32 = bf16[8,256,640]{1,0,2:T(8,128)(2,1)S(1)} copy(bf16[8,256,640]{1,2,0:T(8,128)(2,1)} %all-gather.5.cloned.1.call-done) | data formatting | bytes 5242880 | tf_op jit(solution)/shard_map/all_gather | solution.py:44
  123.3 3.0 %reshape.75 = bf16[16,128,5,128]{1,0,3,2:T(8,128)(2,1)} reshape(bf16[8,256,640]{1,0,2:T(8,128)(2,1)S(1)} %copy.32) | data formatting | bytes 5242880 | tf_op jit(solution)/shard_map/reshape | solution.py:49
  126.2 4.7 %copy.38 = bf16[5,16,128,128]{3,2,1,0:T(8,128)(2,1)} copy(bf16[5,16,128,128]{2,1,3,0:T(8,128)(2,1)} %bitcast.78) | data formatting | bytes 5242880 | tf_op jit(solution)/shard_map/while | solution.py:96
  130.9 3.2 %copy.35 = bf16[8,256,640]{1,0,2:T(8,128)(2,1)S(1)} copy(bf16[8,256,640]{1,2,0:T(8,128)(2,1)} %all-gather.7.cloned.1.call-done) | data formatting | bytes 5242880 | tf_op jit(solution)/shard_map/all_gather | solution.py:45
  134.2 3.0 %reshape.77 = bf16[16,128,5,128]{1,0,3,2:T(8,128)(2,1)} reshape(bf16[8,256,640]{1,0,2:T(8,128)(2,1)S(1)} %copy.35) | data formatting | bytes 5242880 | tf_op jit(solution)/shard_map/reshape | solution.py:50
  137.1 4.7 %copy.40 = bf16[5,16,128,128]{3,2,1,0:T(8,128)(2,1)} copy(bf16[5,16,128,128]{2,1,3,0:T(8,128)(2,1)} %bitcast.79) | data formatting | bytes 5242880 | tf_op jit(solution)/shard_map/while | solution.py:96
  141.8 1.8 broadcast_in_dim.80
  143.6 28.9 %while.14 = (s32[]{:T(128)}, f32[5,8,128]{2,1,0:T(8,128)S(1)}, f32[5,8,128]{2,1,0:T(8,128)S(1)}, f32[5,8,128,128]{3,2,1,0:T(8,128)}, s32[]{:T(128)}, /*index=5*/...) while((s32[]{:T(128)}, f32[5,8,128]{2,1,0:T(8,128)S(1)}, ...), condition=%wide.region_4.6_spmd, body=%wide.region_1.5_spmd.sunk | while | flops 344735328 | bytes 43584192 | solution.py:96
  144.4 0.1 copy.47
  144.5 0.1 reshape.157
  144.5 2.7 %gather_fusion.1 = bf16[40,128,128]{2,1,0:T(8,128)(2,1)S(1)} fusion(bf16[5,16,128,128]{3,2,1,0:T(8,128)(2,1)} %get-tuple-element.229, s32[40]{0:T(128)S(1)} %reshape.157), kind=kCustom, calls=%fused_computation.1.clone.clone.1 | custom fusion | bytes 2621760 | tf_op jit(solution)/shard_map/while/body/vmap(jit(_take))/gather | solution.py:64
  147.3 2.7 %gather_fusion = bf16[40,128,128]{2,1,0:T(8,128)(2,1)S(1)} fusion(bf16[5,16,128,128]{3,2,1,0:T(8,128)(2,1)} %get-tuple-element.227, s32[40]{0:T(128)S(1)} %reshape.157), kind=kCustom, calls=%fused_computation.clone.clone.1 | custom fusion | bytes 2621760 | tf_op jit(solution)/shard_map/while/body/vmap(jit(_take))/gather | solution.py:64
  150.0 2.4 %bitcast_reduce_fusion.2 = (f32[5,8,128]{2,1,0:T(8,128)S(1)}, f32[5,8,128,128]{3,2,1,0:T(8,128)S(1)}) fusion(bf16[5,8,128,128]{3,2,1,0:T(8,128)(2,1)} %get-tuple-element.228, bf16[5,8,128,128]{3,2,1,0:T(8,128)(2,1)S(1)} %bitcast.76, pred[5,8]{1,0:T(8,128)(4,1)S(1)} %get-tuple-element.188), kind=kOutput, calls=%fused_computation.7.clone.1 | convolution fusion | flops 169733120 | bytes 5263400 | tf_op jit(solution)/shard_map/while/body/hqad,hqbd->hqab/dot_general | solution.py:72
  152.4 0.1 maximum_select_fusion.2
  152.5 0.6 fusion.32
  153.1 1.1 copy-done
  154.2 2.1 multiply_add_fusion.5
  156.3 1.5 copy-done.1
  158.5 0.1 copy.47
  158.6 0.1 reshape.157
  158.7 2.7 %gather_fusion.1 = bf16[40,128,128]{2,1,0:T(8,128)(2,1)S(1)} fusion(bf16[5,16,128,128]{3,2,1,0:T(8,128)(2,1)} %get-tuple-element.229, s32[40]{0:T(128)S(1)} %reshape.157), kind=kCustom, calls=%fused_computation.1.clone.clone.1 | custom fusion | bytes 2621760 | tf_op jit(solution)/shard_map/while/body/vmap(jit(_take))/gather | solution.py:64
  161.4 2.7 %gather_fusion = bf16[40,128,128]{2,1,0:T(8,128)(2,1)S(1)} fusion(bf16[5,16,128,128]{3,2,1,0:T(8,128)(2,1)} %get-tuple-element.227, s32[40]{0:T(128)S(1)} %reshape.157), kind=kCustom, calls=%fused_computation.clone.clone.1 | custom fusion | bytes 2621760 | tf_op jit(solution)/shard_map/while/body/vmap(jit(_take))/gather | solution.py:64
  164.1 2.4 %bitcast_reduce_fusion.2 = (f32[5,8,128]{2,1,0:T(8,128)S(1)}, f32[5,8,128,128]{3,2,1,0:T(8,128)S(1)}) fusion(bf16[5,8,128,128]{3,2,1,0:T(8,128)(2,1)} %get-tuple-element.228, bf16[5,8,128,128]{3,2,1,0:T(8,128)(2,1)S(1)} %bitcast.76, pred[5,8]{1,0:T(8,128)(4,1)S(1)} %get-tuple-element.188), kind=kOutput, calls=%fused_computation.7.clone.1 | convolution fusion | flops 169733120 | bytes 5263400 | tf_op jit(solution)/shard_map/while/body/hqad,hqbd->hqab/dot_general | solution.py:72
  166.6 0.6 fusion.32
  167.2 1.1 copy-done
  168.3 2.1 multiply_add_fusion.5
  170.4 1.5 copy-done.1
  172.6 2.2 copy.42
  174.8 0.3 divide_convert_fusion
  175.1 34.8 %all_to_all.22 = bf16[8,128,640]{1,2,0:T(8,128)(2,1)S(1)} all-to-all(bf16[8,128,640]{1,2,0:T(8,128)(2,1)S(1)} %bitcast.81), channel_id=1, replica_groups=mesh['clips'=2,'seq'=4,'px'=2,'pc'=2] {'seq','px'}, dimensions={0} | all-to-all | bytes 2621440 | tf_op jit(solution)/shard_map/all_to_all | solution.py:101
  210.0 1.4 copy.43
  (41 shorter events, 0.5 us)
Async XLA Ops:
  6.5 113.5 %all-gather.5.cloned.1.call-start = ((), (), s32[]{:S(2)}) async-start(), calls=%async_computation.4 | async-start | bytes 3932160 | tf_op jit(solution)/shard_map/all_gather | solution.py:44
  8.3 38.8 %copy-start.2 = (bf16[128,5120]{1,0:T(8,128)(2,1)S(1)}, bf16[128,5120]{1,0:T(8,128)(2,1)}, u32[]{:S(2)}) copy-start(bf16[128,5120]{1,0:T(8,128)(2,1)} %param.11) | copy-start | bytes 3932164
  47.0 83.9 %all-gather.7.cloned.1.call-start = ((), (), s32[]{:S(2)}) async-start(), calls=%async_computation.5 | async-start | bytes 3932160 | tf_op jit(solution)/shard_map/all_gather | solution.py:45
  47.9 34.7 %copy-start.3 = (bf16[128,5120]{1,0:T(8,128)(2,1)S(1)}, bf16[128,5120]{1,0:T(8,128)(2,1)}, u32[]{:S(2)}) copy-start(bf16[128,5120]{1,0:T(8,128)(2,1)} %param.9) | copy-start | bytes 3932164
  82.6 5.1 %copy-start.5 = (s32[40,16]{0,1:T(8,128)S(1)}, s32[40,16]{0,1:T(8,128)}, u32[]{:S(2)}) copy-start(s32[40,16]{0,1:T(8,128)} %param.13) | copy-start | bytes 7684
  82.6 7.3 %copy-start.4 = (s32[40,16,2]{0,2,1:T(2,128)S(1)}, s32[40,16,2]{0,2,1:T(2,128)}, u32[]{:S(2)}) copy-start(s32[40,16,2]{0,2,1:T(2,128)} %param.12) | copy-start | bytes 15364
  84.1 34.5 %all-to-all-start.1 = ((bf16[8,128,640]{1,2,0:T(8,128)(2,1)}), bf16[8,128,640]{1,2,0:T(8,128)(2,1)S(1)}, u32[]{:S(2)}, u32[]{:S(2)}) async-start(bf16[8,128,640]{1,2,0:T(8,128)(2,1)} %bitcast.14), calls=%async_computation.1 | async-start | bytes 2621440 | tf_op jit(solution)/shard_map/all_to_all | solution.py:39
  152.4 1.7 copy-start
  156.3 1.5 copy-start.1
  166.5 1.7 copy-start
  170.4 1.5 copy-start.1
Sparse Core Ops, SparseCore 0:
  47.1 10.0 all-gather.4
  82.7 9.9 all-gather.6

commit v2 on v1

v2 whole, which is shorter than its diff:
```python
import math

import jax
import jax.numpy as jnp
from jax import lax
from jax.experimental import pallas as pl
from jax.experimental.pallas import tpu as pltpu
from jax.sharding import Mesh
from jax.sharding import PartitionSpec as P

HEADS = 40
HD = 128
BLOCK = 128

ROWS = ("clips", "seq", "px", "pc")
GROUP = ("seq", "px")


def body(queries, key_rows, value_rows, block_lists, block_counts):
    seq_count = lax.axis_size("seq")
    px_count = lax.axis_size("px")
    pc_count = lax.axis_size("pc")
    group_count = seq_count * px_count
    group_place = lax.axis_index("seq") * px_count + lax.axis_index("px")
    pc_place = lax.axis_index("pc")
    tok_rows = queries.shape[0]
    local_blocks = tok_rows // BLOCK
    block_total = block_lists.shape[1]
    max_visits = block_lists.shape[2]
    heads_per = -(-HEADS // group_count)
    padded_heads = heads_per * group_count
    score_scale = 1.0 / math.sqrt(HD)

    def to_groups(rows_in):
        widened = rows_in.reshape(tok_rows, HEADS, HD)
        if padded_heads > HEADS:
            widened = jnp.pad(widened, ((0, 0), (0, padded_heads - HEADS), (0, 0)))
        return widened.reshape(tok_rows, group_count, heads_per * HD).transpose(1, 0, 2)

    def exchange(rows_in):
        return lax.all_to_all(to_groups(rows_in), GROUP, 0, 0, tiled=True)

    query_own = exchange(queries)
    key_part = exchange(key_rows)
    value_part = exchange(value_rows)
    key_all = lax.all_gather(key_part, "pc", axis=1)
    value_all = lax.all_gather(value_part, "pc", axis=1)

    own_count = group_count * local_blocks
    local_index = jnp.arange(own_count, dtype=jnp.int32)
    own_blocks = (
        local_index // local_blocks * pc_count + pc_place
    ) * local_blocks + local_index % local_blocks
    head_ids = group_place * heads_per + jnp.arange(heads_per, dtype=jnp.int32)
    head_live = head_ids < HEADS
    head_safe = jnp.minimum(head_ids, HEADS - 1)
    own_lists = jnp.take(block_lists[head_safe], own_blocks, axis=1)
    counts = jnp.where(
        head_live[:, None], jnp.take(block_counts[head_safe], own_blocks, axis=1), 0
    )
    mixed_out = attend(
        own_lists.reshape(-1),
        counts.reshape(-1),
        query_own.reshape(own_count * BLOCK, heads_per * HD),
        key_all.reshape(block_total * BLOCK, heads_per * HD),
        value_all.reshape(block_total * BLOCK, heads_per * HD),
        max_visits,
        score_scale,
    )
    send_back = mixed_out.reshape(group_count, tok_rows, heads_per * HD)
    returned = lax.all_to_all(send_back, GROUP, 0, 0, tiled=True)
    full = returned.transpose(1, 0, 2).reshape(tok_rows, padded_heads * HD)
    return full[:, : HEADS * HD]


def attend(lists, counts, query_rows, key_rows, value_rows, max_visits, score_scale):
    own_rows = query_rows.shape[0]
    all_rows = key_rows.shape[0]
    own_count = own_rows // BLOCK
    heads_per = query_rows.shape[1] // HD

    def kernel(lists_ref, counts_ref, q_ref, k_ref, v_ref, o_ref):
        head = pl.program_id(0)

        def per_block(i, carry):
            slot = head * own_count + i
            visits = counts_ref[slot]
            row = pl.multiple_of(i * BLOCK, BLOCK)
            q = q_ref[pl.ds(row, BLOCK), :]

            def score(j):
                krow = pl.multiple_of(lists_ref[slot * max_visits + j] * BLOCK, BLOCK)
                k = k_ref[pl.ds(krow, BLOCK), :]
                s = lax.dot_general(
                    q, k, (((1,), (1,)), ((), ())), preferred_element_type=jnp.float32
                )
                return s * score_scale, krow

            def max_step(j, m):
                s, _ = score(j)
                return jnp.maximum(m, jnp.max(s, axis=1, keepdims=True))

            m = lax.fori_loop(
                0, visits, max_step, jnp.full((BLOCK, 1), -jnp.inf, jnp.float32)
            )

            def acc_step(j, state):
                total, acc = state
                s, krow = score(j)
                raised = jnp.exp(s - m)
                total = total + jnp.sum(raised, axis=1, keepdims=True)
                acc = acc + jnp.dot(
                    raised.astype(jnp.bfloat16),
                    v_ref[pl.ds(krow, BLOCK), :],
                    preferred_element_type=jnp.float32,
                )
                return total, acc

            total, acc = lax.fori_loop(
                0,
                visits,
                acc_step,
                (jnp.zeros((BLOCK, 1), jnp.float32), jnp.zeros((BLOCK, HD), jnp.float32)),
            )
            total = jnp.where(total > 0.0, total, 1.0)
            o_ref[pl.ds(row, BLOCK), :] = (acc / total).astype(o_ref.dtype)
            return carry

        lax.fori_loop(0, own_count, per_block, 0)

    grid_spec = pltpu.PrefetchScalarGridSpec(
        num_scalar_prefetch=2,
        grid=(heads_per,),
        in_specs=[
            pl.BlockSpec((own_rows, HD), lambda h, *_: (0, h)),
            pl.BlockSpec((all_rows, HD), lambda h, *_: (0, h)),
            pl.BlockSpec((all_rows, HD), lambda h, *_: (0, h)),
        ],
        out_specs=pl.BlockSpec((own_rows, HD), lambda h, *_: (0, h)),
    )
    return pl.pallas_call(
        kernel,
        grid_spec=grid_spec,
        out_shape=jax.ShapeDtypeStruct(query_rows.shape, jnp.bfloat16),
    )(lists, counts, query_rows, key_rows, value_rows)


def solution(mesh):
    sizes = dict(zip(mesh.axis_names, mesh.devices.shape))
    pair_count = sizes["pair"]
    pc_count = 2 if pair_count % 2 == 0 else 1
    view = Mesh(
        mesh.devices.reshape(
            sizes["clips"], sizes["seq"], pair_count // pc_count, pc_count
        ),
        ROWS,
    )
    rows = P(ROWS, None)
    return jax.shard_map(
        body,
        mesh=view,
        in_specs=(rows, rows, rows, P(), P()),
        out_specs=rows,
        check_vma=False,
    )
```

time: 219 us -> 197 us (0.90)
  local copies, waits for them, and re-layouts: 51.6 us -> 11.7 us
  Pallas kernels: 0 us -> 32.5 us
  matrix products: 9.02 us -> 0 us
  other arithmetic: 2.61 us -> 0.2 us
  loops' own time: 2.24 us -> 0 us
    pallas_call x0 -> x1, Pallas kernels: none -> 32.5 us  [attend(): pl.pallas_call(kernel, grid_spec=grid_spec, out_shape=jax.ShapeDtypeStruc...]
    while x15 -> x0, local copies, waits for them, and re-layouts: 18.1 us -> none  [the longest x5 13.1 us: body(): lax.fori_loop(0, visit_count, visit_list, start_state)]
    gather x6 -> x0, local copies, waits for them, and re-layouts: 11 us -> none  [body(): pick_key = jax.vmap(lambda blocks, idx: jnp.take(blocks, idx, axis=0))]
    dot_general x4 -> x0, matrix products: 9.02 us -> none  [the longest x2 4.81 us: visit_list(): jnp.einsum('hqad,hqbd->hqab', query_h, key_block, preferred_element_type=...]
    all_gather x2 -> x0, local copies, waits for them, and re-layouts: 6.43 us -> none  [the longest x1 3.21 us: body(): key_all = lax.all_gather(key_part, 'pc', axis=1)]
    reshape x2 -> x0, local copies, waits for them, and re-layouts: 5.98 us -> none  [the longest x1 2.99 us: body(): key_all.reshape(block_total, BLOCK, heads_per, HD).transpose(2, 0, 1, 3)]
    another operation x1 -> x3, local copies, waits for them, and re-layouts: 0.01 us -> 2.74 us  [to_groups(): widened.reshape(tok_rows, group_count, heads_per * HD).transpose(1, 0, 2)]
    another operation x1 -> x0, loops' own time: 2.24 us -> none  [body(): lax.fori_loop(0, visit_count, visit_list, start_state)]
  transfers between devices with their start and end apart: 3 -> 3, of which waited for: 1 -> 1; matrix products, arithmetic and copies ran while one was open for 8% -> 3% of each run, Pallas kernels for 0% -> 0%
where the time goes in v2:
time: 197 us; the launch traced here: 195 us
  blocking collectives  107 us (54%)
  Pallas kernels  32.5 us (16%)
  waiting for transfers between devices  26.6 us (14%)
  between operations  13.5 us (7%)
  local copies, waits for them, and re-layouts  11.7 us (6%)
  starting transfers between devices  3.77 us (2%)
    all_to_all x2, blocking collectives, exchange(): return lax.all_to_all(to_groups(rows_in), GROUP, 0, 0, tiled=True)  73.1 us
    all_to_all x1, blocking collectives, body(): returned = lax.all_to_all(send_back, GROUP, 0, 0, tiled=True)  33.9 us
    pallas_call x1, Pallas kernels, attend(): pl.pallas_call(kernel, grid_spec=grid_spec, out_shape=jax.ShapeDtypeStruc...  32.5 us
    all_to_all x1, waiting for transfers between devices, exchange(): return lax.all_to_all(to_groups(rows_in), GROUP, 0, 0, tiled=True)  26.5 us
  transfers between devices with their start and end apart: 3, of which 1 were waited for; matrix products, arithmetic and copies ran while one was open for 3% of the time, Pallas kernels for 0%

profile of v2, /device:TPU:0, one launch (start us, length us, event | category | flops | bytes accessed | tf_op | source)
XLA Modules:
  0.0 195.2 jit_solution(9237780718669736411)
XLA Ops:
  6.5 0.0 all-gather.5.cloned.1.call-start
  6.5 1.4 copy.41
  8.0 38.5 %all_to_all.20 = bf16[8,128,640]{2,1,0:T(8,128)(2,1)} all-to-all(bf16[8,128,640]{2,1,0:T(8,128)(2,1)S(1)} %bitcast.37), channel_id=1, replica_groups=mesh['clips'=2,'seq'=4,'px'=2,'pc'=2] {'seq','px'}, dimensions={0} | all-to-all | bytes 2621440 | tf_op jit(solution)/shard_map/all_to_all | solution.py:41
  46.5 0.0 copy-start.1
  46.5 0.0 all-gather.5.cloned.1.call-update
  46.6 0.0 all-gather.7.cloned.1.call-start
  46.6 1.2 copy-done.1
  47.8 0.1 copy.40
  48.0 34.6 %all_to_all.21 = bf16[8,128,640]{2,1,0:T(8,128)(2,1)} all-to-all(bf16[8,128,640]{2,1,0:T(8,128)(2,1)S(1)} %bitcast.38), channel_id=1, replica_groups=mesh['clips'=2,'seq'=4,'px'=2,'pc'=2] {'seq','px'}, dimensions={0} | all-to-all | bytes 2621440 | tf_op jit(solution)/shard_map/all_to_all | solution.py:41
  82.5 0.0 copy-start.2
  82.5 0.0 all-gather.7.cloned.1.call-update
  82.6 1.3 copy-done.2
  83.9 1.2 copy.42
  85.0 0.0 copy-start.4
  85.0 0.0 copy-start.3
  85.0 3.7 %all-to-all-start = ((bf16[8,128,640]{2,1,0:T(8,128)(2,1)}), bf16[8,128,640]{2,1,0:T(8,128)(2,1)S(1)}, u32[]{:S(2)}, u32[]{:S(2)}) async-start(bf16[8,128,640]{2,1,0:T(8,128)(2,1)} %bitcast.35), calls=%async_computation | async-start | bytes 2621440 | tf_op jit(solution)/shard_map/all_to_all | solution.py:41
  88.8 0.0 copy-done.4
  88.8 0.1 copy.26
  88.9 0.6 gather_fusion.2
  89.5 0.1 copy.27
  89.6 0.6 gather_fusion.3
  90.1 0.1 select_bitcast_fusion.1
  90.2 0.1 copy.28
  90.3 0.6 select_n.73.counts_ref
  90.9 0.0 copy-done.3
  90.9 0.1 copy.23
  91.0 0.6 gather_fusion
  91.6 0.1 copy.24
  91.7 0.6 gather_fusion.1
  92.2 0.1 select_bitcast_fusion
  92.3 0.1 copy.25
  92.5 0.7 select_n.70.lists_ref
  93.2 26.5 %all-to-all-done = bf16[8,128,640]{2,1,0:T(8,128)(2,1)S(1)} async-done(((bf16[8,128,640]{2,1,0:T(8,128)(2,1)}), bf16[8,128,640]{2,1,0:T(8,128)(2,1)S(1)}, u32[]{:S(2)}, u32[]{:S(2)}) %all-to-all-start) | async-done | bytes 1310752 | tf_op jit(solution)/shard_map/all_to_all | solution.py:41
  119.7 0.0 copy-start
  119.7 0.0 all-gather.5.cloned.1.call-done
  119.7 0.0 all-gather.7.cloned.1.call-done
  119.7 1.1 copy-done
  120.8 32.5 %shard_map.55 = bf16[1024,640]{1,0:T(8,128)(2,1)} custom-call(s32[80]{0:T(128)} %select_n.70.lists_ref, s32[40]{0:T(128)} %select_n.73.counts_ref, bf16[1024,640]{1,0:T(8,128)(2,1)} %bitcast.39, bf16[2048,640]{1,0:T(8,128)(2,1)} %bitcast.41, bf16[2048,640]{1,0:T(8,128)(2,1)} %bitcast.42), custom_call_target="tpu_custom_call" | custom-call | tf_op jit(solution)/shard_map/pallas_call | solution.py:141
  153.3 33.9 %all_to_all.22 = bf16[8,128,640]{2,1,0:T(8,128)(2,1)S(1)} all-to-all(bf16[8,128,640]{2,1,0:T(8,128)(2,1)} %bitcast.40), channel_id=1, replica_groups=mesh['clips'=2,'seq'=4,'px'=2,'pc'=2] {'seq','px'}, dimensions={0} | all-to-all | bytes 2621440 | tf_op jit(solution)/shard_map/all_to_all | solution.py:71
  187.2 1.2 copy.36
  (6 shorter events, 0.1 us)
Async XLA Ops:
  6.5 113.2 %all-gather.5.cloned.1.call-start = ((), (), s32[]{:S(2)}) async-start(), calls=%async_computation.4 | async-start | bytes 3932160 | tf_op jit(solution)/shard_map/all_gather | solution.py:46
  46.5 1.3 copy-start.1
  46.6 73.2 %all-gather.7.cloned.1.call-start = ((), (), s32[]{:S(2)}) async-start(), calls=%async_computation.5 | async-start | bytes 3932160 | tf_op jit(solution)/shard_map/all_gather | solution.py:47
  82.5 1.3 copy-start.2
  85.0 3.7 %copy-start.4 = (s32[40,16]{0,1:T(8,128)S(1)}, s32[40,16]{0,1:T(8,128)}, u32[]{:S(2)}) copy-start(s32[40,16]{0,1:T(8,128)} %param.9) | copy-start | bytes 7684
  85.0 5.9 %copy-start.3 = (s32[40,16,2]{0,2,1:T(2,128)S(1)}, s32[40,16,2]{0,2,1:T(2,128)}, u32[]{:S(2)}) copy-start(s32[40,16,2]{0,2,1:T(2,128)} %param.8) | copy-start | bytes 15364
  85.0 34.7 %all-to-all-start = ((bf16[8,128,640]{2,1,0:T(8,128)(2,1)}), bf16[8,128,640]{2,1,0:T(8,128)(2,1)S(1)}, u32[]{:S(2)}, u32[]{:S(2)}) async-start(bf16[8,128,640]{2,1,0:T(8,128)(2,1)} %bitcast.35), calls=%async_computation | async-start | bytes 2621440 | tf_op jit(solution)/shard_map/all_to_all | solution.py:41
  119.7 1.1 copy-start
Sparse Core Ops, SparseCore 0:
  46.7 10.3 all-gather.4
  82.7 10.3 all-gather.6

commit v3 on v2

--- a/solution.py
+++ b/solution.py
@@ -78,6 +78,7 @@
     all_rows = key_rows.shape[0]
     own_count = own_rows // BLOCK
     heads_per = query_rows.shape[1] // HD
+    kv_blocks = all_rows // BLOCK
 
     def kernel(lists_ref, counts_ref, q_ref, k_ref, v_ref, o_ref):
         head = pl.program_id(0)
@@ -87,46 +88,39 @@
             visits = counts_ref[slot]
             row = pl.multiple_of(i * BLOCK, BLOCK)
             q = q_ref[pl.ds(row, BLOCK), :]
-
-            def score(j):
-                krow = pl.multiple_of(lists_ref[slot * max_visits + j] * BLOCK, BLOCK)
-                k = k_ref[pl.ds(krow, BLOCK), :]
+            key_starts = []
+            scores = []
+            for j in range(max_visits):
+                picked = jnp.clip(lists_ref[slot * max_visits + j], 0, kv_blocks - 1)
+                krow = pl.multiple_of(picked * BLOCK, BLOCK)
                 s = lax.dot_general(
-                    q, k, (((1,), (1,)), ((), ())), preferred_element_type=jnp.float32
+                    q,
+                    k_ref[pl.ds(krow, BLOCK), :],
+                    (((1,), (1,)), ((), ())),
+                    preferred_element_type=jnp.float32,
                 )
-                return s * score_scale, krow
-
-            def max_step(j, m):
-                s, _ = score(j)
-                return jnp.maximum(m, jnp.max(s, axis=1, keepdims=True))
-
-            m = lax.fori_loop(
-                0, visits, max_step, jnp.full((BLOCK, 1), -jnp.inf, jnp.float32)
-            )
-
-            def acc_step(j, state):
-                total, acc = state
-                s, krow = score(j)
-                raised = jnp.exp(s - m)
+                key_starts.append(krow)
+                scores.append(jnp.where(j < visits, s * score_scale, -jnp.inf))
+            peak = scores[0]
+            for s in scores[1:]:
+                peak = jnp.maximum(peak, s)
+            row_max = jnp.max(peak, axis=1, keepdims=True)
+            row_max = jnp.where(row_max > -jnp.inf, row_max, 0.0)
+            total = jnp.zeros((BLOCK, 1), jnp.float32)
+            acc = jnp.zeros((BLOCK, HD), jnp.float32)
+            for s, krow in zip(scores, key_starts):
+                raised = jnp.exp(s - row_max)
                 total = total + jnp.sum(raised, axis=1, keepdims=True)
                 acc = acc + jnp.dot(
                     raised.astype(jnp.bfloat16),
                     v_ref[pl.ds(krow, BLOCK), :],
                     preferred_element_type=jnp.float32,
                 )
-                return total, acc
-
-            total, acc = lax.fori_loop(
-                0,
-                visits,
-                acc_step,
-                (jnp.zeros((BLOCK, 1), jnp.float32), jnp.zeros((BLOCK, HD), jnp.float32)),
-            )
             total = jnp.where(total > 0.0, total, 1.0)
             o_ref[pl.ds(row, BLOCK), :] = (acc / total).astype(o_ref.dtype)
             return carry
 
-        lax.fori_loop(0, own_count, per_block, 0)
+        lax.fori_loop(0, own_count, per_block, 0, unroll=min(own_count, 4))
 
     grid_spec = pltpu.PrefetchScalarGridSpec(
         num_scalar_prefetch=2,

time: 197 us -> 179 us (0.909)
  Pallas kernels: 32.5 us -> 14.8 us
    pallas_call x1, Pallas kernels: 32.5 us -> 14.8 us  [attend(): pl.pallas_call(kernel, grid_spec=grid_spec, out_shape=jax.ShapeDtypeStruc...]
where the time goes in v3:
time: 179 us
  blocking collectives  108 us (60%)
  waiting for transfers between devices  26.6 us (15%)
  Pallas kernels  14.8 us (8%)
  between operations  13.5 us (8%)
  local copies, waits for them, and re-layouts  11.7 us (7%)
  starting transfers between devices  3.77 us (2%)
    all_to_all x2, blocking collectives, exchange(): return lax.all_to_all(to_groups(rows_in), GROUP, 0, 0, tiled=True)  73.1 us
    all_to_all x1, blocking collectives, body(): returned = lax.all_to_all(send_back, GROUP, 0, 0, tiled=True)  35 us
    all_to_all x1, waiting for transfers between devices, exchange(): return lax.all_to_all(to_groups(rows_in), GROUP, 0, 0, tiled=True)  26.5 us
    pallas_call x1, Pallas kernels, attend(): pl.pallas_call(kernel, grid_spec=grid_spec, out_shape=jax.ShapeDtypeStruc...  14.8 us
    unnamed x12, local copies, waits for them, and re-layouts  3.76 us
    all_to_all x1, starting transfers between devices, exchange(): return lax.all_to_all(to_groups(rows_in), GROUP, 0, 0, tiled=True)  3.73 us
  transfers between devices with their start and end apart: 3, of which 1 were waited for; matrix products, arithmetic and copies ran while one was open for 3% of the time, Pallas kernels for 0%

profile of v3, /device:TPU:0, one launch (start us, length us, event | category | flops | bytes accessed | tf_op | source)
XLA Modules:
  0.0 178.7 jit_solution(17529134480374063716)
XLA Ops:
  6.5 0.0 all-gather.5.cloned.1.call-start
  6.5 1.4 copy.41
  8.0 38.5 %all_to_all.20 = bf16[8,128,640]{2,1,0:T(8,128)(2,1)} all-to-all(bf16[8,128,640]{2,1,0:T(8,128)(2,1)S(1)} %bitcast.37), channel_id=1, replica_groups=mesh['clips'=2,'seq'=4,'px'=2,'pc'=2] {'seq','px'}, dimensions={0} | all-to-all | bytes 2621440 | tf_op jit(solution)/shard_map/all_to_all | solution.py:41
  46.5 0.0 copy-start.1
  46.5 0.0 all-gather.5.cloned.1.call-update
  46.6 0.0 all-gather.7.cloned.1.call-start
  46.6 1.2 copy-done.1
  47.8 0.1 copy.40
  48.0 34.6 %all_to_all.21 = bf16[8,128,640]{2,1,0:T(8,128)(2,1)} all-to-all(bf16[8,128,640]{2,1,0:T(8,128)(2,1)S(1)} %bitcast.38), channel_id=1, replica_groups=mesh['clips'=2,'seq'=4,'px'=2,'pc'=2] {'seq','px'}, dimensions={0} | all-to-all | bytes 2621440 | tf_op jit(solution)/shard_map/all_to_all | solution.py:41
  82.5 0.0 copy-start.2
  82.5 0.0 all-gather.7.cloned.1.call-update
  82.6 1.3 copy-done.2
  83.9 1.2 copy.42
  85.0 0.0 copy-start.4
  85.0 0.0 copy-start.3
  85.0 3.7 %all-to-all-start = ((bf16[8,128,640]{2,1,0:T(8,128)(2,1)}), bf16[8,128,640]{2,1,0:T(8,128)(2,1)S(1)}, u32[]{:S(2)}, u32[]{:S(2)}) async-start(bf16[8,128,640]{2,1,0:T(8,128)(2,1)} %bitcast.35), calls=%async_computation | async-start | bytes 2621440 | tf_op jit(solution)/shard_map/all_to_all | solution.py:41
  88.8 0.0 copy-done.4
  88.8 0.1 copy.26
  88.9 0.6 gather_fusion.2
  89.5 0.1 copy.27
  89.6 0.6 gather_fusion.3
  90.1 0.1 select_bitcast_fusion.1
  90.2 0.1 copy.28
  90.3 0.6 select_n.73.counts_ref
  90.9 0.0 copy-done.3
  90.9 0.1 copy.23
  91.0 0.6 gather_fusion
  91.6 0.1 copy.24
  91.7 0.6 gather_fusion.1
  92.2 0.1 select_bitcast_fusion
  92.3 0.1 copy.25
  92.5 0.7 select_n.70.lists_ref
  93.2 26.5 %all-to-all-done = bf16[8,128,640]{2,1,0:T(8,128)(2,1)S(1)} async-done(((bf16[8,128,640]{2,1,0:T(8,128)(2,1)}), bf16[8,128,640]{2,1,0:T(8,128)(2,1)S(1)}, u32[]{:S(2)}, u32[]{:S(2)}) %all-to-all-start) | async-done | bytes 1310752 | tf_op jit(solution)/shard_map/all_to_all | solution.py:41
  119.7 0.0 copy-start
  119.7 0.0 all-gather.5.cloned.1.call-done
  119.7 0.0 all-gather.7.cloned.1.call-done
  119.7 1.1 copy-done
  120.8 14.8 %shard_map.55 = bf16[1024,640]{1,0:T(8,128)(2,1)} custom-call(s32[80]{0:T(128)} %select_n.70.lists_ref, s32[40]{0:T(128)} %select_n.73.counts_ref, bf16[1024,640]{1,0:T(8,128)(2,1)} %bitcast.39, bf16[2048,640]{1,0:T(8,128)(2,1)} %bitcast.41, bf16[2048,640]{1,0:T(8,128)(2,1)} %bitcast.42), custom_call_target="tpu_custom_call" | custom-call | tf_op jit(solution)/shard_map/pallas_call | solution.py:135
  135.6 35.0 %all_to_all.22 = bf16[8,128,640]{2,1,0:T(8,128)(2,1)S(1)} all-to-all(bf16[8,128,640]{2,1,0:T(8,128)(2,1)} %bitcast.40), channel_id=1, replica_groups=mesh['clips'=2,'seq'=4,'px'=2,'pc'=2] {'seq','px'}, dimensions={0} | all-to-all | bytes 2621440 | tf_op jit(solution)/shard_map/all_to_all | solution.py:71
  170.6 1.2 copy.36
  (6 shorter events, 0.1 us)
Async XLA Ops:
  6.5 113.2 %all-gather.5.cloned.1.call-start = ((), (), s32[]{:S(2)}) async-start(), calls=%async_computation.4 | async-start | bytes 3932160 | tf_op jit(solution)/shard_map/all_gather | solution.py:46
  46.5 1.3 copy-start.1
  46.6 73.2 %all-gather.7.cloned.1.call-start = ((), (), s32[]{:S(2)}) async-start(), calls=%async_computation.5 | async-start | bytes 3932160 | tf_op jit(solution)/shard_map/all_gather | solution.py:47
  82.5 1.3 copy-start.2
  85.0 3.7 %copy-start.4 = (s32[40,16]{0,1:T(8,128)S(1)}, s32[40,16]{0,1:T(8,128)}, u32[]{:S(2)}) copy-start(s32[40,16]{0,1:T(8,128)} %param.9) | copy-start | bytes 7684
  85.0 5.9 %copy-start.3 = (s32[40,16,2]{0,2,1:T(2,128)S(1)}, s32[40,16,2]{0,2,1:T(2,128)}, u32[]{:S(2)}) copy-start(s32[40,16,2]{0,2,1:T(2,128)} %param.8) | copy-start | bytes 15364
  85.0 34.7 %all-to-all-start = ((bf16[8,128,640]{2,1,0:T(8,128)(2,1)}), bf16[8,128,640]{2,1,0:T(8,128)(2,1)S(1)}, u32[]{:S(2)}, u32[]{:S(2)}) async-start(bf16[8,128,640]{2,1,0:T(8,128)(2,1)} %bitcast.35), calls=%async_computation | async-start | bytes 2621440 | tf_op jit(solution)/shard_map/all_to_all | solution.py:41
  119.7 1.1 copy-start
Sparse Core Ops, SparseCore 0:
  46.7 10.3 all-gather.4
  82.7 10.3 all-gather.6

commit v4 on v3

--- a/solution.py
+++ b/solution.py
@@ -81,56 +81,57 @@
     kv_blocks = all_rows // BLOCK
 
     def kernel(lists_ref, counts_ref, q_ref, k_ref, v_ref, o_ref):
-        head = pl.program_id(0)
+        for head in range(heads_per):
+            cols = pl.ds(head * HD, HD)
 
-        def per_block(i, carry):
-            slot = head * own_count + i
-            visits = counts_ref[slot]
-            row = pl.multiple_of(i * BLOCK, BLOCK)
-            q = q_ref[pl.ds(row, BLOCK), :]
-            key_starts = []
-            scores = []
-            for j in range(max_visits):
-                picked = jnp.clip(lists_ref[slot * max_visits + j], 0, kv_blocks - 1)
-                krow = pl.multiple_of(picked * BLOCK, BLOCK)
-                s = lax.dot_general(
-                    q,
-                    k_ref[pl.ds(krow, BLOCK), :],
-                    (((1,), (1,)), ((), ())),
-                    preferred_element_type=jnp.float32,
-                )
-                key_starts.append(krow)
-                scores.append(jnp.where(j < visits, s * score_scale, -jnp.inf))
-            peak = scores[0]
-            for s in scores[1:]:
-                peak = jnp.maximum(peak, s)
-            row_max = jnp.max(peak, axis=1, keepdims=True)
-            row_max = jnp.where(row_max > -jnp.inf, row_max, 0.0)
-            total = jnp.zeros((BLOCK, 1), jnp.float32)
-            acc = jnp.zeros((BLOCK, HD), jnp.float32)
-            for s, krow in zip(scores, key_starts):
-                raised = jnp.exp(s - row_max)
-                total = total + jnp.sum(raised, axis=1, keepdims=True)
-                acc = acc + jnp.dot(
-                    raised.astype(jnp.bfloat16),
-                    v_ref[pl.ds(krow, BLOCK), :],
-                    preferred_element_type=jnp.float32,
-                )
-            total = jnp.where(total > 0.0, total, 1.0)
-            o_ref[pl.ds(row, BLOCK), :] = (acc / total).astype(o_ref.dtype)
-            return carry
+            def per_block(i, carry):
+                slot = head * own_count + i
+                visits = counts_ref[slot]
+                row = pl.multiple_of(i * BLOCK, BLOCK)
+                q = q_ref[pl.ds(row, BLOCK), cols]
+                key_starts = []
+                scores = []
+                for j in range(max_visits):
+                    picked = jnp.clip(lists_ref[slot * max_visits + j], 0, kv_blocks - 1)
+                    krow = pl.multiple_of(picked * BLOCK, BLOCK)
+                    s = lax.dot_general(
+                        q,
+                        k_ref[pl.ds(krow, BLOCK), cols],
+                        (((1,), (1,)), ((), ())),
+                        preferred_element_type=jnp.float32,
+                    )
+                    key_starts.append(krow)
+                    scores.append(jnp.where(j < visits, s * score_scale, -jnp.inf))
+                peak = scores[0]
+                for s in scores[1:]:
+                    peak = jnp.maximum(peak, s)
+                row_max = jnp.max(peak, axis=1, keepdims=True)
+                row_max = jnp.where(row_max > -jnp.inf, row_max, 0.0)
+                total = jnp.zeros((BLOCK, 1), jnp.float32)
+                acc = jnp.zeros((BLOCK, HD), jnp.float32)
+                for s, krow in zip(scores, key_starts):
+                    raised = jnp.exp(s - row_max)
+                    total = total + jnp.sum(raised, axis=1, keepdims=True)
+                    acc = acc + jnp.dot(
+                        raised.astype(jnp.bfloat16),
+                        v_ref[pl.ds(krow, BLOCK), cols],
+                        preferred_element_type=jnp.float32,
+                    )
+                total = jnp.where(total > 0.0, total, 1.0)
+                o_ref[pl.ds(row, BLOCK), cols] = (acc / total).astype(o_ref.dtype)
+                return carry
 
-        lax.fori_loop(0, own_count, per_block, 0, unroll=min(own_count, 4))
+            lax.fori_loop(0, own_count, per_block, 0, unroll=min(own_count, 4))
 
     grid_spec = pltpu.PrefetchScalarGridSpec(
         num_scalar_prefetch=2,
-        grid=(heads_per,),
+        grid=(1,),
         in_specs=[
-            pl.BlockSpec((own_rows, HD), lambda h, *_: (0, h)),
-            pl.BlockSpec((all_rows, HD), lambda h, *_: (0, h)),
-            pl.BlockSpec((all_rows, HD), lambda h, *_: (0, h)),
+            pl.BlockSpec(query_rows.shape, lambda h, *_: (0, 0)),
+            pl.BlockSpec(key_rows.shape, lambda h, *_: (0, 0)),
+            pl.BlockSpec(value_rows.shape, lambda h, *_: (0, 0)),
         ],
-        out_specs=pl.BlockSpec((own_rows, HD), lambda h, *_: (0, h)),
+        out_specs=pl.BlockSpec(query_rows.shape, lambda h, *_: (0, 0)),
     )
     return pl.pallas_call(
         kernel,

time: 179 us -> 181 us (1.011)
  Pallas kernels: 14.8 us -> 16.7 us
    pallas_call x1, Pallas kernels: 14.8 us -> 16.7 us  [attend(): pl.pallas_call(kernel, grid_spec=grid_spec, out_shape=jax.ShapeDtypeStruc...]
where the time goes in v4:
time: 181 us
  blocking collectives  108 us (60%)
  waiting for transfers between devices  26.6 us (15%)
  Pallas kernels  16.7 us (9%)
  between operations  13.5 us (7%)
  local copies, waits for them, and re-layouts  11.7 us (6%)
  starting transfers between devices  3.77 us (2%)
    all_to_all x2, blocking collectives, exchange(): return lax.all_to_all(to_groups(rows_in), GROUP, 0, 0, tiled=True)  73.1 us
    all_to_all x1, blocking collectives, body(): returned = lax.all_to_all(send_back, GROUP, 0, 0, tiled=True)  35 us
    all_to_all x1, waiting for transfers between devices, exchange(): return lax.all_to_all(to_groups(rows_in), GROUP, 0, 0, tiled=True)  26.5 us
    pallas_call x1, Pallas kernels, attend(): pl.pallas_call(kernel, grid_spec=grid_spec, out_shape=jax.ShapeDtypeStruc...  16.7 us
    unnamed x12, local copies, waits for them, and re-layouts  3.76 us
    all_to_all x1, starting transfers between devices, exchange(): return lax.all_to_all(to_groups(rows_in), GROUP, 0, 0, tiled=True)  3.73 us
  transfers between devices with their start and end apart: 3, of which 1 were waited for; matrix products, arithmetic and copies ran while one was open for 3% of the time, Pallas kernels for 0%

profile of v4, /device:TPU:0, one launch (start us, length us, event | category | flops | bytes accessed | tf_op | source)
XLA Modules:
  0.0 180.5 jit_solution(14631046562268663190)
XLA Ops:
  6.5 0.0 all-gather.5.cloned.1.call-start
  6.5 1.4 copy.41
  8.0 38.5 %all_to_all.20 = bf16[8,128,640]{2,1,0:T(8,128)(2,1)} all-to-all(bf16[8,128,640]{2,1,0:T(8,128)(2,1)S(1)} %bitcast.37), channel_id=1, replica_groups=mesh['clips'=2,'seq'=4,'px'=2,'pc'=2] {'seq','px'}, dimensions={0} | all-to-all | bytes 2621440 | tf_op jit(solution)/shard_map/all_to_all | solution.py:41
  46.5 0.0 copy-start.1
  46.5 0.0 all-gather.5.cloned.1.call-update
  46.6 0.0 all-gather.7.cloned.1.call-start
  46.6 1.2 copy-done.1
  47.8 0.1 copy.40
  48.0 34.6 %all_to_all.21 = bf16[8,128,640]{2,1,0:T(8,128)(2,1)} all-to-all(bf16[8,128,640]{2,1,0:T(8,128)(2,1)S(1)} %bitcast.38), channel_id=1, replica_groups=mesh['clips'=2,'seq'=4,'px'=2,'pc'=2] {'seq','px'}, dimensions={0} | all-to-all | bytes 2621440 | tf_op jit(solution)/shard_map/all_to_all | solution.py:41
  82.5 0.0 copy-start.2
  82.5 0.0 all-gather.7.cloned.1.call-update
  82.6 1.3 copy-done.2
  83.9 1.2 copy.42
  85.0 0.0 copy-start.4
  85.0 0.0 copy-start.3
  85.0 3.7 %all-to-all-start = ((bf16[8,128,640]{2,1,0:T(8,128)(2,1)}), bf16[8,128,640]{2,1,0:T(8,128)(2,1)S(1)}, u32[]{:S(2)}, u32[]{:S(2)}) async-start(bf16[8,128,640]{2,1,0:T(8,128)(2,1)} %bitcast.35), calls=%async_computation | async-start | bytes 2621440 | tf_op jit(solution)/shard_map/all_to_all | solution.py:41
  88.8 0.0 copy-done.4
  88.8 0.1 copy.26
  88.9 0.6 gather_fusion.2
  89.5 0.1 copy.27
  89.6 0.6 gather_fusion.3
  90.1 0.1 select_bitcast_fusion.1
  90.2 0.1 copy.28
  90.3 0.6 select_n.73.counts_ref
  90.9 0.0 copy-done.3
  90.9 0.1 copy.23
  91.0 0.6 gather_fusion
  91.6 0.1 copy.24
  91.7 0.6 gather_fusion.1
  92.2 0.1 select_bitcast_fusion
  92.3 0.1 copy.25
  92.5 0.7 select_n.70.lists_ref
  93.2 26.5 %all-to-all-done = bf16[8,128,640]{2,1,0:T(8,128)(2,1)S(1)} async-done(((bf16[8,128,640]{2,1,0:T(8,128)(2,1)}), bf16[8,128,640]{2,1,0:T(8,128)(2,1)S(1)}, u32[]{:S(2)}, u32[]{:S(2)}) %all-to-all-start) | async-done | bytes 1310752 | tf_op jit(solution)/shard_map/all_to_all | solution.py:41
  119.7 0.0 copy-start
  119.7 0.0 all-gather.5.cloned.1.call-done
  119.7 0.0 all-gather.7.cloned.1.call-done
  119.7 1.1 copy-done
  120.8 16.7 %shard_map.55 = bf16[1024,640]{1,0:T(8,128)(2,1)} custom-call(s32[80]{0:T(128)} %select_n.70.lists_ref, s32[40]{0:T(128)} %select_n.73.counts_ref, bf16[1024,640]{1,0:T(8,128)(2,1)} %bitcast.39, bf16[2048,640]{1,0:T(8,128)(2,1)} %bitcast.41, bf16[2048,640]{1,0:T(8,128)(2,1)} %bitcast.42), custom_call_target="tpu_custom_call" | custom-call | tf_op jit(solution)/shard_map/pallas_call | solution.py:136
  137.4 35.0 %all_to_all.22 = bf16[8,128,640]{2,1,0:T(8,128)(2,1)S(1)} all-to-all(bf16[8,128,640]{2,1,0:T(8,128)(2,1)} %bitcast.40), channel_id=1, replica_groups=mesh['clips'=2,'seq'=4,'px'=2,'pc'=2] {'seq','px'}, dimensions={0} | all-to-all | bytes 2621440 | tf_op jit(solution)/shard_map/all_to_all | solution.py:71
  172.5 1.2 copy.36
  (6 shorter events, 0.1 us)
Async XLA Ops:
  6.5 113.2 %all-gather.5.cloned.1.call-start = ((), (), s32[]{:S(2)}) async-start(), calls=%async_computation.4 | async-start | bytes 3932160 | tf_op jit(solution)/shard_map/all_gather | solution.py:46
  46.5 1.3 copy-start.1
  46.6 73.2 %all-gather.7.cloned.1.call-start = ((), (), s32[]{:S(2)}) async-start(), calls=%async_computation.5 | async-start | bytes 3932160 | tf_op jit(solution)/shard_map/all_gather | solution.py:47
  82.5 1.3 copy-start.2
  85.0 3.7 %copy-start.4 = (s32[40,16]{0,1:T(8,128)S(1)}, s32[40,16]{0,1:T(8,128)}, u32[]{:S(2)}) copy-start(s32[40,16]{0,1:T(8,128)} %param.9) | copy-start | bytes 7684
  85.0 5.9 %copy-start.3 = (s32[40,16,2]{0,2,1:T(2,128)S(1)}, s32[40,16,2]{0,2,1:T(2,128)}, u32[]{:S(2)}) copy-start(s32[40,16,2]{0,2,1:T(2,128)} %param.8) | copy-start | bytes 15364
  85.0 34.7 %all-to-all-start = ((bf16[8,128,640]{2,1,0:T(8,128)(2,1)}), bf16[8,128,640]{2,1,0:T(8,128)(2,1)S(1)}, u32[]{:S(2)}, u32[]{:S(2)}) async-start(bf16[8,128,640]{2,1,0:T(8,128)(2,1)} %bitcast.35), calls=%async_computation | async-start | bytes 2621440 | tf_op jit(solution)/shard_map/all_to_all | solution.py:41
  119.7 1.1 copy-start
Sparse Core Ops, SparseCore 0:
  46.7 10.3 all-gather.4
  82.7 10.3 all-gather.6

commit v5 on v3

--- a/solution.py
+++ b/solution.py
@@ -43,8 +43,12 @@
     query_own = exchange(queries)
     key_part = exchange(key_rows)
     value_part = exchange(value_rows)
-    key_all = lax.all_gather(key_part, "pc", axis=1)
-    value_all = lax.all_gather(value_part, "pc", axis=1)
+    if pc_count > 1:
+        swap = [(c, (c + 1) % pc_count) for c in range(pc_count)]
+        key_other = lax.ppermute(key_part, "pc", swap)
+        value_other = lax.ppermute(value_part, "pc", swap)
+    else:
+        key_other, value_other = key_part, value_part
 
     own_count = group_count * local_blocks
     local_index = jnp.arange(own_count, dtype=jnp.int32)
@@ -55,6 +59,9 @@
     head_live = head_ids < HEADS
     head_safe = jnp.minimum(head_ids, HEADS - 1)
     own_lists = jnp.take(block_lists[head_safe], own_blocks, axis=1)
+    source_pc = own_lists // local_blocks % pc_count
+    row_block = own_lists // local_blocks // pc_count * local_blocks + own_lists % local_blocks
+    own_lists = jnp.where(source_pc == pc_place, 0, own_count) + row_block
     counts = jnp.where(
         head_live[:, None], jnp.take(block_counts[head_safe], own_blocks, axis=1), 0
     )
@@ -62,8 +69,10 @@
         own_lists.reshape(-1),
         counts.reshape(-1),
         query_own.reshape(own_count * BLOCK, heads_per * HD),
-        key_all.reshape(block_total * BLOCK, heads_per * HD),
-        value_all.reshape(block_total * BLOCK, heads_per * HD),
+        key_part.reshape(own_count * BLOCK, heads_per * HD),
+        key_other.reshape(own_count * BLOCK, heads_per * HD),
+        value_part.reshape(own_count * BLOCK, heads_per * HD),
+        value_other.reshape(own_count * BLOCK, heads_per * HD),
         max_visits,
         score_scale,
     )
@@ -73,14 +82,14 @@
     return full[:, : HEADS * HD]
 
 
-def attend(lists, counts, query_rows, key_rows, value_rows, max_visits, score_scale):
+def attend(
+    lists, counts, query_rows, key_mine, key_other, value_mine, value_other, max_visits, score_scale
+):
     own_rows = query_rows.shape[0]
-    all_rows = key_rows.shape[0]
     own_count = own_rows // BLOCK
     heads_per = query_rows.shape[1] // HD
-    kv_blocks = all_rows // BLOCK
 
-    def kernel(lists_ref, counts_ref, q_ref, k_ref, v_ref, o_ref):
+    def kernel(lists_ref, counts_ref, q_ref, k_ref, ko_ref, v_ref, vo_ref, o_ref):
         head = pl.program_id(0)
 
         def per_block(i, carry):
@@ -91,15 +100,19 @@
             key_starts = []
             scores = []
             for j in range(max_visits):
-                picked = jnp.clip(lists_ref[slot * max_visits + j], 0, kv_blocks - 1)
-                krow = pl.multiple_of(picked * BLOCK, BLOCK)
+                picked = jnp.clip(lists_ref[slot * max_visits + j], 0, 2 * own_count - 1)
+                other = picked >= own_count
+                krow = pl.multiple_of((picked - jnp.where(other, own_count, 0)) * BLOCK, BLOCK)
+                key_block = jnp.where(
+                    other, ko_ref[pl.ds(krow, BLOCK), :], k_ref[pl.ds(krow, BLOCK), :]
+                )
                 s = lax.dot_general(
                     q,
-                    k_ref[pl.ds(krow, BLOCK), :],
+                    key_block,
                     (((1,), (1,)), ((), ())),
                     preferred_element_type=jnp.float32,
                 )
-                key_starts.append(krow)
+                key_starts.append((krow, other))
                 scores.append(jnp.where(j < visits, s * score_scale, -jnp.inf))
             peak = scores[0]
             for s in scores[1:]:
@@ -108,12 +121,14 @@
             row_max = jnp.where(row_max > -jnp.inf, row_max, 0.0)
             total = jnp.zeros((BLOCK, 1), jnp.float32)
             acc = jnp.zeros((BLOCK, HD), jnp.float32)
-            for s, krow in zip(scores, key_starts):
+            for s, (krow, other) in zip(scores, key_starts):
                 raised = jnp.exp(s - row_max)
                 total = total + jnp.sum(raised, axis=1, keepdims=True)
                 acc = acc + jnp.dot(
                     raised.astype(jnp.bfloat16),
-                    v_ref[pl.ds(krow, BLOCK), :],
+                    jnp.where(
+                        other, vo_ref[pl.ds(krow, BLOCK), :], v_ref[pl.ds(krow, BLOCK), :]
+                    ),
                     preferred_element_type=jnp.float32,
                 )
             total = jnp.where(total > 0.0, total, 1.0)
@@ -127,8 +142,10 @@
         grid=(heads_per,),
         in_specs=[
             pl.BlockSpec((own_rows, HD), lambda h, *_: (0, h)),
-            pl.BlockSpec((all_rows, HD), lambda h, *_: (0, h)),
-            pl.BlockSpec((all_rows, HD), lambda h, *_: (0, h)),
+            pl.BlockSpec((own_rows, HD), lambda h, *_: (0, h)),
+            pl.BlockSpec((own_rows, HD), lambda h, *_: (0, h)),
+            pl.BlockSpec((own_rows, HD), lambda h, *_: (0, h)),
+            pl.BlockSpec((own_rows, HD), lambda h, *_: (0, h)),
         ],
         out_specs=pl.BlockSpec((own_rows, HD), lambda h, *_: (0, h)),
     )
@@ -136,7 +153,7 @@
         kernel,
         grid_spec=grid_spec,
         out_shape=jax.ShapeDtypeStruct(query_rows.shape, jnp.bfloat16),
-    )(lists, counts, query_rows, key_rows, value_rows)
+    )(lists, counts, query_rows, key_mine, key_other, value_mine, value_other)
 
 
 def solution(mesh):

time: 179 us -> 164 us (0.916)
  blocking collectives: 108 us -> 35.1 us
  waiting for transfers between devices: 26.6 us -> 85.4 us
  between operations: 13.5 us -> 0.08 us
  starting transfers between devices: 3.77 us -> 15.9 us
    all_to_all x2 -> x0, blocking collectives: 73.1 us -> none  [exchange(): return lax.all_to_all(to_groups(rows_in), GROUP, 0, 0, tiled=True)]
    all_to_all x1 -> x3, waiting for transfers between devices: 26.5 us -> 85.4 us  [exchange(): return lax.all_to_all(to_groups(rows_in), GROUP, 0, 0, tiled=True)]
    all_to_all x1 -> x3, starting transfers between devices: 3.73 us -> 15.4 us  [exchange(): return lax.all_to_all(to_groups(rows_in), GROUP, 0, 0, tiled=True)]
    unnamed x12, local copies, waits for them, and re-layouts: 3.76 us -> 0.19 us
    another operation x3, local copies, waits for them, and re-layouts: 2.74 us -> 6.18 us  [to_groups(): widened.reshape(tok_rows, group_count, heads_per * HD).transpose(1, 0, 2)]
  transfers between devices with their start and end apart: 3 -> 5, of which waited for: 1 -> 3; matrix products, arithmetic and copies ran while one was open for 3% -> 5% of each run, Pallas kernels for 0% -> 0%
where the time goes in v5:
time: 164 us; the launch traced here: 163 us
  waiting for transfers between devices  85.4 us (52%)
  blocking collectives  35.1 us (21%)
  starting transfers between devices  15.9 us (10%)
  Pallas kernels  14.9 us (9%)
  local copies, waits for them, and re-layouts  11 us (7%)
    all_to_all x3, waiting for transfers between devices, exchange(): return lax.all_to_all(to_groups(rows_in), GROUP, 0, 0, tiled=True)  85.4 us
    all_to_all x1, blocking collectives, body(): returned = lax.all_to_all(send_back, GROUP, 0, 0, tiled=True)  35.1 us
    all_to_all x3, starting transfers between devices, exchange(): return lax.all_to_all(to_groups(rows_in), GROUP, 0, 0, tiled=True)  15.4 us
    pallas_call x1, Pallas kernels, attend(): pl.pallas_call(kernel, grid_spec=grid_spec, out_shape=jax.ShapeDtypeStruc...  14.9 us
    another operation x3, local copies, waits for them, and re-layouts, to_groups(): widened.reshape(tok_rows, group_count, heads_per * HD).transpose(1, 0, 2)  6.18 us
  transfers between devices with their start and end apart: 5, of which 3 were waited for; matrix products, arithmetic and copies ran while one was open for 5% of the time, Pallas kernels for 0%

profile of v5, /device:TPU:0, one launch (start us, length us, event | category | flops | bytes accessed | tf_op | source)
XLA Modules:
  0.0 163.2 jit_solution(411062679938034838)
XLA Ops:
  0.0 2.5 %copy.41 = bf16[16,8,8,640]{3,2,0,1:T(8,128)(2,1)} copy(bf16[16,8,8,640]{3,2,1,0:T(8,128)(2,1)} %bitcast.42) | data formatting | bytes 2621440 | tf_op jit(solution)/shard_map/reshape;reshape | solution.py:38
  2.5 0.0 copy-start.2
  2.5 7.4 %all-to-all-start.1 = ((bf16[8,128,640]{2,1,0:T(8,128)(2,1)}), bf16[8,128,640]{2,1,0:T(8,128)(2,1)S(1)}, u32[]{:S(2)}, u32[]{:S(2)}) async-start(bf16[8,128,640]{2,1,0:T(8,128)(2,1)} %bitcast.35), calls=%async_computation.1 | async-start | bytes 2621440 | tf_op jit(solution)/shard_map/all_to_all | solution.py:41
  9.9 0.0 copy-done.2
  9.9 1.2 copy.40
  11.1 30.2 %all-to-all-done.1 = bf16[8,128,640]{2,1,0:T(8,128)(2,1)S(1)} async-done(((bf16[8,128,640]{2,1,0:T(8,128)(2,1)}), bf16[8,128,640]{2,1,0:T(8,128)(2,1)S(1)}, u32[]{:S(2)}, u32[]{:S(2)}) %all-to-all-start.1) | async-done | bytes 1310752 | tf_op jit(solution)/shard_map/all_to_all | solution.py:41
  41.3 0.0 copy-start
  41.3 3.6 %all-to-all-start.2 = ((bf16[8,128,640]{2,1,0:T(8,128)(2,1)}), bf16[8,128,640]{2,1,0:T(8,128)(2,1)S(1)}, u32[]{:S(2)}, u32[]{:S(2)}) async-start(bf16[8,128,640]{2,1,0:T(8,128)(2,1)} %bitcast.33), calls=%async_computation.2 | async-start | bytes 2621440 | tf_op jit(solution)/shard_map/all_to_all | solution.py:41
  44.9 2.5 %copy.42 = bf16[16,8,8,640]{3,2,0,1:T(8,128)(2,1)} copy(bf16[16,8,8,640]{3,2,1,0:T(8,128)(2,1)} %bitcast.44) | data formatting | bytes 2621440 | tf_op jit(solution)/shard_map/reshape;reshape | solution.py:38
  47.4 29.1 %all-to-all-done.2 = bf16[8,128,640]{2,1,0:T(8,128)(2,1)S(1)} async-done(((bf16[8,128,640]{2,1,0:T(8,128)(2,1)}), bf16[8,128,640]{2,1,0:T(8,128)(2,1)S(1)}, u32[]{:S(2)}, u32[]{:S(2)}) %all-to-all-start.2) | async-done | bytes 1310752 | tf_op jit(solution)/shard_map/all_to_all | solution.py:41
  76.5 0.0 copy-start.1
  76.5 0.0 copy-start.4
  76.5 0.0 copy-start.3
  76.5 4.4 %all-to-all-start = ((bf16[8,128,640]{2,1,0:T(8,128)(2,1)}), bf16[8,128,640]{2,1,0:T(8,128)(2,1)}, u32[]{:S(2)}, u32[]{:S(2)}) async-start(bf16[8,128,640]{2,1,0:T(8,128)(2,1)} %bitcast.37), calls=%async_computation | async-start | bytes 2621440 | tf_op jit(solution)/shard_map/all_to_all | solution.py:41
  80.9 0.0 copy-done.4
  80.9 0.1 copy.26
  81.0 0.0 copy-done.1
  81.0 0.0 collective-permute-start.1
  81.0 0.0 copy-done
  81.0 0.5 collective-permute-start
  81.5 0.6 gather_fusion.2
  82.1 0.1 copy.27
  82.2 0.6 gather_fusion.3
  82.8 0.1 select_bitcast_fusion.1
  82.9 0.1 copy.28
  82.9 0.6 select_n.104.counts_ref
  83.6 0.0 copy-done.3
  83.6 0.1 copy.23
  83.7 0.6 gather_fusion
  84.2 0.1 copy.24
  84.3 0.6 gather_fusion.1
  84.9 0.1 select_bitcast_fusion
  85.0 0.1 copy.25
  85.1 0.1 select_n.97
  85.2 0.6 fusion.lists_ref
  85.8 26.1 %all-to-all-done = bf16[8,128,640]{2,1,0:T(8,128)(2,1)} async-done(((bf16[8,128,640]{2,1,0:T(8,128)(2,1)}), bf16[8,128,640]{2,1,0:T(8,128)(2,1)}, u32[]{:S(2)}, u32[]{:S(2)}) %all-to-all-start) | async-done | bytes 1310752 | tf_op jit(solution)/shard_map/all_to_all | solution.py:41
  111.9 0.0 collective-permute-done.1
  111.9 0.0 collective-permute-done
  111.9 14.9 %shard_map.55 = bf16[1024,640]{1,0:T(8,128)(2,1)} custom-call(s32[80]{0:T(128)} %fusion.lists_ref, s32[40]{0:T(128)} %select_n.104.counts_ref, bf16[1024,640]{1,0:T(8,128)(2,1)} %bitcast.5.q_ref, bf16[1024,640]{1,0:T(8,128)(2,1)} %bitcast.39, bf16[1024,640]{1,0:T(8,128)(2,1)} %bitcast.8.ko_ref, bf16[1024,640]{1,0:T(8,128)(2,1)} %bitcast.40, ...), custom_call_target="tpu_custom_call" | custom-call | tf_op jit(solution)/shard_map/pallas_call | solution.py:152
  126.8 35.1 %all_to_all.20 = bf16[8,128,640]{2,1,0:T(8,128)(2,1)S(1)} all-to-all(bf16[8,128,640]{2,1,0:T(8,128)(2,1)} %bitcast.41), channel_id=1, replica_groups=mesh['clips'=2,'seq'=4,'px'=2,'pc'=2] {'seq','px'}, dimensions={0} | all-to-all | bytes 2621440 | tf_op jit(solution)/shard_map/all_to_all | solution.py:80
  161.9 1.2 copy.36
  (6 shorter events, 0.1 us)
Async XLA Ops:
  2.5 7.4 %copy-start.2 = (bf16[128,5120]{1,0:T(8,128)(2,1)S(1)}, bf16[128,5120]{1,0:T(8,128)(2,1)}, u32[]{:S(2)}) copy-start(bf16[128,5120]{1,0:T(8,128)(2,1)} %param.7) | copy-start | bytes 3932164
  2.5 38.8 %all-to-all-start.1 = ((bf16[8,128,640]{2,1,0:T(8,128)(2,1)}), bf16[8,128,640]{2,1,0:T(8,128)(2,1)S(1)}, u32[]{:S(2)}, u32[]{:S(2)}) async-start(bf16[8,128,640]{2,1,0:T(8,128)(2,1)} %bitcast.35), calls=%async_computation.1 | async-start | bytes 2621440 | tf_op jit(solution)/shard_map/all_to_all | solution.py:41
  41.3 39.8 %copy-start = (bf16[8,128,640]{2,1,0:T(8,128)(2,1)}, bf16[8,128,640]{2,1,0:T(8,128)(2,1)S(1)}, u32[]{:S(2)}) copy-start(bf16[8,128,640]{2,1,0:T(8,128)(2,1)S(1)} %all-to-all-done.1) | copy-start | bytes 3932164
  41.3 35.2 %all-to-all-start.2 = ((bf16[8,128,640]{2,1,0:T(8,128)(2,1)}), bf16[8,128,640]{2,1,0:T(8,128)(2,1)S(1)}, u32[]{:S(2)}, u32[]{:S(2)}) async-start(bf16[8,128,640]{2,1,0:T(8,128)(2,1)} %bitcast.33), calls=%async_computation.2 | async-start | bytes 2621440 | tf_op jit(solution)/shard_map/all_to_all | solution.py:41
  76.5 4.5 %copy-start.1 = (bf16[8,128,640]{2,1,0:T(8,128)(2,1)}, bf16[8,128,640]{2,1,0:T(8,128)(2,1)S(1)}, u32[]{:S(2)}) copy-start(bf16[8,128,640]{2,1,0:T(8,128)(2,1)S(1)} %all-to-all-done.2) | copy-start | bytes 3932164
  76.5 4.4 %copy-start.4 = (s32[40,16]{0,1:T(8,128)S(1)}, s32[40,16]{0,1:T(8,128)}, u32[]{:S(2)}) copy-start(s32[40,16]{0,1:T(8,128)} %param.9) | copy-start | bytes 7684
  76.5 7.1 %copy-start.3 = (s32[40,16,2]{0,2,1:T(2,128)S(1)}, s32[40,16,2]{0,2,1:T(2,128)}, u32[]{:S(2)}) copy-start(s32[40,16,2]{0,2,1:T(2,128)} %param.8) | copy-start | bytes 15364
  76.5 35.5 %all-to-all-start = ((bf16[8,128,640]{2,1,0:T(8,128)(2,1)}), bf16[8,128,640]{2,1,0:T(8,128)(2,1)}, u32[]{:S(2)}, u32[]{:S(2)}) async-start(bf16[8,128,640]{2,1,0:T(8,128)(2,1)} %bitcast.37), calls=%async_computation | async-start | bytes 2621440 | tf_op jit(solution)/shard_map/all_to_all | solution.py:41
  81.0 31.0 %collective-permute-start.1 = (bf16[8,128,640]{2,1,0:T(8,128)(2,1)S(1)}, bf16[8,128,640]{2,1,0:T(8,128)(2,1)}, u32[]{:S(2)}, u32[]{:S(2)}) collective-permute-start(bf16[8,128,640]{2,1,0:T(8,128)(2,1)S(1)} %all-to-all-done.2), channel_id=1, source_target_pairs={{0,1},{1,0},{2,3},{3,2},{4,5},{5,4},{6,7},{7,6},{8,9},{9,8},{10,11... | collective-permute-start | bytes 3932168 | tf_op jit(solution)/shard_map/ppermute | solution.py:49
  81.0 30.9 %collective-permute-start = (bf16[8,128,640]{2,1,0:T(8,128)(2,1)S(1)}, bf16[8,128,640]{2,1,0:T(8,128)(2,1)}, u32[]{:S(2)}, u32[]{:S(2)}) collective-permute-start(bf16[8,128,640]{2,1,0:T(8,128)(2,1)S(1)} %all-to-all-done.1), channel_id=1, source_target_pairs={{0,1},{1,0},{2,3},{3,2},{4,5},{5,4},{6,7},{7,6},{8,9},{9,8},{10,11... | collective-permute-start | bytes 3932168 | tf_op jit(solution)/shard_map/ppermute | solution.py:48

commit v6 on v5

--- a/solution.py
+++ b/solution.py
@@ -40,15 +40,15 @@
     def exchange(rows_in):
         return lax.all_to_all(to_groups(rows_in), GROUP, 0, 0, tiled=True)
 
-    query_own = exchange(queries)
-    key_part = exchange(key_rows)
-    value_part = exchange(value_rows)
+    pair_mine = lax.all_to_all(
+        jnp.stack([to_groups(key_rows), to_groups(value_rows)], axis=1), GROUP, 0, 0, tiled=True
+    )
     if pc_count > 1:
         swap = [(c, (c + 1) % pc_count) for c in range(pc_count)]
-        key_other = lax.ppermute(key_part, "pc", swap)
-        value_other = lax.ppermute(value_part, "pc", swap)
+        pair_other = lax.ppermute(pair_mine, "pc", swap)
     else:
-        key_other, value_other = key_part, value_part
+        pair_other = pair_mine
+    query_own = exchange(queries)
 
     own_count = group_count * local_blocks
     local_index = jnp.arange(own_count, dtype=jnp.int32)
@@ -69,10 +69,8 @@
         own_lists.reshape(-1),
         counts.reshape(-1),
         query_own.reshape(own_count * BLOCK, heads_per * HD),
-        key_part.reshape(own_count * BLOCK, heads_per * HD),
-        key_other.reshape(own_count * BLOCK, heads_per * HD),
-        value_part.reshape(own_count * BLOCK, heads_per * HD),
-        value_other.reshape(own_count * BLOCK, heads_per * HD),
+        pair_mine,
+        pair_other,
         max_visits,
         score_scale,
     )
@@ -82,14 +80,14 @@
     return full[:, : HEADS * HD]
 
 
-def attend(
-    lists, counts, query_rows, key_mine, key_other, value_mine, value_other, max_visits, score_scale
-):
+def attend(lists, counts, query_rows, pair_mine, pair_other, max_visits, score_scale):
     own_rows = query_rows.shape[0]
     own_count = own_rows // BLOCK
     heads_per = query_rows.shape[1] // HD
+    group_count, _, tok_rows, _ = pair_mine.shape
+    local_blocks = tok_rows // BLOCK
 
-    def kernel(lists_ref, counts_ref, q_ref, k_ref, ko_ref, v_ref, vo_ref, o_ref):
+    def kernel(lists_ref, counts_ref, q_ref, mine_ref, other_ref, o_ref):
         head = pl.program_id(0)
 
         def per_block(i, carry):
@@ -102,9 +100,13 @@
             for j in range(max_visits):
                 picked = jnp.clip(lists_ref[slot * max_visits + j], 0, 2 * own_count - 1)
                 other = picked >= own_count
-                krow = pl.multiple_of((picked - jnp.where(other, own_count, 0)) * BLOCK, BLOCK)
+                held = picked - jnp.where(other, own_count, 0)
+                source = held // local_blocks
+                krow = pl.multiple_of(held % local_blocks * BLOCK, BLOCK)
                 key_block = jnp.where(
-                    other, ko_ref[pl.ds(krow, BLOCK), :], k_ref[pl.ds(krow, BLOCK), :]
+                    other,
+                    other_ref[source, 0, pl.ds(krow, BLOCK), :],
+                    mine_ref[source, 0, pl.ds(krow, BLOCK), :],
                 )
                 s = lax.dot_general(
                     q,
@@ -112,7 +114,7 @@
                     (((1,), (1,)), ((), ())),
                     preferred_element_type=jnp.float32,
                 )
-                key_starts.append((krow, other))
+                key_starts.append((source, krow, other))
                 scores.append(jnp.where(j < visits, s * score_scale, -jnp.inf))
             peak = scores[0]
             for s in scores[1:]:
@@ -121,13 +123,15 @@
             row_max = jnp.where(row_max > -jnp.inf, row_max, 0.0)
             total = jnp.zeros((BLOCK, 1), jnp.float32)
             acc = jnp.zeros((BLOCK, HD), jnp.float32)
-            for s, (krow, other) in zip(scores, key_starts):
+            for s, (source, krow, other) in zip(scores, key_starts):
                 raised = jnp.exp(s - row_max)
                 total = total + jnp.sum(raised, axis=1, keepdims=True)
                 acc = acc + jnp.dot(
                     raised.astype(jnp.bfloat16),
                     jnp.where(
-                        other, vo_ref[pl.ds(krow, BLOCK), :], v_ref[pl.ds(krow, BLOCK), :]
+                        other,
+                        other_ref[source, 1, pl.ds(krow, BLOCK), :],
+                        mine_ref[source, 1, pl.ds(krow, BLOCK), :],
                     ),
                     preferred_element_type=jnp.float32,
                 )
@@ -142,10 +146,8 @@
         grid=(heads_per,),
         in_specs=[
             pl.BlockSpec((own_rows, HD), lambda h, *_: (0, h)),
-            pl.BlockSpec((own_rows, HD), lambda h, *_: (0, h)),
-            pl.BlockSpec((own_rows, HD), lambda h, *_: (0, h)),
-            pl.BlockSpec((own_rows, HD), lambda h, *_: (0, h)),
-            pl.BlockSpec((own_rows, HD), lambda h, *_: (0, h)),
+            pl.BlockSpec((group_count, 2, tok_rows, HD), lambda h, *_: (0, 0, 0, h)),
+            pl.BlockSpec((group_count, 2, tok_rows, HD), lambda h, *_: (0, 0, 0, h)),
         ],
         out_specs=pl.BlockSpec((own_rows, HD), lambda h, *_: (0, h)),
     )
@@ -153,7 +155,7 @@
         kernel,
         grid_spec=grid_spec,
         out_shape=jax.ShapeDtypeStruct(query_rows.shape, jnp.bfloat16),
-    )(lists, counts, query_rows, key_mine, key_other, value_mine, value_other)
+    )(lists, counts, query_rows, pair_mine, pair_other)
 
 
 def solution(mesh):

time: 164 us -> 163 us (level)
  blocking collectives: 35.1 us -> 102 us
  waiting for transfers between devices: 85.4 us -> 27.1 us
  starting transfers between devices: 15.9 us -> 4.42 us
  local copies, waits for them, and re-layouts: 11 us -> 13.5 us
    all_to_all x0 -> x1, blocking collectives: none -> 66.7 us  [body(): lax.all_to_all(jnp.stack([to_groups(key_rows), to_groups(value_rows)], ax...]
    all_to_all x3 -> x1, waiting for transfers between devices: 85.4 us -> 27.1 us  [exchange(): return lax.all_to_all(to_groups(rows_in), GROUP, 0, 0, tiled=True)]
    all_to_all x3 -> x1, starting transfers between devices: 15.4 us -> 4.42 us  [exchange(): return lax.all_to_all(to_groups(rows_in), GROUP, 0, 0, tiled=True)]
    unnamed x12, local copies, waits for them, and re-layouts: 0.19 us -> 5.05 us
    another operation x3, local copies, waits for them, and re-layouts: 6.18 us -> 3.73 us  [to_groups(): widened.reshape(tok_rows, group_count, heads_per * HD).transpose(1, 0, 2)]
  transfers between devices with their start and end apart: 5 -> 2, of which waited for: 3 -> 1; matrix products, arithmetic and copies ran while one was open for 5% -> 4% of each run, Pallas kernels for 0% -> 0%
where the time goes in v6:
time: 163 us
  blocking collectives  102 us (63%)
  waiting for transfers between devices  27.1 us (17%)
  Pallas kernels  14.8 us (9%)
  local copies, waits for them, and re-layouts  13.5 us (8%)
  starting transfers between devices  4.42 us (3%)
    all_to_all x1, blocking collectives, body(): lax.all_to_all(jnp.stack([to_groups(key_rows), to_groups(value_rows)], ax...  66.7 us
    all_to_all x1, blocking collectives, body(): returned = lax.all_to_all(send_back, GROUP, 0, 0, tiled=True)  35.1 us
    all_to_all x1, waiting for transfers between devices, exchange(): return lax.all_to_all(to_groups(rows_in), GROUP, 0, 0, tiled=True)  27.1 us
    pallas_call x1, Pallas kernels, attend(): pl.pallas_call(kernel, grid_spec=grid_spec, out_shape=jax.ShapeDtypeStruc...  14.8 us
    unnamed x12, local copies, waits for them, and re-layouts  5.05 us
    all_to_all x1, starting transfers between devices, exchange(): return lax.all_to_all(to_groups(rows_in), GROUP, 0, 0, tiled=True)  4.42 us
    another operation x3, local copies, waits for them, and re-layouts, to_groups(): widened.reshape(tok_rows, group_count, heads_per * HD).transpose(1, 0, 2)  3.73 us
  transfers between devices with their start and end apart: 2, of which 1 were waited for; matrix products, arithmetic and copies ran while one was open for 4% of the time, Pallas kernels for 0%

profile of v6, /device:TPU:0, one launch (start us, length us, event | category | flops | bytes accessed | tf_op | source)
XLA Modules:
  0.0 162.7 jit_solution(14796843378180397285)
XLA Ops:
  0.0 1.8 %copy.30 = bf16[128,5120]{0,1:T(8,128)(2,1)S(1)} copy(bf16[128,5120]{1,0:T(8,128)(2,1)} %param.6) | data formatting | bytes 2621440 | tf_op args[1]
  1.8 0.7 copy.31
  2.5 2.4 %copy.32 = bf16[128,5120]{0,1:T(8,128)(2,1)} copy(bf16[128,5120]{1,0:T(8,128)(2,1)} %param.7) | data formatting | bytes 2621440 | tf_op args[2]
  4.9 1.7 %copy.33 = bf16[128,8,640]{2,0,1:T(8,128)(2,1)S(1)} copy(bf16[128,8,640]{0,2,1:T(8,128)(2,1)} %bitcast.33) | data formatting | bytes 2621440 | tf_op jit(solution)/shard_map/reshape;reshape | solution.py:38
  6.6 0.3 pad_maximum_fusion
  6.9 0.0 copy-start.1
  6.9 66.7 %all_to_all.15.mine_ref = bf16[8,2,128,640]{3,2,1,0:T(8,128)(2,1)S(1)} all-to-all(bf16[8,2,128,640]{3,2,1,0:T(8,128)(2,1)S(1)} %pad_maximum_fusion), channel_id=1, replica_groups=mesh['clips'=2,'seq'=4,'px'=2,'pc'=2] {'seq','px'}, dimensions={0} | all-to-all | bytes 5242880 | tf_op jit(solution)/shard_map/all_to_all | solution.py:43
  73.6 0.0 copy-start
  73.6 0.0 collective-permute-start
  73.6 0.0 copy-done.1
  73.6 1.3 copy.38
  74.9 0.7 copy-done
  75.6 0.0 copy-start.3
  75.6 0.0 copy-start.2
  75.6 4.4 %all-to-all-start = ((bf16[8,128,640]{2,1,0:T(8,128)(2,1)}), bf16[8,128,640]{2,1,0:T(8,128)(2,1)}, u32[]{:S(2)}, u32[]{:S(2)}) async-start(bf16[8,128,640]{2,1,0:T(8,128)(2,1)} %bitcast.30), calls=%async_computation | async-start | bytes 2621440 | tf_op jit(solution)/shard_map/all_to_all | solution.py:41
  80.0 0.0 copy-done.3
  80.0 0.1 copy.26
  80.1 0.6 gather_fusion.2
  80.7 0.1 copy.27
  80.8 0.6 gather_fusion.3
  81.4 0.1 select_bitcast_fusion.1
  81.4 0.1 copy.28
  81.5 0.7 select_n.104.counts_ref
  82.2 0.0 copy-done.2
  82.2 0.1 copy.23
  82.3 0.6 gather_fusion
  82.9 0.1 copy.24
  83.0 0.6 gather_fusion.1
  83.5 0.1 select_bitcast_fusion
  83.6 0.1 copy.25
  83.8 0.1 select_n.97
  83.9 0.6 fusion.lists_ref
  84.5 27.1 %all-to-all-done = bf16[8,128,640]{2,1,0:T(8,128)(2,1)} async-done(((bf16[8,128,640]{2,1,0:T(8,128)(2,1)}), bf16[8,128,640]{2,1,0:T(8,128)(2,1)}, u32[]{:S(2)}, u32[]{:S(2)}) %all-to-all-start) | async-done | bytes 1310752 | tf_op jit(solution)/shard_map/all_to_all | solution.py:41
  111.5 0.0 collective-permute-done.other_ref
  111.5 14.8 %shard_map.55 = bf16[1024,640]{1,0:T(8,128)(2,1)} custom-call(s32[80]{0:T(128)} %fusion.lists_ref, s32[40]{0:T(128)} %select_n.104.counts_ref, bf16[1024,640]{1,0:T(8,128)(2,1)} %bitcast.5.q_ref, bf16[8,2,128,640]{3,2,1,0:T(8,128)(2,1)} %copy-done, bf16[8,2,128,640]{3,2,1,0:T(8,128)(2,1)} %collective-permute-done.other_ref), custom_call_target="tpu_custom_call" | custom-call | tf_op jit(solution)/shard_map/pallas_call | solution.py:154
  126.4 35.1 %all_to_all.16 = bf16[8,128,640]{2,1,0:T(8,128)(2,1)S(1)} all-to-all(bf16[8,128,640]{2,1,0:T(8,128)(2,1)} %bitcast.34), channel_id=1, replica_groups=mesh['clips'=2,'seq'=4,'px'=2,'pc'=2] {'seq','px'}, dimensions={0} | all-to-all | bytes 2621440 | tf_op jit(solution)/shard_map/all_to_all | solution.py:78
  161.5 1.2 copy.36
  (6 shorter events, 0.1 us)
Async XLA Ops:
  6.9 66.7 %copy-start.1 = (bf16[128,5120]{1,0:T(8,128)(2,1)S(1)}, bf16[128,5120]{1,0:T(8,128)(2,1)}, u32[]{:S(2)}) copy-start(bf16[128,5120]{1,0:T(8,128)(2,1)} %param.5) | copy-start | bytes 3932164
  73.6 2.0 %copy-start = (bf16[8,2,128,640]{3,2,1,0:T(8,128)(2,1)}, bf16[8,2,128,640]{3,2,1,0:T(8,128)(2,1)S(1)}, u32[]{:S(2)}) copy-start(bf16[8,2,128,640]{3,2,1,0:T(8,128)(2,1)S(1)} %all_to_all.15.mine_ref) | copy-start | bytes 7864324
  73.6 38.0 %collective-permute-start = (bf16[8,2,128,640]{3,2,1,0:T(8,128)(2,1)S(1)}, bf16[8,2,128,640]{3,2,1,0:T(8,128)(2,1)}, u32[]{:S(2)}, u32[]{:S(2)}) collective-permute-start(bf16[8,2,128,640]{3,2,1,0:T(8,128)(2,1)S(1)} %all_to_all.15.mine_ref), channel_id=1, source_target_pairs={{0,1},{1,0},{2,3},{3,2},{4,5},{5,4},{6,7},{7,6},{8,9},{9,8},{10,11... | collective-permute-start | bytes 7864328 | tf_op jit(solution)/shard_map/ppermute | solution.py:48
  75.6 4.4 %copy-start.3 = (s32[40,16]{0,1:T(8,128)S(1)}, s32[40,16]{0,1:T(8,128)}, u32[]{:S(2)}) copy-start(s32[40,16]{0,1:T(8,128)} %param.9) | copy-start | bytes 7684
  75.6 6.6 %copy-start.2 = (s32[40,16,2]{0,2,1:T(2,128)S(1)}, s32[40,16,2]{0,2,1:T(2,128)}, u32[]{:S(2)}) copy-start(s32[40,16,2]{0,2,1:T(2,128)} %param.8) | copy-start | bytes 15364
  75.6 35.9 %all-to-all-start = ((bf16[8,128,640]{2,1,0:T(8,128)(2,1)}), bf16[8,128,640]{2,1,0:T(8,128)(2,1)}, u32[]{:S(2)}, u32[]{:S(2)}) async-start(bf16[8,128,640]{2,1,0:T(8,128)(2,1)} %bitcast.30), calls=%async_computation | async-start | bytes 2621440 | tf_op jit(solution)/shard_map/all_to_all | solution.py:41

commit v7 on v6

--- a/solution.py
+++ b/solution.py
@@ -37,9 +37,6 @@
             widened = jnp.pad(widened, ((0, 0), (0, padded_heads - HEADS), (0, 0)))
         return widened.reshape(tok_rows, group_count, heads_per * HD).transpose(1, 0, 2)
 
-    def exchange(rows_in):
-        return lax.all_to_all(to_groups(rows_in), GROUP, 0, 0, tiled=True)
-
     pair_mine = lax.all_to_all(
         jnp.stack([to_groups(key_rows), to_groups(value_rows)], axis=1), GROUP, 0, 0, tiled=True
     )
@@ -48,7 +45,7 @@
         pair_other = lax.ppermute(pair_mine, "pc", swap)
     else:
         pair_other = pair_mine
-    query_own = exchange(queries)
+    query_groups = to_groups(queries)
 
     own_count = group_count * local_blocks
     local_index = jnp.arange(own_count, dtype=jnp.int32)
@@ -65,22 +62,35 @@
     counts = jnp.where(
         head_live[:, None], jnp.take(block_counts[head_safe], own_blocks, axis=1), 0
     )
-    mixed_out = attend(
-        own_lists.reshape(-1),
-        counts.reshape(-1),
-        query_own.reshape(own_count * BLOCK, heads_per * HD),
-        pair_mine,
-        pair_other,
-        max_visits,
-        score_scale,
-    )
-    send_back = mixed_out.reshape(group_count, tok_rows, heads_per * HD)
-    returned = lax.all_to_all(send_back, GROUP, 0, 0, tiled=True)
+    split = (heads_per + 1) // 2
+    chunks = [(0, split), (split, heads_per)] if heads_per > 1 else [(0, heads_per)]
+    pieces = []
+    for head_lo, head_hi in chunks:
+        width = (head_hi - head_lo) * HD
+        query_own = lax.all_to_all(
+            query_groups[:, :, head_lo * HD : head_hi * HD], GROUP, 0, 0, tiled=True
+        )
+        mixed_out = attend(
+            own_lists[head_lo:head_hi].reshape(-1),
+            counts[head_lo:head_hi].reshape(-1),
+            query_own.reshape(own_count * BLOCK, width),
+            pair_mine,
+            pair_other,
+            head_lo,
+            max_visits,
+            score_scale,
+        )
+        pieces.append(
+            lax.all_to_all(
+                mixed_out.reshape(group_count, tok_rows, width), GROUP, 0, 0, tiled=True
+            )
+        )
+    returned = jnp.concatenate(pieces, axis=2)
     full = returned.transpose(1, 0, 2).reshape(tok_rows, padded_heads * HD)
     return full[:, : HEADS * HD]
 
 
-def attend(lists, counts, query_rows, pair_mine, pair_other, max_visits, score_scale):
+def attend(lists, counts, query_rows, pair_mine, pair_other, head_lo, max_visits, score_scale):
     own_rows = query_rows.shape[0]
     own_count = own_rows // BLOCK
     heads_per = query_rows.shape[1] // HD
@@ -146,8 +156,8 @@
         grid=(heads_per,),
         in_specs=[
             pl.BlockSpec((own_rows, HD), lambda h, *_: (0, h)),
-            pl.BlockSpec((group_count, 2, tok_rows, HD), lambda h, *_: (0, 0, 0, h)),
-            pl.BlockSpec((group_count, 2, tok_rows, HD), lambda h, *_: (0, 0, 0, h)),
+            pl.BlockSpec((group_count, 2, tok_rows, HD), lambda h, *_: (0, 0, 0, h + head_lo)),
+            pl.BlockSpec((group_count, 2, tok_rows, HD), lambda h, *_: (0, 0, 0, h + head_lo)),
         ],
         out_specs=pl.BlockSpec((own_rows, HD), lambda h, *_: (0, h)),
     )

time: 163 us -> 163 us (level)
  blocking collectives: 102 us -> 90.6 us
  local copies, waits for them, and re-layouts: 13.5 us -> 19.9 us
  starting transfers between devices: 4.42 us -> 10.8 us
  waiting for transfers between devices: 27.1 us -> 23.3 us
  Pallas kernels: 14.8 us -> 17.6 us
    all_to_all x1, blocking collectives: 35.1 us -> 23.9 us  [body(): lax.all_to_all(mixed_out.reshape(group_count, tok_rows, width), GROUP, 0,...]
    all_to_all x1 -> x3, starting transfers between devices: 4.42 us -> 10.8 us  [the longest x2 7.22 us: body(): lax.all_to_all(query_groups[:, :, head_lo * HD:head_hi * HD], GROUP, 0, 0...]
    all_to_all x1 -> x3, waiting for transfers between devices: 27.1 us -> 23.3 us  [the longest x2 20.1 us: body(): lax.all_to_all(query_groups[:, :, head_lo * HD:head_hi * HD], GROUP, 0, 0...]
    slice x0 -> x8, local copies, waits for them, and re-layouts: none -> 3.58 us  [the longest x2 3 us: body(): query_groups[:, :, head_lo * HD:head_hi * HD]]
    pallas_call x1 -> x2, Pallas kernels: 14.8 us -> 17.6 us  [attend(): pl.pallas_call(kernel, grid_spec=grid_spec, out_shape=jax.ShapeDtypeStruc...]
    unnamed x12 -> x18, local copies, waits for them, and re-layouts: 5.05 us -> 7.59 us
    reshape x0 -> x4, local copies, waits for them, and re-layouts: none -> 2.5 us  [the longest x2 1.29 us: body(): own_lists[head_lo:head_hi].reshape(-1)]
  transfers between devices with their start and end apart: 2 -> 4, of which waited for: 1 -> 3; matrix products, arithmetic and copies ran while one was open for 4% -> 6% of each run, Pallas kernels for 0% -> 11%
where the time goes in v7:
time: 163 us
  blocking collectives  90.6 us (56%)
  waiting for transfers between devices  23.3 us (14%)
  local copies, waits for them, and re-layouts  19.9 us (12%)
  Pallas kernels  17.6 us (11%)
  starting transfers between devices  10.8 us (7%)
    all_to_all x1, blocking collectives, body(): lax.all_to_all(jnp.stack([to_groups(key_rows), to_groups(value_rows)], ax...  66.7 us
    all_to_all x1, blocking collectives, body(): lax.all_to_all(mixed_out.reshape(group_count, tok_rows, width), GROUP, 0,...  23.9 us
    all_to_all x2, waiting for transfers between devices, body(): lax.all_to_all(query_groups[:, :, head_lo * HD:head_hi * HD], GROUP, 0, 0...  20.1 us
    pallas_call x2, Pallas kernels, attend(): pl.pallas_call(kernel, grid_spec=grid_spec, out_shape=jax.ShapeDtypeStruc...  17.6 us
    unnamed x18, local copies, waits for them, and re-layouts  7.59 us
    all_to_all x2, starting transfers between devices, body(): lax.all_to_all(query_groups[:, :, head_lo * HD:head_hi * HD], GROUP, 0, 0...  7.22 us
    all_to_all x1, starting transfers between devices, body(): lax.all_to_all(mixed_out.reshape(group_count, tok_rows, width), GROUP, 0,...  3.53 us
  transfers between devices with their start and end apart: 4, of which 3 were waited for; matrix products, arithmetic and copies ran while one was open for 6% of the time, Pallas kernels for 11%

profile of v7, /device:TPU:0, one launch (start us, length us, event | category | flops | bytes accessed | tf_op | source)
XLA Modules:
  0.0 162.9 jit_solution(12674825673423984934)
XLA Ops:
  0.0 1.8 %copy.34 = bf16[128,5120]{0,1:T(8,128)(2,1)S(1)} copy(bf16[128,5120]{1,0:T(8,128)(2,1)} %param.6) | data formatting | bytes 2621440 | tf_op args[1]
  1.8 0.7 copy.35
  2.5 2.4 %copy.36 = bf16[128,5120]{0,1:T(8,128)(2,1)} copy(bf16[128,5120]{1,0:T(8,128)(2,1)} %param.7) | data formatting | bytes 2621440 | tf_op args[2]
  4.9 1.7 %copy.37 = bf16[128,8,640]{2,0,1:T(8,128)(2,1)S(1)} copy(bf16[128,8,640]{0,2,1:T(8,128)(2,1)} %bitcast.44) | data formatting | bytes 2621440 | tf_op jit(solution)/shard_map/reshape;reshape | solution.py:38
  6.6 0.3 pad_maximum_fusion
  6.9 0.0 copy-start.4
  6.9 66.7 %all_to_all.25.mine_ref = bf16[8,2,128,640]{3,2,1,0:T(8,128)(2,1)S(1)} all-to-all(bf16[8,2,128,640]{3,2,1,0:T(8,128)(2,1)S(1)} %pad_maximum_fusion), channel_id=1, replica_groups=mesh['clips'=2,'seq'=4,'px'=2,'pc'=2] {'seq','px'}, dimensions={0} | all-to-all | bytes 5242880 | tf_op jit(solution)/shard_map/all_to_all | solution.py:40
  73.6 0.0 collective-permute-start
  73.6 0.1 copy.44
  73.7 1.4 copy-done
  75.1 1.1 copy-done.1
  76.1 0.8 slice.35
  77.0 3.6 %all-to-all-start.3 = ((bf16[8,128,256]{2,1,0:T(8,128)(2,1)}), bf16[8,128,256]{2,1,0:T(8,128)(2,1)S(1)}, u32[]{:S(2)}, u32[]{:S(2)}) async-start(bf16[8,128,256]{2,1,0:T(8,128)(2,1)} %slice.35), calls=%async_computation.3 | async-start | bytes 1048576 | tf_op jit(solution)/shard_map/all_to_all | solution.py:70
  80.6 0.0 copy-start.5
  80.6 2.2 %slice.33 = bf16[8,128,384]{2,1,0:T(8,128)(2,1)} slice(bf16[8,128,640]{2,1,0:T(8,128)(2,1)} %bitcast.42), slice={[0:8], [0:128], [0:384]} | slice | bytes 1572864 | tf_op jit(solution)/shard_map/slice | solution.py:71
  82.8 12.0 %all-to-all-done.3 = bf16[8,128,256]{2,1,0:T(8,128)(2,1)S(1)} async-done(((bf16[8,128,256]{2,1,0:T(8,128)(2,1)}), bf16[8,128,256]{2,1,0:T(8,128)(2,1)S(1)}, u32[]{:S(2)}, u32[]{:S(2)}) %all-to-all-start.3) | async-done | bytes 524320 | tf_op jit(solution)/shard_map/all_to_all | solution.py:70
  94.8 0.8 copy-done.3
  95.6 3.6 %all-to-all-start = ((bf16[8,128,384]{2,1,0:T(8,128)(2,1)}), bf16[8,128,384]{2,1,0:T(8,128)(2,1)S(1)}, u32[]{:S(2)}, u32[]{:S(2)}) async-start(bf16[8,128,384]{2,1,0:T(8,128)(2,1)} %slice.33), calls=%async_computation | async-start | bytes 1572864 | tf_op jit(solution)/shard_map/all_to_all | solution.py:70
  99.2 0.1 copy.30
  99.3 0.6 gather_fusion.2
  99.9 0.1 copy.31
  100.0 0.6 gather_fusion.3
  100.5 0.1 select_bitcast_fusion
  100.6 0.1 slice.22
  100.7 0.1 copy.39
  100.8 0.6 reshape.78.counts_ref
  101.4 0.0 copy-done.5
  101.4 0.1 copy.27
  101.5 0.6 gather_fusion
  102.0 0.1 copy.28
  102.1 0.6 gather_fusion.1
  102.7 0.1 fusion
  102.8 0.1 slice.34
  102.9 0.1 copy.38
  103.0 0.6 reshape.77.lists_ref
  103.7 0.0 collective-permute-done.other_ref
  103.7 7.5 %shard_map.56 = bf16[1024,256]{1,0:T(8,128)(2,1)} custom-call(s32[32]{0:T(128)} %reshape.77.lists_ref, s32[16]{0:T(128)} %reshape.78.counts_ref, bf16[1024,256]{1,0:T(8,128)(2,1)} %bitcast.47, bf16[8,2,128,640]{3,2,1,0:T(8,128)(2,1)} %copy-done, bf16[8,2,128,640]{3,2,1,0:T(8,128)(2,1)} %collective-permute-done.other_ref), custom_call_target="tpu_custom_call" | custom-call | tf_op jit(solution)/shard_map/pallas_call | solution.py:164
  111.2 8.1 %all-to-all-done = bf16[8,128,384]{2,1,0:T(8,128)(2,1)S(1)} async-done(((bf16[8,128,384]{2,1,0:T(8,128)(2,1)}), bf16[8,128,384]{2,1,0:T(8,128)(2,1)S(1)}, u32[]{:S(2)}, u32[]{:S(2)}) %all-to-all-start) | async-done | bytes 786464 | tf_op jit(solution)/shard_map/all_to_all | solution.py:70
  119.4 3.5 %all-to-all-start.4 = ((bf16[8,128,256]{2,1,0:T(8,128)(2,1)}), bf16[8,128,256]{2,1,0:T(8,128)(2,1)S(1)}, u32[]{:S(2)}, u32[]{:S(2)}) async-start(bf16[8,128,256]{2,1,0:T(8,128)(2,1)} %bitcast.48), calls=%async_computation.4 | async-start | bytes 1048576 | tf_op jit(solution)/shard_map/all_to_all | solution.py:84
  122.9 0.1 copy.32
  123.0 0.6 reshape.74.counts_ref
  123.6 0.1 copy.29
  123.7 0.6 reshape.73.lists_ref
  124.4 10.0 %shard_map.55 = bf16[1024,384]{1,0:T(8,128)(2,1)} custom-call(s32[48]{0:T(128)} %reshape.73.lists_ref, s32[24]{0:T(128)} %reshape.74.counts_ref, bf16[1024,384]{1,0:T(8,128)(2,1)} %bitcast.45, bf16[8,2,128,640]{3,2,1,0:T(8,128)(2,1)} %copy-done, bf16[8,2,128,640]{3,2,1,0:T(8,128)(2,1)} %collective-permute-done.other_ref), custom_call_target="tpu_custom_call" | custom-call | tf_op jit(solution)/shard_map/pallas_call | solution.py:164
  134.4 3.2 %all-to-all-done.4 = bf16[8,128,256]{2,1,0:T(8,128)(2,1)S(1)} async-done(((bf16[8,128,256]{2,1,0:T(8,128)(2,1)}), bf16[8,128,256]{2,1,0:T(8,128)(2,1)S(1)}, u32[]{:S(2)}, u32[]{:S(2)}) %all-to-all-start.4) | async-done | bytes 524320 | tf_op jit(solution)/shard_map/all_to_all | solution.py:84
  137.6 23.9 %all_to_all.26 = bf16[8,128,384]{2,1,0:T(8,128)(2,1)S(1)} all-to-all(bf16[8,128,384]{2,1,0:T(8,128)(2,1)} %bitcast.46), channel_id=1, replica_groups=mesh['clips'=2,'seq'=4,'px'=2,'pc'=2] {'seq','px'}, dimensions={0} | all-to-all | bytes 1572864 | tf_op jit(solution)/shard_map/all_to_all | solution.py:84
  161.5 0.1 maximum_bitcast_fusion
  161.6 1.2 copy.42
  (14 shorter events, 0.1 us)
Async XLA Ops:
  6.9 66.7 %copy-start.4 = (bf16[128,5120]{1,0:T(8,128)(2,1)S(1)}, bf16[128,5120]{1,0:T(8,128)(2,1)}, u32[]{:S(2)}) copy-start(bf16[128,5120]{1,0:T(8,128)(2,1)} %param.5) | copy-start | bytes 3932164
  73.6 1.5 copy-start
  73.6 30.1 %collective-permute-start = (bf16[8,2,128,640]{3,2,1,0:T(8,128)(2,1)S(1)}, bf16[8,2,128,640]{3,2,1,0:T(8,128)(2,1)}, u32[]{:S(2)}, u32[]{:S(2)}) collective-permute-start(bf16[8,2,128,640]{3,2,1,0:T(8,128)(2,1)S(1)} %all_to_all.25.mine_ref), channel_id=1, source_target_pairs={{0,1},{1,0},{2,3},{3,2},{4,5},{5,4},{6,7},{7,6},{8,9},{9,8},{10,11... | collective-permute-start | bytes 7864328 | tf_op jit(solution)/shard_map/ppermute | solution.py:45
  75.1 1.1 copy-start.1
  77.0 17.8 %all-to-all-start.3 = ((bf16[8,128,256]{2,1,0:T(8,128)(2,1)}), bf16[8,128,256]{2,1,0:T(8,128)(2,1)S(1)}, u32[]{:S(2)}, u32[]{:S(2)}) async-start(bf16[8,128,256]{2,1,0:T(8,128)(2,1)} %slice.35), calls=%async_computation.3 | async-start | bytes 1048576 | tf_op jit(solution)/shard_map/all_to_all | solution.py:70
  80.6 18.6 %copy-start.6 = (s32[40,16]{0,1:T(8,128)S(1)}, s32[40,16]{0,1:T(8,128)}, u32[]{:S(2)}) copy-start(s32[40,16]{0,1:T(8,128)} %param.9) | copy-start | bytes 7684
  80.6 20.8 %copy-start.5 = (s32[40,16,2]{0,2,1:T(2,128)S(1)}, s32[40,16,2]{0,2,1:T(2,128)}, u32[]{:S(2)}) copy-start(s32[40,16,2]{0,2,1:T(2,128)} %param.8) | copy-start | bytes 15364
  94.8 0.8 copy-start.3
  95.6 23.8 %all-to-all-start = ((bf16[8,128,384]{2,1,0:T(8,128)(2,1)}), bf16[8,128,384]{2,1,0:T(8,128)(2,1)S(1)}, u32[]{:S(2)}, u32[]{:S(2)}) async-start(bf16[8,128,384]{2,1,0:T(8,128)(2,1)} %slice.33), calls=%async_computation | async-start | bytes 1572864 | tf_op jit(solution)/shard_map/all_to_all | solution.py:70
  119.3 5.0 %copy-start.2 = (bf16[8,128,384]{2,1,0:T(8,128)(2,1)}, bf16[8,128,384]{2,1,0:T(8,128)(2,1)S(1)}, u32[]{:S(2)}) copy-start(bf16[8,128,384]{2,1,0:T(8,128)(2,1)S(1)} %all-to-all-done) | copy-start | bytes 2359300
  119.4 18.2 %all-to-all-start.4 = ((bf16[8,128,256]{2,1,0:T(8,128)(2,1)}), bf16[8,128,256]{2,1,0:T(8,128)(2,1)S(1)}, u32[]{:S(2)}, u32[]{:S(2)}) async-start(bf16[8,128,256]{2,1,0:T(8,128)(2,1)} %bitcast.48), calls=%async_computation.4 | async-start | bytes 1048576 | tf_op jit(solution)/shard_map/all_to_all | solution.py:84

commit v8 on v6

--- a/solution.py
+++ b/solution.py
@@ -95,51 +95,50 @@
             visits = counts_ref[slot]
             row = pl.multiple_of(i * BLOCK, BLOCK)
             q = q_ref[pl.ds(row, BLOCK), :]
-            key_starts = []
-            scores = []
+            key_blocks = []
+            value_blocks = []
             for j in range(max_visits):
                 picked = jnp.clip(lists_ref[slot * max_visits + j], 0, 2 * own_count - 1)
                 other = picked >= own_count
                 held = picked - jnp.where(other, own_count, 0)
                 source = held // local_blocks
                 krow = pl.multiple_of(held % local_blocks * BLOCK, BLOCK)
-                key_block = jnp.where(
-                    other,
-                    other_ref[source, 0, pl.ds(krow, BLOCK), :],
-                    mine_ref[source, 0, pl.ds(krow, BLOCK), :],
+                key_blocks.append(
+                    jnp.where(
+                        other,
+                        other_ref[source, 0, pl.ds(krow, BLOCK), :],
+                        mine_ref[source, 0, pl.ds(krow, BLOCK), :],
+                    )
                 )
-                s = lax.dot_general(
-                    q,
-                    key_block,
-                    (((1,), (1,)), ((), ())),
-                    preferred_element_type=jnp.float32,
-                )
-                key_starts.append((source, krow, other))
-                scores.append(jnp.where(j < visits, s * score_scale, -jnp.inf))
-            peak = scores[0]
-            for s in scores[1:]:
-                peak = jnp.maximum(peak, s)
-            row_max = jnp.max(peak, axis=1, keepdims=True)
-            row_max = jnp.where(row_max > -jnp.inf, row_max, 0.0)
-            total = jnp.zeros((BLOCK, 1), jnp.float32)
-            acc = jnp.zeros((BLOCK, HD), jnp.float32)
-            for s, (source, krow, other) in zip(scores, key_starts):
-                raised = jnp.exp(s - row_max)
-                total = total + jnp.sum(raised, axis=1, keepdims=True)
-                acc = acc + jnp.dot(
-                    raised.astype(jnp.bfloat16),
+                value_blocks.append(
                     jnp.where(
                         other,
                         other_ref[source, 1, pl.ds(krow, BLOCK), :],
                         mine_ref[source, 1, pl.ds(krow, BLOCK), :],
-                    ),
-                    preferred_element_type=jnp.float32,
+                    )
                 )
+            s = lax.dot_general(
+                q,
+                jnp.concatenate(key_blocks, axis=0),
+                (((1,), (1,)), ((), ())),
+                preferred_element_type=jnp.float32,
+            )
+            live = lax.broadcasted_iota(jnp.int32, s.shape, 1) < visits * BLOCK
+            s = jnp.where(live, s * score_scale, -jnp.inf)
+            row_max = jnp.max(s, axis=1, keepdims=True)
+            row_max = jnp.where(row_max > -jnp.inf, row_max, 0.0)
+            raised = jnp.exp(s - row_max)
+            total = jnp.sum(raised, axis=1, keepdims=True)
+            acc = jnp.dot(
+                raised.astype(jnp.bfloat16),
+                jnp.concatenate(value_blocks, axis=0),
+                preferred_element_type=jnp.float32,
+            )
             total = jnp.where(total > 0.0, total, 1.0)
             o_ref[pl.ds(row, BLOCK), :] = (acc / total).astype(o_ref.dtype)
             return carry
 
-        lax.fori_loop(0, own_count, per_block, 0, unroll=min(own_count, 4))
+        lax.fori_loop(0, own_count, per_block, 0, unroll=min(own_count, 8))
 
     grid_spec = pltpu.PrefetchScalarGridSpec(
         num_scalar_prefetch=2,

time: 163 us -> 157 us (0.963)
  Pallas kernels: 14.8 us -> 8.17 us
    pallas_call x1, Pallas kernels: 14.8 us -> 8.17 us  [attend(): pl.pallas_call(kernel, grid_spec=grid_spec, out_shape=jax.ShapeDtypeStruc...]
where the time goes in v8:
time: 157 us; the launch traced here: 156 us
  blocking collectives  102 us (65%)
  waiting for transfers between devices  27.1 us (17%)
  local copies, waits for them, and re-layouts  13.5 us (9%)
  Pallas kernels  8.17 us (5%)
  starting transfers between devices  4.42 us (3%)
    all_to_all x1, blocking collectives, body(): lax.all_to_all(jnp.stack([to_groups(key_rows), to_groups(value_rows)], ax...  66.7 us
    all_to_all x1, blocking collectives, body(): returned = lax.all_to_all(send_back, GROUP, 0, 0, tiled=True)  35.1 us
    all_to_all x1, waiting for transfers between devices, exchange(): return lax.all_to_all(to_groups(rows_in), GROUP, 0, 0, tiled=True)  27.1 us
    pallas_call x1, Pallas kernels, attend(): pl.pallas_call(kernel, grid_spec=grid_spec, out_shape=jax.ShapeDtypeStruc...  8.17 us
    unnamed x12, local copies, waits for them, and re-layouts  5.05 us
    all_to_all x1, starting transfers between devices, exchange(): return lax.all_to_all(to_groups(rows_in), GROUP, 0, 0, tiled=True)  4.42 us
    another operation x3, local copies, waits for them, and re-layouts, to_groups(): widened.reshape(tok_rows, group_count, heads_per * HD).transpose(1, 0, 2)  3.73 us
  transfers between devices with their start and end apart: 2, of which 1 were waited for; matrix products, arithmetic and copies ran while one was open for 4% of the time, Pallas kernels for 0%

profile of v8, /device:TPU:0, one launch (start us, length us, event | category | flops | bytes accessed | tf_op | source)
XLA Modules:
  0.0 156.1 jit_solution(6349039968111204097)
XLA Ops:
  0.0 1.8 %copy.30 = bf16[128,5120]{0,1:T(8,128)(2,1)S(1)} copy(bf16[128,5120]{1,0:T(8,128)(2,1)} %param.6) | data formatting | bytes 2621440 | tf_op args[1]
  1.8 0.7 copy.31
  2.5 2.4 %copy.32 = bf16[128,5120]{0,1:T(8,128)(2,1)} copy(bf16[128,5120]{1,0:T(8,128)(2,1)} %param.7) | data formatting | bytes 2621440 | tf_op args[2]
  4.9 1.7 %copy.33 = bf16[128,8,640]{2,0,1:T(8,128)(2,1)S(1)} copy(bf16[128,8,640]{0,2,1:T(8,128)(2,1)} %bitcast.33) | data formatting | bytes 2621440 | tf_op jit(solution)/shard_map/reshape;reshape | solution.py:38
  6.6 0.3 pad_maximum_fusion
  6.9 0.0 copy-start.1
  6.9 66.7 %all_to_all.15.mine_ref = bf16[8,2,128,640]{3,2,1,0:T(8,128)(2,1)S(1)} all-to-all(bf16[8,2,128,640]{3,2,1,0:T(8,128)(2,1)S(1)} %pad_maximum_fusion), channel_id=1, replica_groups=mesh['clips'=2,'seq'=4,'px'=2,'pc'=2] {'seq','px'}, dimensions={0} | all-to-all | bytes 5242880 | tf_op jit(solution)/shard_map/all_to_all | solution.py:43
  73.6 0.0 copy-start
  73.6 0.0 collective-permute-start
  73.6 0.0 copy-done.1
  73.6 1.3 copy.38
  74.9 0.7 copy-done
  75.6 0.0 copy-start.3
  75.6 0.0 copy-start.2
  75.6 4.4 %all-to-all-start = ((bf16[8,128,640]{2,1,0:T(8,128)(2,1)}), bf16[8,128,640]{2,1,0:T(8,128)(2,1)}, u32[]{:S(2)}, u32[]{:S(2)}) async-start(bf16[8,128,640]{2,1,0:T(8,128)(2,1)} %bitcast.30), calls=%async_computation | async-start | bytes 2621440 | tf_op jit(solution)/shard_map/all_to_all | solution.py:41
  80.0 0.0 copy-done.3
  80.0 0.1 copy.26
  80.1 0.6 gather_fusion.2
  80.7 0.1 copy.27
  80.8 0.6 gather_fusion.3
  81.4 0.1 select_bitcast_fusion.1
  81.4 0.1 copy.28
  81.5 0.7 select_n.104.counts_ref
  82.2 0.0 copy-done.2
  82.2 0.1 copy.23
  82.3 0.6 gather_fusion
  82.9 0.1 copy.24
  83.0 0.6 gather_fusion.1
  83.5 0.1 select_bitcast_fusion
  83.6 0.1 copy.25
  83.8 0.1 select_n.97
  83.9 0.6 fusion.lists_ref
  84.5 27.1 %all-to-all-done = bf16[8,128,640]{2,1,0:T(8,128)(2,1)} async-done(((bf16[8,128,640]{2,1,0:T(8,128)(2,1)}), bf16[8,128,640]{2,1,0:T(8,128)(2,1)}, u32[]{:S(2)}, u32[]{:S(2)}) %all-to-all-start) | async-done | bytes 1310752 | tf_op jit(solution)/shard_map/all_to_all | solution.py:41
  111.5 0.0 collective-permute-done.other_ref
  111.5 8.2 %shard_map.55 = bf16[1024,640]{1,0:T(8,128)(2,1)} custom-call(s32[80]{0:T(128)} %fusion.lists_ref, s32[40]{0:T(128)} %select_n.104.counts_ref, bf16[1024,640]{1,0:T(8,128)(2,1)} %bitcast.5.q_ref, bf16[8,2,128,640]{3,2,1,0:T(8,128)(2,1)} %copy-done, bf16[8,2,128,640]{3,2,1,0:T(8,128)(2,1)} %collective-permute-done.other_ref), custom_call_target="tpu_custom_call" | custom-call | tf_op jit(solution)/shard_map/pallas_call | solution.py:153
  119.7 35.1 %all_to_all.16 = bf16[8,128,640]{2,1,0:T(8,128)(2,1)S(1)} all-to-all(bf16[8,128,640]{2,1,0:T(8,128)(2,1)} %bitcast.34), channel_id=1, replica_groups=mesh['clips'=2,'seq'=4,'px'=2,'pc'=2] {'seq','px'}, dimensions={0} | all-to-all | bytes 2621440 | tf_op jit(solution)/shard_map/all_to_all | solution.py:78
  154.8 1.2 copy.36
  (6 shorter events, 0.1 us)
Async XLA Ops:
  6.9 66.7 %copy-start.1 = (bf16[128,5120]{1,0:T(8,128)(2,1)S(1)}, bf16[128,5120]{1,0:T(8,128)(2,1)}, u32[]{:S(2)}) copy-start(bf16[128,5120]{1,0:T(8,128)(2,1)} %param.5) | copy-start | bytes 3932164
  73.6 2.0 %copy-start = (bf16[8,2,128,640]{3,2,1,0:T(8,128)(2,1)}, bf16[8,2,128,640]{3,2,1,0:T(8,128)(2,1)S(1)}, u32[]{:S(2)}) copy-start(bf16[8,2,128,640]{3,2,1,0:T(8,128)(2,1)S(1)} %all_to_all.15.mine_ref) | copy-start | bytes 7864324
  73.6 38.0 %collective-permute-start = (bf16[8,2,128,640]{3,2,1,0:T(8,128)(2,1)S(1)}, bf16[8,2,128,640]{3,2,1,0:T(8,128)(2,1)}, u32[]{:S(2)}, u32[]{:S(2)}) collective-permute-start(bf16[8,2,128,640]{3,2,1,0:T(8,128)(2,1)S(1)} %all_to_all.15.mine_ref), channel_id=1, source_target_pairs={{0,1},{1,0},{2,3},{3,2},{4,5},{5,4},{6,7},{7,6},{8,9},{9,8},{10,11... | collective-permute-start | bytes 7864328 | tf_op jit(solution)/shard_map/ppermute | solution.py:48
  75.6 4.4 %copy-start.3 = (s32[40,16]{0,1:T(8,128)S(1)}, s32[40,16]{0,1:T(8,128)}, u32[]{:S(2)}) copy-start(s32[40,16]{0,1:T(8,128)} %param.9) | copy-start | bytes 7684
  75.6 6.6 %copy-start.2 = (s32[40,16,2]{0,2,1:T(2,128)S(1)}, s32[40,16,2]{0,2,1:T(2,128)}, u32[]{:S(2)}) copy-start(s32[40,16,2]{0,2,1:T(2,128)} %param.8) | copy-start | bytes 15364
  75.6 35.9 %all-to-all-start = ((bf16[8,128,640]{2,1,0:T(8,128)(2,1)}), bf16[8,128,640]{2,1,0:T(8,128)(2,1)}, u32[]{:S(2)}, u32[]{:S(2)}) async-start(bf16[8,128,640]{2,1,0:T(8,128)(2,1)} %bitcast.30), calls=%async_computation | async-start | bytes 2621440 | tf_op jit(solution)/shard_map/all_to_all | solution.py:41

commit v9 on v8

--- a/solution.py
+++ b/solution.py
@@ -31,24 +31,35 @@
     padded_heads = heads_per * group_count
     score_scale = 1.0 / math.sqrt(HD)
 
+    def group_slices(rows_in):
+        widened = rows_in
+        if padded_heads > HEADS:
+            widened = jnp.pad(widened, ((0, 0), (0, (padded_heads - HEADS) * HD)))
+        width = heads_per * HD
+        return [widened[:, g * width : (g + 1) * width] for g in range(group_count)]
+
     def to_groups(rows_in):
-        widened = rows_in.reshape(tok_rows, HEADS, HD)
-        if padded_heads > HEADS:
-            widened = jnp.pad(widened, ((0, 0), (0, padded_heads - HEADS), (0, 0)))
-        return widened.reshape(tok_rows, group_count, heads_per * HD).transpose(1, 0, 2)
-
-    def exchange(rows_in):
-        return lax.all_to_all(to_groups(rows_in), GROUP, 0, 0, tiled=True)
+        return jnp.stack(group_slices(rows_in), axis=0)
 
     pair_mine = lax.all_to_all(
-        jnp.stack([to_groups(key_rows), to_groups(value_rows)], axis=1), GROUP, 0, 0, tiled=True
+        jnp.stack(
+            [
+                jnp.stack([key_g, value_g], axis=0)
+                for key_g, value_g in zip(group_slices(key_rows), group_slices(value_rows))
+            ],
+            axis=0,
+        ),
+        GROUP,
+        0,
+        0,
+        tiled=True,
     )
     if pc_count > 1:
         swap = [(c, (c + 1) % pc_count) for c in range(pc_count)]
         pair_other = lax.ppermute(pair_mine, "pc", swap)
     else:
         pair_other = pair_mine
-    query_own = exchange(queries)
+    query_own = lax.all_to_all(to_groups(queries), GROUP, 0, 0, tiled=True)
 
     own_count = group_count * local_blocks
     local_index = jnp.arange(own_count, dtype=jnp.int32)

time: 157 us -> 160 us (1.019)
  blocking collectives: 102 us -> 35.2 us
  waiting for transfers between devices: 27.1 us -> 77.6 us
  starting transfers between devices: 4.42 us -> 11.7 us
  local copies, waits for them, and re-layouts: 13.5 us -> 19.9 us
  other arithmetic: 1.07 us -> 6.8 us
    all_to_all x1 -> x0, blocking collectives: 66.7 us -> none  [body(): lax.all_to_all(jnp.stack([to_groups(key_rows), to_groups(value_rows)], ax...]
    all_to_all x1 -> x2, waiting for transfers between devices: 27.1 us -> 77.6 us  [the longest x1 49.9 us: body(): lax.all_to_all(jnp.stack([jnp.stack([key_g, value_g], axis=0) for key_g,...]
    all_to_all x1 -> x2, starting transfers between devices: 4.42 us -> 11.6 us  [the longest x1 7.25 us: body(): lax.all_to_all(jnp.stack([jnp.stack([key_g, value_g], axis=0) for key_g,...]
    unnamed x12 -> x15, local copies, waits for them, and re-layouts: 5.05 us -> 11.5 us
    unnamed x0 -> x7, other arithmetic: none -> 5.29 us
    another operation x3 -> x2, local copies, waits for them, and re-layouts: 3.73 us -> 3.74 us  [the longest x1 2.15 us: body(): jnp.stack([key_g, value_g], axis=0)]
  transfers between devices with their start and end apart: 2 -> 3, of which waited for: 1 -> 2; matrix products, arithmetic and copies ran while one was open for 4% -> 11% of each run, Pallas kernels for 0% -> 0%
where the time goes in v9:
time: 160 us; the launch traced here: 159 us
  waiting for transfers between devices  77.6 us (48%)
  blocking collectives  35.2 us (22%)
  local copies, waits for them, and re-layouts  19.9 us (12%)
  starting transfers between devices  11.7 us (7%)
  Pallas kernels  8.17 us (5%)
  other arithmetic  6.8 us (4%)
    all_to_all x1, waiting for transfers between devices, body(): lax.all_to_all(jnp.stack([jnp.stack([key_g, value_g], axis=0) for key_g,...  49.9 us
    all_to_all x1, blocking collectives, body(): returned = lax.all_to_all(send_back, GROUP, 0, 0, tiled=True)  35.2 us
    all_to_all x1, waiting for transfers between devices, body(): query_own = lax.all_to_all(to_groups(queries), GROUP, 0, 0, tiled=True)  27.7 us
    unnamed x15, local copies, waits for them, and re-layouts  11.5 us
    pallas_call x1, Pallas kernels, attend(): pl.pallas_call(kernel, grid_spec=grid_spec, out_shape=jax.ShapeDtypeStruc...  8.17 us
    all_to_all x1, starting transfers between devices, body(): lax.all_to_all(jnp.stack([jnp.stack([key_g, value_g], axis=0) for key_g,...  7.25 us
    unnamed x7, other arithmetic  5.29 us
    all_to_all x1, starting transfers between devices, body(): query_own = lax.all_to_all(to_groups(queries), GROUP, 0, 0, tiled=True)  4.4 us
  transfers between devices with their start and end apart: 3, of which 2 were waited for; matrix products, arithmetic and copies ran while one was open for 11% of the time, Pallas kernels for 0%

profile of v9, /device:TPU:0, one launch (start us, length us, event | category | flops | bytes accessed | tf_op | source)
XLA Modules:
  0.0 159.4 jit_solution(10949333229950613561)
XLA Ops:
  0.0 2.1 %slice_bitcast_fusion = (bf16[1,128,640]{2,1,0:T(8,128)(2,1)S(1)}, bf16[1,128,640]{2,1,0:T(8,128)(2,1)S(1)}, bf16[1,128,640]{2,1,0:T(8,128)(2,1)S(1)}, bf16[1,12...) fusion(bf16[128,5120]{1,0:T(8,128)(2,1)} %param.7, ...), kind=kLoop, calls=%fused_computation.28 | loop fusion | bytes 5242880 | tf_op jit(solution)/shard_map/stack | solution.py:47
  2.2 0.7 fusion
  2.9 0.7 fusion.1
  3.6 0.8 fusion.2
  4.4 0.8 fusion.3
  5.2 0.8 fusion.4
  5.9 0.8 fusion.5
  6.7 0.8 fusion.6
  7.4 0.7 fusion.7
  8.2 7.3 %all-to-all-start.1 = ((bf16[8,2,128,640]{3,2,1,0:T(8,128)(2,1)}), bf16[8,2,128,640]{3,2,1,0:T(8,128)(2,1)S(1)}, u32[]{:S(2)}, u32[]{:S(2)}) async-start(bf16[8,2,128,640]{3,2,1,0:T(8,128)(2,1)} %fusion.7), calls=%async_computation.1 | async-start | bytes 5242880 | tf_op jit(solution)/shard_map/all_to_all | solution.py:44
  15.4 1.6 %bitcast_dynamic-update-slice_fusion.7 = bf16[8,128,640]{2,1,0:T(8,128)(2,1)} fusion(bf16[128,5120]{1,0:T(8,128)(2,1)} %param.5), kind=kLoop, calls=%fused_computation.27 | loop fusion | bytes 327680
  17.0 1.6 %bitcast_dynamic-update-slice_fusion.6 = bf16[8,128,640]{2,1,0:T(8,128)(2,1)} fusion(bf16[8,128,640]{2,1,0:T(8,128)(2,1)} %bitcast_dynamic-update-slice_fusion.7, bf16[128,5120]{1,0:T(8,128)(2,1)} %param.5), kind=kLoop, calls=%fused_computation.26 | loop fusion | bytes 327680
  18.6 1.6 %bitcast_dynamic-update-slice_fusion.5 = bf16[8,128,640]{2,1,0:T(8,128)(2,1)} fusion(bf16[8,128,640]{2,1,0:T(8,128)(2,1)} %bitcast_dynamic-update-slice_fusion.6, bf16[128,5120]{1,0:T(8,128)(2,1)} %param.5), kind=kLoop, calls=%fused_computation.25 | loop fusion | bytes 327680
  20.2 1.6 %bitcast_dynamic-update-slice_fusion.4 = bf16[8,128,640]{2,1,0:T(8,128)(2,1)} fusion(bf16[8,128,640]{2,1,0:T(8,128)(2,1)} %bitcast_dynamic-update-slice_fusion.5, bf16[128,5120]{1,0:T(8,128)(2,1)} %param.5), kind=kLoop, calls=%fused_computation.24 | loop fusion | bytes 327680
  21.8 1.6 %bitcast_dynamic-update-slice_fusion.3 = bf16[8,128,640]{2,1,0:T(8,128)(2,1)} fusion(bf16[8,128,640]{2,1,0:T(8,128)(2,1)} %bitcast_dynamic-update-slice_fusion.4, bf16[128,5120]{1,0:T(8,128)(2,1)} %param.5), kind=kLoop, calls=%fused_computation.23 | loop fusion | bytes 327680
  23.4 1.6 %bitcast_dynamic-update-slice_fusion.2 = bf16[8,128,640]{2,1,0:T(8,128)(2,1)} fusion(bf16[8,128,640]{2,1,0:T(8,128)(2,1)} %bitcast_dynamic-update-slice_fusion.3, bf16[128,5120]{1,0:T(8,128)(2,1)} %param.5), kind=kLoop, calls=%fused_computation.22 | loop fusion | bytes 327680
  25.0 49.9 %all-to-all-done.1.mine_ref = bf16[8,2,128,640]{3,2,1,0:T(8,128)(2,1)S(1)} async-done(((bf16[8,2,128,640]{3,2,1,0:T(8,128)(2,1)}), bf16[8,2,128,640]{3,2,1,0:T(8,128)(2,1)S(1)}, u32[]{:S(2)}, u32[]{:S(2)}) %all-to-all-start.1) | async-done | bytes 2621472 | tf_op jit(solution)/shard_map/all_to_all | solution.py:44
  74.9 0.0 copy-start
  74.9 0.0 collective-permute-start
  74.9 1.8 %bitcast_dynamic-update-slice_fusion.1 = bf16[8,128,640]{2,1,0:T(8,128)(2,1)} fusion(bf16[8,128,640]{2,1,0:T(8,128)(2,1)} %bitcast_dynamic-update-slice_fusion.2, bf16[128,5120]{1,0:T(8,128)(2,1)} %param.5), kind=kLoop, calls=%fused_computation.21 | loop fusion | bytes 327680
  76.7 1.6 %bitcast_dynamic-update-slice_fusion = bf16[8,128,640]{2,1,0:T(8,128)(2,1)} fusion(bf16[8,128,640]{2,1,0:T(8,128)(2,1)} %bitcast_dynamic-update-slice_fusion.1, bf16[128,5120]{1,0:T(8,128)(2,1)} %param.5), kind=kLoop, calls=%fused_computation.20 | loop fusion | bytes 327680 | tf_op jit(solution)/shard_map/stack | solution.py:42
  78.3 0.0 copy-start.2
  78.3 0.0 copy-start.1
  78.3 0.0 copy-done
  78.3 4.4 %all-to-all-start = ((bf16[8,128,640]{2,1,0:T(8,128)(2,1)}), bf16[8,128,640]{2,1,0:T(8,128)(2,1)}, u32[]{:S(2)}, u32[]{:S(2)}) async-start(bf16[8,128,640]{2,1,0:T(8,128)(2,1)} %bitcast_dynamic-update-slice_fusion), calls=%async_computation | async-start | bytes 2621440 | tf_op jit(solution)/shard_map/all_to_all | solution.py:62
  82.7 0.0 copy-done.2
  82.7 0.1 copy.20
  82.8 0.6 gather_fusion.2
  83.4 0.1 copy.21
  83.5 0.6 gather_fusion.3
  84.1 0.1 select_bitcast_fusion.1
  84.1 0.1 copy.22
  84.2 0.7 select_n.104.counts_ref
  84.9 0.0 copy-done.1
  84.9 0.1 copy.17
  85.0 0.6 gather_fusion
  85.5 0.1 copy.18
  85.6 0.6 gather_fusion.1
  86.2 0.1 select_bitcast_fusion
  86.3 0.1 copy.19
  86.4 0.1 select_n.97
  86.6 0.6 fusion.8.lists_ref
  87.1 27.7 %all-to-all-done = bf16[8,128,640]{2,1,0:T(8,128)(2,1)} async-done(((bf16[8,128,640]{2,1,0:T(8,128)(2,1)}), bf16[8,128,640]{2,1,0:T(8,128)(2,1)}, u32[]{:S(2)}, u32[]{:S(2)}) %all-to-all-start) | async-done | bytes 1310752 | tf_op jit(solution)/shard_map/all_to_all | solution.py:62
  114.9 0.0 collective-permute-done.other_ref
  114.9 8.2 %shard_map.55 = bf16[1024,640]{1,0:T(8,128)(2,1)} custom-call(s32[80]{0:T(128)} %fusion.8.lists_ref, s32[40]{0:T(128)} %select_n.104.counts_ref, bf16[1024,640]{1,0:T(8,128)(2,1)} %bitcast.12.q_ref, bf16[8,2,128,640]{3,2,1,0:T(8,128)(2,1)} %copy-done, bf16[8,2,128,640]{3,2,1,0:T(8,128)(2,1)} %collective-permute-done.other_ref), custom_call_target="tpu_custom_call" | custom-call | tf_op jit(solution)/shard_map/pallas_call | solution.py:164
  123.0 35.2 %all_to_all.15 = bf16[8,128,640]{2,1,0:T(8,128)(2,1)S(1)} all-to-all(bf16[8,128,640]{2,1,0:T(8,128)(2,1)} %bitcast.94), channel_id=1, replica_groups=mesh['clips'=2,'seq'=4,'px'=2,'pc'=2] {'seq','px'}, dimensions={0} | all-to-all | bytes 2621440 | tf_op jit(solution)/shard_map/all_to_all | solution.py:89
  158.2 1.2 copy.24
  (5 shorter events, 0.0 us)
Async XLA Ops:
  8.2 66.7 %all-to-all-start.1 = ((bf16[8,2,128,640]{3,2,1,0:T(8,128)(2,1)}), bf16[8,2,128,640]{3,2,1,0:T(8,128)(2,1)S(1)}, u32[]{:S(2)}, u32[]{:S(2)}) async-start(bf16[8,2,128,640]{3,2,1,0:T(8,128)(2,1)} %fusion.7), calls=%async_computation.1 | async-start | bytes 5242880 | tf_op jit(solution)/shard_map/all_to_all | solution.py:44
  74.9 3.4 %copy-start = (bf16[8,2,128,640]{3,2,1,0:T(8,128)(2,1)}, bf16[8,2,128,640]{3,2,1,0:T(8,128)(2,1)S(1)}, u32[]{:S(2)}) copy-start(bf16[8,2,128,640]{3,2,1,0:T(8,128)(2,1)S(1)} %all-to-all-done.1.mine_ref) | copy-start | bytes 7864324
  74.9 39.9 %collective-permute-start = (bf16[8,2,128,640]{3,2,1,0:T(8,128)(2,1)S(1)}, bf16[8,2,128,640]{3,2,1,0:T(8,128)(2,1)}, u32[]{:S(2)}, u32[]{:S(2)}) collective-permute-start(bf16[8,2,128,640]{3,2,1,0:T(8,128)(2,1)S(1)} %all-to-all-done.1.mine_ref), channel_id=1, source_target_pairs={{0,1},{1,0},{2,3},{3,2},{4,5},{5,4},{6,7},{7,6},{8,9},{9,8},{10,11... | collective-permute-start | bytes 7864328 | tf_op jit(solution)/shard_map/ppermute | solution.py:59
  78.3 4.4 %copy-start.2 = (s32[40,16]{0,1:T(8,128)S(1)}, s32[40,16]{0,1:T(8,128)}, u32[]{:S(2)}) copy-start(s32[40,16]{0,1:T(8,128)} %param.9) | copy-start | bytes 7684
  78.3 6.6 %copy-start.1 = (s32[40,16,2]{0,2,1:T(2,128)S(1)}, s32[40,16,2]{0,2,1:T(2,128)}, u32[]{:S(2)}) copy-start(s32[40,16,2]{0,2,1:T(2,128)} %param.8) | copy-start | bytes 15364
  78.3 36.6 %all-to-all-start = ((bf16[8,128,640]{2,1,0:T(8,128)(2,1)}), bf16[8,128,640]{2,1,0:T(8,128)(2,1)}, u32[]{:S(2)}, u32[]{:S(2)}) async-start(bf16[8,128,640]{2,1,0:T(8,128)(2,1)} %bitcast_dynamic-update-slice_fusion), calls=%async_computation | async-start | bytes 2621440 | tf_op jit(solution)/shard_map/all_to_all | solution.py:62

commit v10 on v8

--- a/solution.py
+++ b/solution.py
@@ -37,18 +37,20 @@
             widened = jnp.pad(widened, ((0, 0), (0, padded_heads - HEADS), (0, 0)))
         return widened.reshape(tok_rows, group_count, heads_per * HD).transpose(1, 0, 2)
 
-    def exchange(rows_in):
-        return lax.all_to_all(to_groups(rows_in), GROUP, 0, 0, tiled=True)
-
-    pair_mine = lax.all_to_all(
-        jnp.stack([to_groups(key_rows), to_groups(value_rows)], axis=1), GROUP, 0, 0, tiled=True
-    )
+    if padded_heads == HEADS:
+        pair_groups, query_groups = regroup_in(
+            key_rows, value_rows, queries, group_count, heads_per * HD
+        )
+    else:
+        pair_groups = jnp.stack([to_groups(key_rows), to_groups(value_rows)], axis=1)
+        query_groups = to_groups(queries)
+    pair_mine = lax.all_to_all(pair_groups, GROUP, 0, 0, tiled=True)
     if pc_count > 1:
         swap = [(c, (c + 1) % pc_count) for c in range(pc_count)]
         pair_other = lax.ppermute(pair_mine, "pc", swap)
     else:
         pair_other = pair_mine
-    query_own = exchange(queries)
+    query_own = lax.all_to_all(query_groups, GROUP, 0, 0, tiled=True)
 
     own_count = group_count * local_blocks
     local_index = jnp.arange(own_count, dtype=jnp.int32)
@@ -76,6 +78,8 @@
     )
     send_back = mixed_out.reshape(group_count, tok_rows, heads_per * HD)
     returned = lax.all_to_all(send_back, GROUP, 0, 0, tiled=True)
+    if padded_heads == HEADS:
+        return regroup_out(returned)
     full = returned.transpose(1, 0, 2).reshape(tok_rows, padded_heads * HD)
     return full[:, : HEADS * HD]
 
@@ -157,6 +161,58 @@
     )(lists, counts, query_rows, pair_mine, pair_other)
 
 
+def regroup_in(key_rows, value_rows, queries, group_count, width):
+    tok_rows = queries.shape[0]
+
+    def kernel(k_hbm, v_hbm, q_hbm, pair_out, query_out, sems):
+        copies = []
+        for g in range(group_count):
+            cols = pl.ds(g * width, width)
+            routes = ((k_hbm, pair_out.at[g, 0]), (v_hbm, pair_out.at[g, 1]), (q_hbm, query_out.at[g]))
+            for n, (src, dst) in enumerate(routes):
+                copy = pltpu.make_async_copy(src.at[:, cols], dst, sems.at[3 * g + n])
+                copy.start()
+                copies.append(copy)
+        for copy in copies:
+            copy.wait()
+
+    anywhere = pl.BlockSpec(memory_space=pl.ANY)
+    return pl.pallas_call(
+        kernel,
+        out_shape=(
+            jax.ShapeDtypeStruct((group_count, 2, tok_rows, width), queries.dtype),
+            jax.ShapeDtypeStruct((group_count, tok_rows, width), queries.dtype),
+        ),
+        in_specs=[anywhere, anywhere, anywhere],
+        out_specs=(anywhere, anywhere),
+        scratch_shapes=[pltpu.SemaphoreType.DMA((3 * group_count,))],
+    )(key_rows, value_rows, queries)
+
+
+def regroup_out(returned):
+    group_count, tok_rows, width = returned.shape
+
+    def kernel(r_hbm, o_hbm, sems):
+        copies = []
+        for g in range(group_count):
+            copy = pltpu.make_async_copy(
+                r_hbm.at[g], o_hbm.at[:, pl.ds(g * width, width)], sems.at[g]
+            )
+            copy.start()
+            copies.append(copy)
+        for copy in copies:
+            copy.wait()
+
+    anywhere = pl.BlockSpec(memory_space=pl.ANY)
+    return pl.pallas_call(
+        kernel,
+        out_shape=jax.ShapeDtypeStruct((tok_rows, group_count * width), returned.dtype),
+        in_specs=[anywhere],
+        out_specs=anywhere,
+        scratch_shapes=[pltpu.SemaphoreType.DMA((group_count,))],
+    )(returned)
+
+
 def solution(mesh):
     sizes = dict(zip(mesh.axis_names, mesh.devices.shape))
     pair_count = sizes["pair"]

time: 157 us -> 309 us (1.97)
  Pallas kernels: 8.17 us -> 169 us
  local copies, waits for them, and re-layouts: 13.5 us -> 5.13 us
    pallas_call x0 -> x2, Pallas kernels: none -> 161 us  [the longest x1 120 us: regroup_in(): pl.pallas_call(kernel, out_shape=(jax.ShapeDtypeStruct((group_count, 2, t...]
    another operation x3 -> x0, local copies, waits for them, and re-layouts: 3.73 us -> none  [to_groups(): widened.reshape(tok_rows, group_count, heads_per * HD).transpose(1, 0, 2)]
    unnamed x12 -> x8, local copies, waits for them, and re-layouts: 5.05 us -> 1.69 us
  transfers between devices with their start and end apart: 2 -> 2, of which waited for: 1 -> 1; matrix products, arithmetic and copies ran while one was open for 4% -> 1% of each run, Pallas kernels for 0% -> 0%
where the time goes in v10:
time: 309 us; the launch traced here: 308 us
  Pallas kernels  169 us (55%)
  blocking collectives  102 us (33%)
  waiting for transfers between devices  26.5 us (9%)
  local copies, waits for them, and re-layouts  5.13 us (2%)
  starting transfers between devices  4.29 us (1%)
    pallas_call x1, Pallas kernels, regroup_in(): pl.pallas_call(kernel, out_shape=(jax.ShapeDtypeStruct((group_count, 2, t...  120 us
    all_to_all x1, blocking collectives, body(): pair_mine = lax.all_to_all(pair_groups, GROUP, 0, 0, tiled=True)  66.7 us
    pallas_call x1, Pallas kernels, regroup_out(): pl.pallas_call(kernel, out_shape=jax.ShapeDtypeStruct((tok_rows, group_co...  40.9 us
    all_to_all x1, blocking collectives, body(): returned = lax.all_to_all(send_back, GROUP, 0, 0, tiled=True)  35.3 us
    all_to_all x1, waiting for transfers between devices, body(): query_own = lax.all_to_all(query_groups, GROUP, 0, 0, tiled=True)  26.5 us
    pallas_call x1, Pallas kernels, attend(): pl.pallas_call(kernel, grid_spec=grid_spec, out_shape=jax.ShapeDtypeStruc...  8.17 us
  transfers between devices with their start and end apart: 2, of which 1 were waited for; matrix products, arithmetic and copies ran while one was open for 1% of the time, Pallas kernels for 0%

profile of v10, /device:TPU:0, one launch (start us, length us, event | category | flops | bytes accessed | tf_op | source)
XLA Modules:
  0.0 308.3 jit_solution(14913143478866762902)
XLA Ops:
  0.0 120.4 %shard_map.55 = (bf16[8,2,128,640]{3,2,1,0:T(8,128)(2,1)}, bf16[8,128,640]{2,1,0:T(8,128)(2,1)}) custom-call(bf16[128,5120]{1,0:T(8,128)(2,1)} %k_hbm.1, bf16[128,5120]{1,0:T(8,128)(2,1)} %v_hbm.1, bf16[128,5120]{1,0:T(8,128)(2,1)} %q_hbm.1), custom_call_target="tpu_custom_call" | custom-call | tf_op jit(solution)/shard_map/pallas_call | solution.py:180
  120.4 66.7 %all_to_all.15.mine_ref = bf16[8,2,128,640]{3,2,1,0:T(8,128)(2,1)S(1)} all-to-all(bf16[8,2,128,640]{3,2,1,0:T(8,128)(2,1)} %get-tuple-element.8), channel_id=1, replica_groups=mesh['clips'=2,'seq'=4,'px'=2,'pc'=2] {'seq','px'}, dimensions={0} | all-to-all | bytes 5242880 | tf_op jit(solution)/shard_map/all_to_all | solution.py:47
  187.2 0.0 copy-start
  187.2 0.0 collective-permute-start
  187.2 0.0 copy-start.2
  187.2 0.0 copy-start.1
  187.2 1.5 copy-done
  188.7 4.3 %all-to-all-start = ((bf16[8,128,640]{2,1,0:T(8,128)(2,1)}), bf16[8,128,640]{2,1,0:T(8,128)(2,1)}, u32[]{:S(2)}, u32[]{:S(2)}) async-start(bf16[8,128,640]{2,1,0:T(8,128)(2,1)} %get-tuple-element.7), calls=%async_computation | async-start | bytes 2621440 | tf_op jit(solution)/shard_map/all_to_all | solution.py:53
  193.0 0.0 copy-done.2
  193.0 0.1 copy.18
  193.1 0.6 gather_fusion.2
  193.7 0.1 copy.19
  193.8 0.6 gather_fusion.3
  194.4 0.1 select_bitcast_fusion.1
  194.4 0.1 copy.20
  194.5 0.7 select_n.104.counts_ref
  195.2 0.0 copy-done.1
  195.2 0.1 copy.15
  195.3 0.6 gather_fusion
  195.8 0.1 copy.16
  195.9 0.6 gather_fusion.1
  196.5 0.1 select_bitcast_fusion
  196.6 0.1 copy.17
  196.7 0.1 select_n.97
  196.9 0.6 fusion.lists_ref
  197.5 26.5 %all-to-all-done = bf16[8,128,640]{2,1,0:T(8,128)(2,1)} async-done(((bf16[8,128,640]{2,1,0:T(8,128)(2,1)}), bf16[8,128,640]{2,1,0:T(8,128)(2,1)}, u32[]{:S(2)}, u32[]{:S(2)}) %all-to-all-start) | async-done | bytes 1310752 | tf_op jit(solution)/shard_map/all_to_all | solution.py:53
  224.0 0.0 collective-permute-done.other_ref
  224.0 8.2 %shard_map.56 = bf16[1024,640]{1,0:T(8,128)(2,1)} custom-call(s32[80]{0:T(128)} %fusion.lists_ref, s32[40]{0:T(128)} %select_n.104.counts_ref, bf16[1024,640]{1,0:T(8,128)(2,1)} %bitcast.4.q_ref, bf16[8,2,128,640]{3,2,1,0:T(8,128)(2,1)} %copy-done, bf16[8,2,128,640]{3,2,1,0:T(8,128)(2,1)} %collective-permute-done.other_ref), custom_call_target="tpu_custom_call" | custom-call | tf_op jit(solution)/shard_map/pallas_call | solution.py:157
  232.1 35.3 %all_to_all.16.r_hbm = bf16[8,128,640]{2,1,0:T(8,128)(2,1)} all-to-all(bf16[8,128,640]{2,1,0:T(8,128)(2,1)} %bitcast.10), channel_id=1, replica_groups=mesh['clips'=2,'seq'=4,'px'=2,'pc'=2] {'seq','px'}, dimensions={0} | all-to-all | bytes 2621440 | tf_op jit(solution)/shard_map/all_to_all | solution.py:80
  267.4 40.9 %shard_map.57 = bf16[128,5120]{1,0:T(8,128)(2,1)} custom-call(bf16[8,128,640]{2,1,0:T(8,128)(2,1)} %all_to_all.16.r_hbm), custom_call_target="tpu_custom_call" | custom-call | tf_op jit(solution)/shard_map/pallas_call | solution.py:207
  (6 shorter events, 0.1 us)
Async XLA Ops:
  187.2 1.5 copy-start
  187.2 36.8 %collective-permute-start = (bf16[8,2,128,640]{3,2,1,0:T(8,128)(2,1)S(1)}, bf16[8,2,128,640]{3,2,1,0:T(8,128)(2,1)}, u32[]{:S(2)}, u32[]{:S(2)}) collective-permute-start(bf16[8,2,128,640]{3,2,1,0:T(8,128)(2,1)S(1)} %all_to_all.15.mine_ref), channel_id=1, source_target_pairs={{0,1},{1,0},{2,3},{3,2},{4,5},{5,4},{6,7},{7,6},{8,9},{9,8},{10,11... | collective-permute-start | bytes 7864328 | tf_op jit(solution)/shard_map/ppermute | solution.py:50
  187.2 5.8 %copy-start.2 = (s32[40,16]{0,1:T(8,128)S(1)}, s32[40,16]{0,1:T(8,128)}, u32[]{:S(2)}) copy-start(s32[40,16]{0,1:T(8,128)} %param.9) | copy-start | bytes 7684
  187.2 8.0 %copy-start.1 = (s32[40,16,2]{0,2,1:T(2,128)S(1)}, s32[40,16,2]{0,2,1:T(2,128)}, u32[]{:S(2)}) copy-start(s32[40,16,2]{0,2,1:T(2,128)} %param.8) | copy-start | bytes 15364
  188.7 35.3 %all-to-all-start = ((bf16[8,128,640]{2,1,0:T(8,128)(2,1)}), bf16[8,128,640]{2,1,0:T(8,128)(2,1)}, u32[]{:S(2)}, u32[]{:S(2)}) async-start(bf16[8,128,640]{2,1,0:T(8,128)(2,1)} %get-tuple-element.7), calls=%async_computation | async-start | bytes 2621440 | tf_op jit(solution)/shard_map/all_to_all | solution.py:53

commit v11 on v8

--- a/solution.py
+++ b/solution.py
@@ -37,18 +37,20 @@
             widened = jnp.pad(widened, ((0, 0), (0, padded_heads - HEADS), (0, 0)))
         return widened.reshape(tok_rows, group_count, heads_per * HD).transpose(1, 0, 2)
 
-    def exchange(rows_in):
-        return lax.all_to_all(to_groups(rows_in), GROUP, 0, 0, tiled=True)
-
-    pair_mine = lax.all_to_all(
-        jnp.stack([to_groups(key_rows), to_groups(value_rows)], axis=1), GROUP, 0, 0, tiled=True
-    )
+    if padded_heads == HEADS:
+        pair_groups, query_groups = regroup_in(
+            key_rows, value_rows, queries, group_count, heads_per * HD
+        )
+    else:
+        pair_groups = jnp.stack([to_groups(key_rows), to_groups(value_rows)], axis=1)
+        query_groups = to_groups(queries)
+    pair_mine = lax.all_to_all(pair_groups, GROUP, 0, 0, tiled=True)
     if pc_count > 1:
         swap = [(c, (c + 1) % pc_count) for c in range(pc_count)]
         pair_other = lax.ppermute(pair_mine, "pc", swap)
     else:
         pair_other = pair_mine
-    query_own = exchange(queries)
+    query_own = lax.all_to_all(query_groups, GROUP, 0, 0, tiled=True)
 
     own_count = group_count * local_blocks
     local_index = jnp.arange(own_count, dtype=jnp.int32)
@@ -157,6 +159,25 @@
     )(lists, counts, query_rows, pair_mine, pair_other)
 
 
+def regroup_in(key_rows, value_rows, queries, group_count, width):
+    tok_rows = queries.shape[0]
+
+    def kernel(k_ref, v_ref, q_ref, pair_ref, query_ref):
+        for g in range(group_count):
+            cols = pl.ds(g * width, width)
+            pair_ref[g, 0] = k_ref[:, cols]
+            pair_ref[g, 1] = v_ref[:, cols]
+            query_ref[g] = q_ref[:, cols]
+
+    return pl.pallas_call(
+        kernel,
+        out_shape=(
+            jax.ShapeDtypeStruct((group_count, 2, tok_rows, width), queries.dtype),
+            jax.ShapeDtypeStruct((group_count, tok_rows, width), queries.dtype),
+        ),
+    )(key_rows, value_rows, queries)
+
+
 def solution(mesh):
     sizes = dict(zip(mesh.axis_names, mesh.devices.shape))
     pair_count = sizes["pair"]

time: 157 us -> 153 us (0.975)
  local copies, waits for them, and re-layouts: 13.5 us -> 6.37 us
  Pallas kernels: 8.17 us -> 12.5 us
    pallas_call x0 -> x1, Pallas kernels: none -> 4.31 us  [regroup_in(): pl.pallas_call(kernel, out_shape=(jax.ShapeDtypeStruct((group_count, 2, t...]
    another operation x3 -> x0, local copies, waits for them, and re-layouts: 3.73 us -> none  [to_groups(): widened.reshape(tok_rows, group_count, heads_per * HD).transpose(1, 0, 2)]
    unnamed x12 -> x8, local copies, waits for them, and re-layouts: 5.05 us -> 1.69 us
  transfers between devices with their start and end apart: 2 -> 2, of which waited for: 1 -> 1; matrix products, arithmetic and copies ran while one was open for 4% -> 3% of each run, Pallas kernels for 0% -> 0%
where the time goes in v11:
time: 153 us; the launch traced here: 152 us
  blocking collectives  102 us (67%)
  waiting for transfers between devices  26.5 us (17%)
  Pallas kernels  12.5 us (8%)
  local copies, waits for them, and re-layouts  6.37 us (4%)
  starting transfers between devices  4.29 us (3%)
    all_to_all x1, blocking collectives, body(): pair_mine = lax.all_to_all(pair_groups, GROUP, 0, 0, tiled=True)  66.7 us
    all_to_all x1, blocking collectives, body(): returned = lax.all_to_all(send_back, GROUP, 0, 0, tiled=True)  35.1 us
    all_to_all x1, waiting for transfers between devices, body(): query_own = lax.all_to_all(query_groups, GROUP, 0, 0, tiled=True)  26.5 us
    pallas_call x1, Pallas kernels, attend(): pl.pallas_call(kernel, grid_spec=grid_spec, out_shape=jax.ShapeDtypeStruc...  8.17 us
    pallas_call x1, Pallas kernels, regroup_in(): pl.pallas_call(kernel, out_shape=(jax.ShapeDtypeStruct((group_count, 2, t...  4.31 us
    all_to_all x1, starting transfers between devices, body(): query_own = lax.all_to_all(query_groups, GROUP, 0, 0, tiled=True)  4.28 us
  transfers between devices with their start and end apart: 2, of which 1 were waited for; matrix products, arithmetic and copies ran while one was open for 3% of the time, Pallas kernels for 0%

profile of v11, /device:TPU:0, one launch (start us, length us, event | category | flops | bytes accessed | tf_op | source)
XLA Modules:
  0.0 152.3 jit_solution(10101095306450739343)
XLA Ops:
  0.0 4.3 %shard_map.55 = (bf16[8,2,128,640]{3,2,1,0:T(8,128)(2,1)}, bf16[8,128,640]{2,1,0:T(8,128)(2,1)}) custom-call(bf16[128,5120]{1,0:T(8,128)(2,1)} %k_ref.1, bf16[128,5120]{1,0:T(8,128)(2,1)} %v_ref.1, bf16[128,5120]{1,0:T(8,128)(2,1)} %q_ref.1), custom_call_target="tpu_custom_call" | custom-call | tf_op jit(solution)/shard_map/pallas_call | solution.py:172
  4.3 66.7 %all_to_all.15.mine_ref = bf16[8,2,128,640]{3,2,1,0:T(8,128)(2,1)S(1)} all-to-all(bf16[8,2,128,640]{3,2,1,0:T(8,128)(2,1)} %get-tuple-element.8), channel_id=1, replica_groups=mesh['clips'=2,'seq'=4,'px'=2,'pc'=2] {'seq','px'}, dimensions={0} | all-to-all | bytes 5242880 | tf_op jit(solution)/shard_map/all_to_all | solution.py:47
  71.0 0.0 copy-start
  71.0 0.0 collective-permute-start
  71.0 0.0 copy-start.2
  71.0 0.0 copy-start.1
  71.1 1.5 copy-done
  72.6 4.3 %all-to-all-start = ((bf16[8,128,640]{2,1,0:T(8,128)(2,1)}), bf16[8,128,640]{2,1,0:T(8,128)(2,1)}, u32[]{:S(2)}, u32[]{:S(2)}) async-start(bf16[8,128,640]{2,1,0:T(8,128)(2,1)} %get-tuple-element.7), calls=%async_computation | async-start | bytes 2621440 | tf_op jit(solution)/shard_map/all_to_all | solution.py:53
  76.9 0.0 copy-done.2
  76.9 0.1 copy.20
  77.0 0.6 gather_fusion.2
  77.5 0.1 copy.21
  77.6 0.6 gather_fusion.3
  78.2 0.1 select_bitcast_fusion.1
  78.3 0.1 copy.22
  78.4 0.7 select_n.104.counts_ref
  79.0 0.0 copy-done.1
  79.0 0.1 copy.17
  79.1 0.6 gather_fusion
  79.7 0.1 copy.18
  79.8 0.6 gather_fusion.1
  80.4 0.1 select_bitcast_fusion
  80.5 0.1 copy.19
  80.6 0.1 select_n.97
  80.7 0.6 fusion.lists_ref
  81.3 26.5 %all-to-all-done = bf16[8,128,640]{2,1,0:T(8,128)(2,1)} async-done(((bf16[8,128,640]{2,1,0:T(8,128)(2,1)}), bf16[8,128,640]{2,1,0:T(8,128)(2,1)}, u32[]{:S(2)}, u32[]{:S(2)}) %all-to-all-start) | async-done | bytes 1310752 | tf_op jit(solution)/shard_map/all_to_all | solution.py:53
  107.8 0.0 collective-permute-done.other_ref
  107.8 8.2 %shard_map.56 = bf16[1024,640]{1,0:T(8,128)(2,1)} custom-call(s32[80]{0:T(128)} %fusion.lists_ref, s32[40]{0:T(128)} %select_n.104.counts_ref, bf16[1024,640]{1,0:T(8,128)(2,1)} %bitcast.4.q_ref, bf16[8,2,128,640]{3,2,1,0:T(8,128)(2,1)} %copy-done, bf16[8,2,128,640]{3,2,1,0:T(8,128)(2,1)} %collective-permute-done.other_ref), custom_call_target="tpu_custom_call" | custom-call | tf_op jit(solution)/shard_map/pallas_call | solution.py:155
  116.0 35.1 %all_to_all.16 = bf16[8,128,640]{2,1,0:T(8,128)(2,1)S(1)} all-to-all(bf16[8,128,640]{2,1,0:T(8,128)(2,1)} %bitcast.14), channel_id=1, replica_groups=mesh['clips'=2,'seq'=4,'px'=2,'pc'=2] {'seq','px'}, dimensions={0} | all-to-all | bytes 2621440 | tf_op jit(solution)/shard_map/all_to_all | solution.py:80
  151.1 1.2 copy.24
  (6 shorter events, 0.1 us)
Async XLA Ops:
  71.0 1.5 %copy-start = (bf16[8,2,128,640]{3,2,1,0:T(8,128)(2,1)}, bf16[8,2,128,640]{3,2,1,0:T(8,128)(2,1)S(1)}, u32[]{:S(2)}) copy-start(bf16[8,2,128,640]{3,2,1,0:T(8,128)(2,1)S(1)} %all_to_all.15.mine_ref) | copy-start | bytes 7864324
  71.0 36.8 %collective-permute-start = (bf16[8,2,128,640]{3,2,1,0:T(8,128)(2,1)S(1)}, bf16[8,2,128,640]{3,2,1,0:T(8,128)(2,1)}, u32[]{:S(2)}, u32[]{:S(2)}) collective-permute-start(bf16[8,2,128,640]{3,2,1,0:T(8,128)(2,1)S(1)} %all_to_all.15.mine_ref), channel_id=1, source_target_pairs={{0,1},{1,0},{2,3},{3,2},{4,5},{5,4},{6,7},{7,6},{8,9},{9,8},{10,11... | collective-permute-start | bytes 7864328 | tf_op jit(solution)/shard_map/ppermute | solution.py:50
  71.0 5.8 %copy-start.2 = (s32[40,16]{0,1:T(8,128)S(1)}, s32[40,16]{0,1:T(8,128)}, u32[]{:S(2)}) copy-start(s32[40,16]{0,1:T(8,128)} %param.9) | copy-start | bytes 7684
  71.0 8.0 %copy-start.1 = (s32[40,16,2]{0,2,1:T(2,128)S(1)}, s32[40,16,2]{0,2,1:T(2,128)}, u32[]{:S(2)}) copy-start(s32[40,16,2]{0,2,1:T(2,128)} %param.8) | copy-start | bytes 15364
  72.6 35.3 %all-to-all-start = ((bf16[8,128,640]{2,1,0:T(8,128)(2,1)}), bf16[8,128,640]{2,1,0:T(8,128)(2,1)}, u32[]{:S(2)}, u32[]{:S(2)}) async-start(bf16[8,128,640]{2,1,0:T(8,128)(2,1)} %get-tuple-element.7), calls=%async_computation | async-start | bytes 2621440 | tf_op jit(solution)/shard_map/all_to_all | solution.py:53

commit v12 on v11

--- a/solution.py
+++ b/solution.py
@@ -53,26 +53,13 @@
     query_own = lax.all_to_all(query_groups, GROUP, 0, 0, tiled=True)
 
     own_count = group_count * local_blocks
-    local_index = jnp.arange(own_count, dtype=jnp.int32)
-    own_blocks = (
-        local_index // local_blocks * pc_count + pc_place
-    ) * local_blocks + local_index % local_blocks
-    head_ids = group_place * heads_per + jnp.arange(heads_per, dtype=jnp.int32)
-    head_live = head_ids < HEADS
-    head_safe = jnp.minimum(head_ids, HEADS - 1)
-    own_lists = jnp.take(block_lists[head_safe], own_blocks, axis=1)
-    source_pc = own_lists // local_blocks % pc_count
-    row_block = own_lists // local_blocks // pc_count * local_blocks + own_lists % local_blocks
-    own_lists = jnp.where(source_pc == pc_place, 0, own_count) + row_block
-    counts = jnp.where(
-        head_live[:, None], jnp.take(block_counts[head_safe], own_blocks, axis=1), 0
-    )
     mixed_out = attend(
-        own_lists.reshape(-1),
-        counts.reshape(-1),
+        block_lists.reshape(-1),
+        block_counts.reshape(-1),
         query_own.reshape(own_count * BLOCK, heads_per * HD),
         pair_mine,
         pair_other,
+        block_total,
         max_visits,
         score_scale,
     )
@@ -82,7 +69,7 @@
     return full[:, : HEADS * HD]
 
 
-def attend(lists, counts, query_rows, pair_mine, pair_other, max_visits, score_scale):
+def attend(lists, counts, query_rows, pair_mine, pair_other, block_total, max_visits, score_scale):
     own_rows = query_rows.shape[0]
     own_count = own_rows // BLOCK
     heads_per = query_rows.shape[1] // HD
@@ -90,20 +77,26 @@
     local_blocks = tok_rows // BLOCK
 
     def kernel(lists_ref, counts_ref, q_ref, mine_ref, other_ref, o_ref):
-        head = pl.program_id(0)
+        px_count = lax.axis_size("px")
+        pc_count = lax.axis_size("pc")
+        group_place = lax.axis_index("seq") * px_count + lax.axis_index("px")
+        pc_place = lax.axis_index("pc")
+        head_id = group_place * heads_per + pl.program_id(0)
+        head_safe = jnp.minimum(head_id, HEADS - 1)
 
         def per_block(i, carry):
-            slot = head * own_count + i
-            visits = counts_ref[slot]
+            query_block = (i // local_blocks * pc_count + pc_place) * local_blocks + i % local_blocks
+            slot = head_safe * block_total + query_block
+            visits = jnp.where(head_id < HEADS, counts_ref[slot], 0)
             row = pl.multiple_of(i * BLOCK, BLOCK)
             q = q_ref[pl.ds(row, BLOCK), :]
             key_blocks = []
             value_blocks = []
             for j in range(max_visits):
-                picked = jnp.clip(lists_ref[slot * max_visits + j], 0, 2 * own_count - 1)
-                other = picked >= own_count
-                held = picked - jnp.where(other, own_count, 0)
-                source = held // local_blocks
+                picked = jnp.clip(lists_ref[slot * max_visits + j], 0, block_total - 1)
+                other = picked // local_blocks % pc_count != pc_place
+                source = picked // local_blocks // pc_count
+                held = source * local_blocks + picked % local_blocks
                 krow = pl.multiple_of(held % local_blocks * BLOCK, BLOCK)
                 key_blocks.append(
                     jnp.where(

time: 153 us -> 153 us (level)
  waiting for transfers between devices: 26.5 us -> 29.2 us
  local copies, waits for them, and re-layouts: 6.37 us -> 4.54 us
    all_to_all x1, waiting for transfers between devices: 26.5 us -> 29.2 us  [body(): query_own = lax.all_to_all(query_groups, GROUP, 0, 0, tiled=True)]
    gather x6 -> x0, local copies, waits for them, and re-layouts: 2.44 us -> none  [the longest x3 1.24 us: body(): own_lists = jnp.take(block_lists[head_safe], own_blocks, axis=1)]
  transfers between devices with their start and end apart: 2 -> 2, of which waited for: 1 -> 1; matrix products, arithmetic and copies ran while one was open for 3% -> 1% of each run, Pallas kernels for 0% -> 0%
where the time goes in v12:
time: 153 us; the launch traced here: 152 us
  blocking collectives  102 us (67%)
  waiting for transfers between devices  29.2 us (19%)
  Pallas kernels  12.6 us (8%)
  local copies, waits for them, and re-layouts  4.54 us (3%)
  starting transfers between devices  4.29 us (3%)
    all_to_all x1, blocking collectives, body(): pair_mine = lax.all_to_all(pair_groups, GROUP, 0, 0, tiled=True)  66.7 us
    all_to_all x1, blocking collectives, body(): returned = lax.all_to_all(send_back, GROUP, 0, 0, tiled=True)  35.1 us
    all_to_all x1, waiting for transfers between devices, body(): query_own = lax.all_to_all(query_groups, GROUP, 0, 0, tiled=True)  29.2 us
    pallas_call x1, Pallas kernels, attend(): pl.pallas_call(kernel, grid_spec=grid_spec, out_shape=jax.ShapeDtypeStruc...  8.29 us
    pallas_call x1, Pallas kernels, regroup_in(): pl.pallas_call(kernel, out_shape=(jax.ShapeDtypeStruct((group_count, 2, t...  4.31 us
    all_to_all x1, starting transfers between devices, body(): query_own = lax.all_to_all(query_groups, GROUP, 0, 0, tiled=True)  4.28 us
  transfers between devices with their start and end apart: 2, of which 1 were waited for; matrix products, arithmetic and copies ran while one was open for 1% of the time, Pallas kernels for 0%

profile of v12, /device:TPU:0, one launch (start us, length us, event | category | flops | bytes accessed | tf_op | source)
XLA Modules:
  0.0 152.4 jit_solution(1771768417474524005)
XLA Ops:
  0.0 4.3 %shard_map.55 = (bf16[8,2,128,640]{3,2,1,0:T(8,128)(2,1)}, bf16[8,128,640]{2,1,0:T(8,128)(2,1)}) custom-call(bf16[128,5120]{1,0:T(8,128)(2,1)} %k_ref.1, bf16[128,5120]{1,0:T(8,128)(2,1)} %v_ref.1, bf16[128,5120]{1,0:T(8,128)(2,1)} %q_ref.1), custom_call_target="tpu_custom_call" | custom-call | tf_op jit(solution)/shard_map/pallas_call | solution.py:165
  4.3 66.7 %all_to_all.15.mine_ref = bf16[8,2,128,640]{3,2,1,0:T(8,128)(2,1)S(1)} all-to-all(bf16[8,2,128,640]{3,2,1,0:T(8,128)(2,1)} %get-tuple-element.8), channel_id=1, replica_groups=mesh['clips'=2,'seq'=4,'px'=2,'pc'=2] {'seq','px'}, dimensions={0} | all-to-all | bytes 5242880 | tf_op jit(solution)/shard_map/all_to_all | solution.py:47
  71.0 0.0 copy-start
  71.0 0.0 collective-permute-start
  71.0 0.0 copy-start.2
  71.0 0.0 copy-start.1
  71.1 1.5 copy-done
  72.6 4.3 %all-to-all-start = ((bf16[8,128,640]{2,1,0:T(8,128)(2,1)}), bf16[8,128,640]{2,1,0:T(8,128)(2,1)}, u32[]{:S(2)}, u32[]{:S(2)}) async-start(bf16[8,128,640]{2,1,0:T(8,128)(2,1)} %get-tuple-element.7), calls=%async_computation | async-start | bytes 2621440 | tf_op jit(solution)/shard_map/all_to_all | solution.py:53
  76.9 0.0 copy-done.2
  76.9 0.1 copy.8
  76.9 0.7 reshape.16.counts_ref
  77.6 0.0 copy-done.1
  77.6 0.2 copy.7
  77.9 0.8 reshape.15.lists_ref
  78.7 29.2 %all-to-all-done = bf16[8,128,640]{2,1,0:T(8,128)(2,1)} async-done(((bf16[8,128,640]{2,1,0:T(8,128)(2,1)}), bf16[8,128,640]{2,1,0:T(8,128)(2,1)}, u32[]{:S(2)}, u32[]{:S(2)}) %all-to-all-start) | async-done | bytes 1310752 | tf_op jit(solution)/shard_map/all_to_all | solution.py:53
  107.8 0.0 collective-permute-done.other_ref
  107.8 8.3 %shard_map.56 = bf16[1024,640]{1,0:T(8,128)(2,1)} custom-call(s32[1280]{0:T(1024)} %reshape.15.lists_ref, s32[640]{0:T(1024)} %reshape.16.counts_ref, bf16[1024,640]{1,0:T(8,128)(2,1)} %bitcast.q_ref, bf16[8,2,128,640]{3,2,1,0:T(8,128)(2,1)} %copy-done, bf16[8,2,128,640]{3,2,1,0:T(8,128)(2,1)} %collective-permute-done.other_ref), custom_call_target="tpu_custom_call" | custom-call | tf_op jit(solution)/shard_map/pallas_call | solution.py:148
  116.1 35.1 %all_to_all.16 = bf16[8,128,640]{2,1,0:T(8,128)(2,1)S(1)} all-to-all(bf16[8,128,640]{2,1,0:T(8,128)(2,1)} %bitcast.6), channel_id=1, replica_groups=mesh['clips'=2,'seq'=4,'px'=2,'pc'=2] {'seq','px'}, dimensions={0} | all-to-all | bytes 2621440 | tf_op jit(solution)/shard_map/all_to_all | solution.py:67
  151.2 1.2 copy.10
Async XLA Ops:
  71.0 1.5 copy-start
  71.0 36.8 %collective-permute-start = (bf16[8,2,128,640]{3,2,1,0:T(8,128)(2,1)S(1)}, bf16[8,2,128,640]{3,2,1,0:T(8,128)(2,1)}, u32[]{:S(2)}, u32[]{:S(2)}) collective-permute-start(bf16[8,2,128,640]{3,2,1,0:T(8,128)(2,1)S(1)} %all_to_all.15.mine_ref), channel_id=1, source_target_pairs={{0,1},{1,0},{2,3},{3,2},{4,5},{5,4},{6,7},{7,6},{8,9},{9,8},{10,11... | collective-permute-start | bytes 7864328 | tf_op jit(solution)/shard_map/ppermute | solution.py:50
  71.0 5.8 %copy-start.2 = (s32[40,16]{0,1:T(8,128)S(1)}, s32[40,16]{0,1:T(8,128)}, u32[]{:S(2)}) copy-start(s32[40,16]{0,1:T(8,128)} %param.9) | copy-start | bytes 7684
  71.0 6.6 %copy-start.1 = (s32[40,16,2]{0,2,1:T(2,128)S(1)}, s32[40,16,2]{0,2,1:T(2,128)}, u32[]{:S(2)}) copy-start(s32[40,16,2]{0,2,1:T(2,128)} %param.8) | copy-start | bytes 15364
  72.6 35.3 %all-to-all-start = ((bf16[8,128,640]{2,1,0:T(8,128)(2,1)}), bf16[8,128,640]{2,1,0:T(8,128)(2,1)}, u32[]{:S(2)}, u32[]{:S(2)}) async-start(bf16[8,128,640]{2,1,0:T(8,128)(2,1)} %get-tuple-element.7), calls=%async_computation | async-start | bytes 2621440 | tf_op jit(solution)/shard_map/all_to_all | solution.py:53

commit v13 on v12

--- a/solution.py
+++ b/solution.py
@@ -37,39 +37,68 @@
             widened = jnp.pad(widened, ((0, 0), (0, padded_heads - HEADS), (0, 0)))
         return widened.reshape(tok_rows, group_count, heads_per * HD).transpose(1, 0, 2)
 
+    split = (heads_per + 1) // 2
+    chunks = [(0, split), (split, heads_per)] if heads_per > 1 else [(0, heads_per)]
     if padded_heads == HEADS:
-        pair_groups, query_groups = regroup_in(
-            key_rows, value_rows, queries, group_count, heads_per * HD
+        grouped = regroup_in(key_rows, value_rows, queries, group_count, heads_per, chunks)
+    else:
+        grouped = []
+        for head_lo, head_hi in chunks:
+            cols = slice(head_lo * HD, head_hi * HD)
+            grouped.append(
+                (
+                    jnp.stack(
+                        [to_groups(key_rows)[:, :, cols], to_groups(value_rows)[:, :, cols]],
+                        axis=1,
+                    ),
+                    to_groups(queries)[:, :, cols],
+                )
+            )
+    own_count = group_count * local_blocks
+    pieces = []
+    for (head_lo, head_hi), (pair_groups, query_groups) in zip(chunks, grouped):
+        width = (head_hi - head_lo) * HD
+        pair_mine = lax.all_to_all(pair_groups, GROUP, 0, 0, tiled=True)
+        if pc_count > 1:
+            swap = [(c, (c + 1) % pc_count) for c in range(pc_count)]
+            pair_other = lax.ppermute(pair_mine, "pc", swap)
+        else:
+            pair_other = pair_mine
+        query_own = lax.all_to_all(query_groups, GROUP, 0, 0, tiled=True)
+        mixed_out = attend(
+            block_lists.reshape(-1),
+            block_counts.reshape(-1),
+            query_own.reshape(own_count * BLOCK, width),
+            pair_mine,
+            pair_other,
+            head_lo,
+            heads_per,
+            block_total,
+            max_visits,
+            score_scale,
         )
-    else:
-        pair_groups = jnp.stack([to_groups(key_rows), to_groups(value_rows)], axis=1)
-        query_groups = to_groups(queries)
-    pair_mine = lax.all_to_all(pair_groups, GROUP, 0, 0, tiled=True)
-    if pc_count > 1:
-        swap = [(c, (c + 1) % pc_count) for c in range(pc_count)]
-        pair_other = lax.ppermute(pair_mine, "pc", swap)
-    else:
-        pair_other = pair_mine
-    query_own = lax.all_to_all(query_groups, GROUP, 0, 0, tiled=True)
-
-    own_count = group_count * local_blocks
-    mixed_out = attend(
-        block_lists.reshape(-1),
-        block_counts.reshape(-1),
-        query_own.reshape(own_count * BLOCK, heads_per * HD),
-        pair_mine,
-        pair_other,
-        block_total,
-        max_visits,
-        score_scale,
-    )
-    send_back = mixed_out.reshape(group_count, tok_rows, heads_per * HD)
-    returned = lax.all_to_all(send_back, GROUP, 0, 0, tiled=True)
+        pieces.append(
+            lax.all_to_all(
+                mixed_out.reshape(group_count, tok_rows, width), GROUP, 0, 0, tiled=True
+            )
+        )
+    returned = jnp.concatenate(pieces, axis=2)
     full = returned.transpose(1, 0, 2).reshape(tok_rows, padded_heads * HD)
     return full[:, : HEADS * HD]
 
 
-def attend(lists, counts, query_rows, pair_mine, pair_other, block_total, max_visits, score_scale):
+def attend(
+    lists,
+    counts,
+    query_rows,
+    pair_mine,
+    pair_other,
+    head_lo,
+    heads_all,
+    block_total,
+    max_visits,
+    score_scale,
+):
     own_rows = query_rows.shape[0]
     own_count = own_rows // BLOCK
     heads_per = query_rows.shape[1] // HD
@@ -81,7 +110,7 @@
         pc_count = lax.axis_size("pc")
         group_place = lax.axis_index("seq") * px_count + lax.axis_index("px")
         pc_place = lax.axis_index("pc")
-        head_id = group_place * heads_per + pl.program_id(0)
+        head_id = group_place * heads_all + head_lo + pl.program_id(0)
         head_safe = jnp.minimum(head_id, HEADS - 1)
 
         def per_block(i, carry):
@@ -152,23 +181,25 @@
     )(lists, counts, query_rows, pair_mine, pair_other)
 
 
-def regroup_in(key_rows, value_rows, queries, group_count, width):
+def regroup_in(key_rows, value_rows, queries, group_count, heads_per, chunks):
     tok_rows = queries.shape[0]
 
-    def kernel(k_ref, v_ref, q_ref, pair_ref, query_ref):
-        for g in range(group_count):
-            cols = pl.ds(g * width, width)
-            pair_ref[g, 0] = k_ref[:, cols]
-            pair_ref[g, 1] = v_ref[:, cols]
-            query_ref[g] = q_ref[:, cols]
-
-    return pl.pallas_call(
-        kernel,
-        out_shape=(
-            jax.ShapeDtypeStruct((group_count, 2, tok_rows, width), queries.dtype),
-            jax.ShapeDtypeStruct((group_count, tok_rows, width), queries.dtype),
-        ),
-    )(key_rows, value_rows, queries)
+    def kernel(k_ref, v_ref, q_ref, *out_refs):
+        for n, (head_lo, head_hi) in enumerate(chunks):
+            pair_ref, query_ref = out_refs[2 * n], out_refs[2 * n + 1]
+            for g in range(group_count):
+                cols = pl.ds((g * heads_per + head_lo) * HD, (head_hi - head_lo) * HD)
+                pair_ref[g, 0] = k_ref[:, cols]
+                pair_ref[g, 1] = v_ref[:, cols]
+                query_ref[g] = q_ref[:, cols]
+
+    shapes = []
+    for head_lo, head_hi in chunks:
+        width = (head_hi - head_lo) * HD
+        shapes.append(jax.ShapeDtypeStruct((group_count, 2, tok_rows, width), queries.dtype))
+        shapes.append(jax.ShapeDtypeStruct((group_count, tok_rows, width), queries.dtype))
+    outs = pl.pallas_call(kernel, out_shape=tuple(shapes))(key_rows, value_rows, queries)
+    return [(outs[2 * n], outs[2 * n + 1]) for n in range(len(chunks))]
 
 
 def solution(mesh):

time: 153 us -> 163 us (1.065)
  blocking collectives: 102 us -> 115 us
  waiting for transfers between devices: 29.2 us -> 19.8 us
  starting transfers between devices: 4.29 us -> 7.74 us
  Pallas kernels: 12.6 us -> 14.8 us
    all_to_all x1, waiting for transfers between devices: 29.2 us -> 11.1 us  [body(): query_own = lax.all_to_all(query_groups, GROUP, 0, 0, tiled=True)]
    all_to_all x1 -> x2, blocking collectives: 35.1 us -> 45.9 us  [the longest x1 23.9 us: body(): lax.all_to_all(mixed_out.reshape(group_count, tok_rows, width), GROUP, 0,...]
    all_to_all x0 -> x1, waiting for transfers between devices: none -> 8.67 us  [body(): lax.all_to_all(mixed_out.reshape(group_count, tok_rows, width), GROUP, 0,...]
    all_to_all x0 -> x1, starting transfers between devices: none -> 3.5 us  [body(): lax.all_to_all(mixed_out.reshape(group_count, tok_rows, width), GROUP, 0,...]
    pallas_call x1 -> x2, Pallas kernels: 8.29 us -> 10.6 us  [attend(): pl.pallas_call(kernel, grid_spec=grid_spec, out_shape=jax.ShapeDtypeStruc...]
    all_to_all x1 -> x2, blocking collectives: 66.7 us -> 68.9 us  [body(): pair_mine = lax.all_to_all(pair_groups, GROUP, 0, 0, tiled=True)]
  transfers between devices with their start and end apart: 2 -> 4, of which waited for: 1 -> 2; matrix products, arithmetic and copies ran while one was open for 1% -> 2% of each run, Pallas kernels for 0% -> 7%
where the time goes in v13:
time: 163 us; the launch traced here: 162 us
  blocking collectives  115 us (71%)
  waiting for transfers between devices  19.8 us (12%)
  Pallas kernels  14.8 us (9%)
  starting transfers between devices  7.74 us (5%)
  local copies, waits for them, and re-layouts  4.72 us (3%)
    all_to_all x2, blocking collectives, body(): pair_mine = lax.all_to_all(pair_groups, GROUP, 0, 0, tiled=True)  68.9 us
    all_to_all x1, blocking collectives, body(): lax.all_to_all(mixed_out.reshape(group_count, tok_rows, width), GROUP, 0,...  23.9 us
    all_to_all x1, blocking collectives, body(): query_own = lax.all_to_all(query_groups, GROUP, 0, 0, tiled=True)  22 us
    all_to_all x1, waiting for transfers between devices, body(): query_own = lax.all_to_all(query_groups, GROUP, 0, 0, tiled=True)  11.1 us
    pallas_call x2, Pallas kernels, attend(): pl.pallas_call(kernel, grid_spec=grid_spec, out_shape=jax.ShapeDtypeStruc...  10.6 us
    all_to_all x1, waiting for transfers between devices, body(): lax.all_to_all(mixed_out.reshape(group_count, tok_rows, width), GROUP, 0,...  8.67 us
    pallas_call x1, Pallas kernels, regroup_in(): pl.pallas_call(kernel, out_shape=tuple(shapes))  4.23 us
    all_to_all x1, starting transfers between devices, body(): query_own = lax.all_to_all(query_groups, GROUP, 0, 0, tiled=True)  3.68 us
  transfers between devices with their start and end apart: 4, of which 2 were waited for; matrix products, arithmetic and copies ran while one was open for 2% of the time, Pallas kernels for 7%

profile of v13, /device:TPU:0, one launch (start us, length us, event | category | flops | bytes accessed | tf_op | source)
XLA Modules:
  0.0 162.0 jit_solution(14479801139026323279)
XLA Ops:
  0.0 4.2 %shard_map.55 = (bf16[8,2,128,384]{3,2,1,0:T(8,128)(2,1)}, bf16[8,128,384]{2,1,0:T(8,128)(2,1)}, bf16[8,2,128,256]{3,2,1,0:T(8,128)(2,1)}, bf16[8,128,256]{2,1,0:T(8,128)(2,1)}) custom-call(bf16[128,5120]{1,0:T(8,128)(2,1)} %k_ref.1, bf16[128,5120]{1,0:T(8,128)(2,1)} %v_ref.1, bf16[128,5120]{1,0:T(8,128)(2,1)} %q_ref.1), custom_call_target="tpu_custom_call" | custom-call | tf_op jit(solution)/shard_map/pallas_call | solution.py:201
  4.2 0.0 copy-start.4
  4.2 22.0 %all_to_all.30 = bf16[8,128,256]{2,1,0:T(8,128)(2,1)} all-to-all(bf16[8,128,256]{2,1,0:T(8,128)(2,1)} %get-tuple-element.11), channel_id=1, replica_groups=mesh['clips'=2,'seq'=4,'px'=2,'pc'=2] {'seq','px'}, dimensions={0} | all-to-all | bytes 1048576 | tf_op jit(solution)/shard_map/all_to_all | solution.py:67
  26.3 0.0 copy-start.3
  26.3 0.0 copy-done.4
  26.3 29.0 %all_to_all.31.mine_ref = bf16[8,2,128,256]{3,2,1,0:T(8,128)(2,1)S(1)} all-to-all(bf16[8,2,128,256]{3,2,1,0:T(8,128)(2,1)S(1)} %copy-done.4), channel_id=1, replica_groups=mesh['clips'=2,'seq'=4,'px'=2,'pc'=2] {'seq','px'}, dimensions={0} | all-to-all | bytes 2097152 | tf_op jit(solution)/shard_map/all_to_all | solution.py:61
  55.2 0.0 copy-start.1
  55.2 0.0 copy-done.3
  55.2 39.9 %all_to_all.32.mine_ref = bf16[8,2,128,384]{3,2,1,0:T(8,128)(2,1)S(1)} all-to-all(bf16[8,2,128,384]{3,2,1,0:T(8,128)(2,1)S(1)} %copy-done.3), channel_id=1, replica_groups=mesh['clips'=2,'seq'=4,'px'=2,'pc'=2] {'seq','px'}, dimensions={0} | all-to-all | bytes 3145728 | tf_op jit(solution)/shard_map/all_to_all | solution.py:61
  95.1 0.0 copy-start
  95.1 0.0 copy-start.5
  95.1 0.0 copy-start.6
  95.1 3.7 %all-to-all-start = ((bf16[8,128,384]{2,1,0:T(8,128)(2,1)}), bf16[8,128,384]{2,1,0:T(8,128)(2,1)S(1)}, u32[]{:S(2)}, u32[]{:S(2)}) async-start(bf16[8,128,384]{2,1,0:T(8,128)(2,1)} %get-tuple-element.9), calls=%async_computation | async-start | bytes 1572864 | tf_op jit(solution)/shard_map/all_to_all | solution.py:67
  98.8 0.0 copy-done.1
  98.8 0.1 collective-permute-start.1
  98.9 0.5 collective-permute-start
  99.4 0.0 copy-done.5
  99.4 0.9 copy.7
  100.4 1.8 %reshape.23.lists_ref = s32[1280]{0:T(1024)} reshape(s32[40,16,2]{2,1,0:T(8,128)} %copy.7) | data formatting | bytes 10240 | tf_op jit(solution)/shard_map/reshape | solution.py:69
  102.1 0.0 copy-done.6
  102.1 0.1 copy.8
  102.2 0.7 reshape.24.counts_ref
  102.9 0.0 collective-permute-done.1.other_ref
  102.9 4.6 %shard_map.57 = bf16[1024,256]{1,0:T(8,128)(2,1)} custom-call(s32[1280]{0:T(1024)} %reshape.23.lists_ref, s32[640]{0:T(1024)} %reshape.24.counts_ref, bf16[1024,256]{1,0:T(8,128)(2,1)} %bitcast.10, bf16[8,2,128,256]{3,2,1,0:T(8,128)(2,1)} %copy-done.1, bf16[8,2,128,256]{3,2,1,0:T(8,128)(2,1)} %collective-permute-done.1.other_ref), custom_call_target="tpu_custom_call" | custom-call | tf_op jit(solution)/shard_map/pallas_call | solution.py:177
  107.5 0.0 copy-done
  107.5 11.1 %all-to-all-done = bf16[8,128,384]{2,1,0:T(8,128)(2,1)S(1)} async-done(((bf16[8,128,384]{2,1,0:T(8,128)(2,1)}), bf16[8,128,384]{2,1,0:T(8,128)(2,1)S(1)}, u32[]{:S(2)}, u32[]{:S(2)}) %all-to-all-start) | async-done | bytes 786464 | tf_op jit(solution)/shard_map/all_to_all | solution.py:67
  118.6 0.0 copy-start.2
  118.6 3.5 %all-to-all-start.5 = ((bf16[8,128,256]{2,1,0:T(8,128)(2,1)}), bf16[8,128,256]{2,1,0:T(8,128)(2,1)S(1)}, u32[]{:S(2)}, u32[]{:S(2)}) async-start(bf16[8,128,256]{2,1,0:T(8,128)(2,1)} %bitcast.11), calls=%async_computation.5 | async-start | bytes 1048576 | tf_op jit(solution)/shard_map/all_to_all | solution.py:81
  122.1 0.0 collective-permute-done.other_ref
  122.1 0.0 copy-done.2
  122.1 6.0 %shard_map.56 = bf16[1024,384]{1,0:T(8,128)(2,1)} custom-call(s32[1280]{0:T(1024)} %reshape.23.lists_ref, s32[640]{0:T(1024)} %reshape.24.counts_ref, bf16[1024,384]{1,0:T(8,128)(2,1)} %bitcast.8, bf16[8,2,128,384]{3,2,1,0:T(8,128)(2,1)} %copy-done, bf16[8,2,128,384]{3,2,1,0:T(8,128)(2,1)} %collective-permute-done.other_ref), custom_call_target="tpu_custom_call" | custom-call | tf_op jit(solution)/shard_map/pallas_call | solution.py:177
  128.1 8.7 %all-to-all-done.5 = bf16[8,128,256]{2,1,0:T(8,128)(2,1)S(1)} async-done(((bf16[8,128,256]{2,1,0:T(8,128)(2,1)}), bf16[8,128,256]{2,1,0:T(8,128)(2,1)S(1)}, u32[]{:S(2)}, u32[]{:S(2)}) %all-to-all-start.5) | async-done | bytes 524320 | tf_op jit(solution)/shard_map/all_to_all | solution.py:81
  136.7 23.9 %all_to_all.33 = bf16[8,128,384]{2,1,0:T(8,128)(2,1)S(1)} all-to-all(bf16[8,128,384]{2,1,0:T(8,128)(2,1)} %bitcast.9), channel_id=1, replica_groups=mesh['clips'=2,'seq'=4,'px'=2,'pc'=2] {'seq','px'}, dimensions={0} | all-to-all | bytes 1572864 | tf_op jit(solution)/shard_map/all_to_all | solution.py:81
  160.7 0.2 maximum_bitcast_fusion
  160.8 1.2 copy.10
Async XLA Ops:
  4.2 22.0 %copy-start.4 = (bf16[8,2,128,256]{3,2,1,0:T(8,128)(2,1)S(1)}, bf16[8,2,128,256]{3,2,1,0:T(8,128)(2,1)}, u32[]{:S(2)}) copy-start(bf16[8,2,128,256]{3,2,1,0:T(8,128)(2,1)} %get-tuple-element.12) | copy-start | bytes 3145732
  26.3 29.0 %copy-start.3 = (bf16[8,2,128,384]{3,2,1,0:T(8,128)(2,1)S(1)}, bf16[8,2,128,384]{3,2,1,0:T(8,128)(2,1)}, u32[]{:S(2)}) copy-start(bf16[8,2,128,384]{3,2,1,0:T(8,128)(2,1)} %get-tuple-element.10) | copy-start | bytes 4718596
  55.2 43.6 %copy-start.1 = (bf16[8,2,128,256]{3,2,1,0:T(8,128)(2,1)}, bf16[8,2,128,256]{3,2,1,0:T(8,128)(2,1)S(1)}, u32[]{:S(2)}) copy-start(bf16[8,2,128,256]{3,2,1,0:T(8,128)(2,1)S(1)} %all_to_all.31.mine_ref) | copy-start | bytes 3145732
  95.1 12.3 %copy-start = (bf16[8,2,128,384]{3,2,1,0:T(8,128)(2,1)}, bf16[8,2,128,384]{3,2,1,0:T(8,128)(2,1)S(1)}, u32[]{:S(2)}) copy-start(bf16[8,2,128,384]{3,2,1,0:T(8,128)(2,1)S(1)} %all_to_all.32.mine_ref) | copy-start | bytes 4718596
  95.1 4.3 %copy-start.5 = (s32[40,16,2]{0,2,1:T(2,128)S(1)}, s32[40,16,2]{0,2,1:T(2,128)}, u32[]{:S(2)}) copy-start(s32[40,16,2]{0,2,1:T(2,128)} %param.8) | copy-start | bytes 15364
  95.1 7.0 %copy-start.6 = (s32[40,16]{0,1:T(8,128)S(1)}, s32[40,16]{0,1:T(8,128)}, u32[]{:S(2)}) copy-start(s32[40,16]{0,1:T(8,128)} %param.9) | copy-start | bytes 7684
  95.1 23.4 %all-to-all-start = ((bf16[8,128,384]{2,1,0:T(8,128)(2,1)}), bf16[8,128,384]{2,1,0:T(8,128)(2,1)S(1)}, u32[]{:S(2)}, u32[]{:S(2)}) async-start(bf16[8,128,384]{2,1,0:T(8,128)(2,1)} %get-tuple-element.9), calls=%async_computation | async-start | bytes 1572864 | tf_op jit(solution)/shard_map/all_to_all | solution.py:67
  98.8 4.0 %collective-permute-start.1 = (bf16[8,2,128,256]{3,2,1,0:T(8,128)(2,1)S(1)}, bf16[8,2,128,256]{3,2,1,0:T(8,128)(2,1)}, u32[]{:S(2)}, u32[]{:S(2)}) collective-permute-start(bf16[8,2,128,256]{3,2,1,0:T(8,128)(2,1)S(1)} %all_to_all.31.mine_ref), channel_id=1, source_target_pairs={{0,1},{1,0},{2,3},{3,2},{4,5},{5,4},{6,7},{7,6},{8,9},{9,8},{10,11... | collective-permute-start | bytes 3145736 | tf_op jit(solution)/shard_map/ppermute | solution.py:64
  98.9 23.2 %collective-permute-start = (bf16[8,2,128,384]{3,2,1,0:T(8,128)(2,1)S(1)}, bf16[8,2,128,384]{3,2,1,0:T(8,128)(2,1)}, u32[]{:S(2)}, u32[]{:S(2)}) collective-permute-start(bf16[8,2,128,384]{3,2,1,0:T(8,128)(2,1)S(1)} %all_to_all.32.mine_ref), channel_id=1, source_target_pairs={{0,1},{1,0},{2,3},{3,2},{4,5},{5,4},{6,7},{7,6},{8,9},{9,8},{10,11... | collective-permute-start | bytes 4718600 | tf_op jit(solution)/shard_map/ppermute | solution.py:64
  118.6 3.5 %copy-start.2 = (bf16[8,128,384]{2,1,0:T(8,128)(2,1)}, bf16[8,128,384]{2,1,0:T(8,128)(2,1)S(1)}, u32[]{:S(2)}) copy-start(bf16[8,128,384]{2,1,0:T(8,128)(2,1)S(1)} %all-to-all-done) | copy-start | bytes 2359300
  118.6 18.2 %all-to-all-start.5 = ((bf16[8,128,256]{2,1,0:T(8,128)(2,1)}), bf16[8,128,256]{2,1,0:T(8,128)(2,1)S(1)}, u32[]{:S(2)}, u32[]{:S(2)}) async-start(bf16[8,128,256]{2,1,0:T(8,128)(2,1)} %bitcast.11), calls=%async_computation.5 | async-start | bytes 1048576 | tf_op jit(solution)/shard_map/all_to_all | solution.py:81

commit v14 on v12

--- a/solution.py
+++ b/solution.py
@@ -76,74 +76,100 @@
     group_count, _, tok_rows, _ = pair_mine.shape
     local_blocks = tok_rows // BLOCK
 
-    def kernel(lists_ref, counts_ref, q_ref, mine_ref, other_ref, o_ref):
+    def kernel(lists_ref, counts_ref, q_hbm, mine_hbm, other_hbm, o_ref, q_buf, mine_buf, other_buf, sems):
         px_count = lax.axis_size("px")
         pc_count = lax.axis_size("pc")
         group_place = lax.axis_index("seq") * px_count + lax.axis_index("px")
         pc_place = lax.axis_index("pc")
-        head_id = group_place * heads_per + pl.program_id(0)
-        head_safe = jnp.minimum(head_id, HEADS - 1)
-
-        def per_block(i, carry):
-            query_block = (i // local_blocks * pc_count + pc_place) * local_blocks + i % local_blocks
-            slot = head_safe * block_total + query_block
-            visits = jnp.where(head_id < HEADS, counts_ref[slot], 0)
-            row = pl.multiple_of(i * BLOCK, BLOCK)
-            q = q_ref[pl.ds(row, BLOCK), :]
-            key_blocks = []
-            value_blocks = []
-            for j in range(max_visits):
-                picked = jnp.clip(lists_ref[slot * max_visits + j], 0, block_total - 1)
-                other = picked // local_blocks % pc_count != pc_place
-                source = picked // local_blocks // pc_count
-                held = source * local_blocks + picked % local_blocks
-                krow = pl.multiple_of(held % local_blocks * BLOCK, BLOCK)
-                key_blocks.append(
-                    jnp.where(
-                        other,
-                        other_ref[source, 0, pl.ds(krow, BLOCK), :],
-                        mine_ref[source, 0, pl.ds(krow, BLOCK), :],
+        loads = []
+        for head_local in range(heads_per):
+            cols = pl.ds(head_local * HD, HD)
+            routes = (
+                (q_hbm.at[:, cols], q_buf.at[head_local]),
+                (mine_hbm.at[:, :, :, cols], mine_buf.at[head_local]),
+                (other_hbm.at[:, :, :, cols], other_buf.at[head_local]),
+            )
+            head_loads = []
+            for n, (src_ref, dst_ref) in enumerate(routes):
+                copy = pltpu.make_async_copy(src_ref, dst_ref, sems.at[3 * head_local + n])
+                copy.start()
+                head_loads.append(copy)
+            loads.append(head_loads)
+
+        for head_local in range(heads_per):
+            for copy in loads[head_local]:
+                copy.wait()
+            cols = pl.ds(head_local * HD, HD)
+            q_ref = q_buf.at[head_local]
+            mine_ref = mine_buf.at[head_local]
+            other_ref = other_buf.at[head_local]
+            head_id = group_place * heads_per + head_local
+            head_safe = jnp.minimum(head_id, HEADS - 1)
+
+            def per_block(i, carry):
+                query_block = (
+                    i // local_blocks * pc_count + pc_place
+                ) * local_blocks + i % local_blocks
+                slot = head_safe * block_total + query_block
+                visits = jnp.where(head_id < HEADS, counts_ref[slot], 0)
+                row = pl.multiple_of(i * BLOCK, BLOCK)
+                q = q_ref[pl.ds(row, BLOCK), :]
+                key_blocks = []
+                value_blocks = []
+                for j in range(max_visits):
+                    picked = jnp.clip(lists_ref[slot * max_visits + j], 0, block_total - 1)
+                    other = picked // local_blocks % pc_count != pc_place
+                    source = picked // local_blocks // pc_count
+                    krow = pl.multiple_of(picked % local_blocks * BLOCK, BLOCK)
+                    key_blocks.append(
+                        jnp.where(
+                            other,
+                            other_ref[source, 0, pl.ds(krow, BLOCK), :],
+                            mine_ref[source, 0, pl.ds(krow, BLOCK), :],
+                        )
                     )
+                    value_blocks.append(
+                        jnp.where(
+                            other,
+                            other_ref[source, 1, pl.ds(krow, BLOCK), :],
+                            mine_ref[source, 1, pl.ds(krow, BLOCK), :],
+                        )
+                    )
+                s = lax.dot_general(
+                    q,
+                    jnp.concatenate(key_blocks, axis=0),
+                    (((1,), (1,)), ((), ())),
+                    preferred_element_type=jnp.float32,
                 )
-                value_blocks.append(
-                    jnp.where(
-                        other,
-                        other_ref[source, 1, pl.ds(krow, BLOCK), :],
-                        mine_ref[source, 1, pl.ds(krow, BLOCK), :],
-                    )
+                live = lax.broadcasted_iota(jnp.int32, s.shape, 1) < visits * BLOCK
+                s = jnp.where(live, s * score_scale, -jnp.inf)
+                row_max = jnp.max(s, axis=1, keepdims=True)
+                row_max = jnp.where(row_max > -jnp.inf, row_max, 0.0)
+                raised = jnp.exp(s - row_max)
+                total = jnp.sum(raised, axis=1, keepdims=True)
+                acc = jnp.dot(
+                    raised.astype(jnp.bfloat16),
+                    jnp.concatenate(value_blocks, axis=0),
+                    preferred_element_type=jnp.float32,
                 )
-            s = lax.dot_general(
-                q,
-                jnp.concatenate(key_blocks, axis=0),
-                (((1,), (1,)), ((), ())),
-                preferred_element_type=jnp.float32,
-            )
-            live = lax.broadcasted_iota(jnp.int32, s.shape, 1) < visits * BLOCK
-            s = jnp.where(live, s * score_scale, -jnp.inf)
-            row_max = jnp.max(s, axis=1, keepdims=True)
-            row_max = jnp.where(row_max > -jnp.inf, row_max, 0.0)
-            raised = jnp.exp(s - row_max)
-            total = jnp.sum(raised, axis=1, keepdims=True)
-            acc = jnp.dot(
-                raised.astype(jnp.bfloat16),
-                jnp.concatenate(value_blocks, axis=0),
-                preferred_element_type=jnp.float32,
-            )
-            total = jnp.where(total > 0.0, total, 1.0)
-            o_ref[pl.ds(row, BLOCK), :] = (acc / total).astype(o_ref.dtype)
-            return carry
-
-        lax.fori_loop(0, own_count, per_block, 0, unroll=min(own_count, 8))
-
+                total = jnp.where(total > 0.0, total, 1.0)
+                o_ref[pl.ds(row, BLOCK), cols] = (acc / total).astype(o_ref.dtype)
+                return carry
+
+            lax.fori_loop(0, own_count, per_block, 0, unroll=min(own_count, 8))
+
+    anywhere = pl.BlockSpec(memory_space=pl.ANY)
     grid_spec = pltpu.PrefetchScalarGridSpec(
         num_scalar_prefetch=2,
-        grid=(heads_per,),
-        in_specs=[
-            pl.BlockSpec((own_rows, HD), lambda h, *_: (0, h)),
-            pl.BlockSpec((group_count, 2, tok_rows, HD), lambda h, *_: (0, 0, 0, h)),
-            pl.BlockSpec((group_count, 2, tok_rows, HD), lambda h, *_: (0, 0, 0, h)),
+        grid=(1,),
+        in_specs=[anywhere, anywhere, anywhere],
+        out_specs=pl.BlockSpec(query_rows.shape, lambda h, *_: (0, 0)),
+        scratch_shapes=[
+            pltpu.VMEM((heads_per, own_rows, HD), query_rows.dtype),
+            pltpu.VMEM((heads_per, group_count, 2, tok_rows, HD), pair_mine.dtype),
+            pltpu.VMEM((heads_per, group_count, 2, tok_rows, HD), pair_mine.dtype),
+            pltpu.SemaphoreType.DMA((3 * heads_per,)),
         ],
-        out_specs=pl.BlockSpec((own_rows, HD), lambda h, *_: (0, h)),
     )
     return pl.pallas_call(
         kernel,

time: 153 us -> 152 us (level)
  no operation moved by 1% of the time
where the time goes in v14:
time: 152 us; the launch traced here: 151 us
  blocking collectives  102 us (67%)
  waiting for transfers between devices  29.2 us (19%)
  Pallas kernels  11.4 us (8%)
  local copies, waits for them, and re-layouts  4.54 us (3%)
  starting transfers between devices  4.29 us (3%)
    all_to_all x1, blocking collectives, body(): pair_mine = lax.all_to_all(pair_groups, GROUP, 0, 0, tiled=True)  66.7 us
    all_to_all x1, blocking collectives, body(): returned = lax.all_to_all(send_back, GROUP, 0, 0, tiled=True)  35.1 us
    all_to_all x1, waiting for transfers between devices, body(): query_own = lax.all_to_all(query_groups, GROUP, 0, 0, tiled=True)  29.2 us
    pallas_call x1, Pallas kernels, attend(): pl.pallas_call(kernel, grid_spec=grid_spec, out_shape=jax.ShapeDtypeStruc...  7.04 us
    pallas_call x1, Pallas kernels, regroup_in(): pl.pallas_call(kernel, out_shape=(jax.ShapeDtypeStruct((group_count, 2, t...  4.31 us
    all_to_all x1, starting transfers between devices, body(): query_own = lax.all_to_all(query_groups, GROUP, 0, 0, tiled=True)  4.28 us
  transfers between devices with their start and end apart: 2, of which 1 were waited for; matrix products, arithmetic and copies ran while one was open for 1% of the time, Pallas kernels for 0%

profile of v14, /device:TPU:0, one launch (start us, length us, event | category | flops | bytes accessed | tf_op | source)
XLA Modules:
  0.0 151.2 jit_solution(2093692707991781550)
XLA Ops:
  0.0 4.3 %shard_map.55 = (bf16[8,2,128,640]{3,2,1,0:T(8,128)(2,1)}, bf16[8,128,640]{2,1,0:T(8,128)(2,1)}) custom-call(bf16[128,5120]{1,0:T(8,128)(2,1)} %k_ref.1, bf16[128,5120]{1,0:T(8,128)(2,1)} %v_ref.1, bf16[128,5120]{1,0:T(8,128)(2,1)} %q_ref.1), custom_call_target="tpu_custom_call" | custom-call | tf_op jit(solution)/shard_map/pallas_call | solution.py:191
  4.3 66.7 %all_to_all.15.mine_hbm = bf16[8,2,128,640]{3,2,1,0:T(8,128)(2,1)S(1)} all-to-all(bf16[8,2,128,640]{3,2,1,0:T(8,128)(2,1)} %get-tuple-element.8), channel_id=1, replica_groups=mesh['clips'=2,'seq'=4,'px'=2,'pc'=2] {'seq','px'}, dimensions={0} | all-to-all | bytes 5242880 | tf_op jit(solution)/shard_map/all_to_all | solution.py:47
  71.0 0.0 copy-start
  71.0 0.0 collective-permute-start
  71.0 0.0 copy-start.2
  71.0 0.0 copy-start.1
  71.1 1.5 copy-done
  72.6 4.3 %all-to-all-start = ((bf16[8,128,640]{2,1,0:T(8,128)(2,1)}), bf16[8,128,640]{2,1,0:T(8,128)(2,1)}, u32[]{:S(2)}, u32[]{:S(2)}) async-start(bf16[8,128,640]{2,1,0:T(8,128)(2,1)} %get-tuple-element.7), calls=%async_computation | async-start | bytes 2621440 | tf_op jit(solution)/shard_map/all_to_all | solution.py:53
  76.9 0.0 copy-done.2
  76.9 0.1 copy.8
  76.9 0.7 reshape.16.counts_ref
  77.6 0.0 copy-done.1
  77.6 0.2 copy.7
  77.9 0.8 reshape.15.lists_ref
  78.7 29.2 %all-to-all-done = bf16[8,128,640]{2,1,0:T(8,128)(2,1)} async-done(((bf16[8,128,640]{2,1,0:T(8,128)(2,1)}), bf16[8,128,640]{2,1,0:T(8,128)(2,1)}, u32[]{:S(2)}, u32[]{:S(2)}) %all-to-all-start) | async-done | bytes 1310752 | tf_op jit(solution)/shard_map/all_to_all | solution.py:53
  107.8 0.0 collective-permute-done.other_hbm
  107.8 7.0 %shard_map.56 = bf16[1024,640]{1,0:T(8,128)(2,1)} custom-call(s32[1280]{0:T(1024)} %reshape.15.lists_ref, s32[640]{0:T(1024)} %reshape.16.counts_ref, bf16[1024,640]{1,0:T(8,128)(2,1)} %bitcast.q_hbm, bf16[8,2,128,640]{3,2,1,0:T(8,128)(2,1)} %copy-done, bf16[8,2,128,640]{3,2,1,0:T(8,128)(2,1)} %collective-permute-done.other_hbm), custom_call_target="tpu_custom_call" | custom-call | tf_op jit(solution)/shard_map/pallas_call | solution.py:174
  114.9 35.1 %all_to_all.16 = bf16[8,128,640]{2,1,0:T(8,128)(2,1)S(1)} all-to-all(bf16[8,128,640]{2,1,0:T(8,128)(2,1)} %bitcast.6), channel_id=1, replica_groups=mesh['clips'=2,'seq'=4,'px'=2,'pc'=2] {'seq','px'}, dimensions={0} | all-to-all | bytes 2621440 | tf_op jit(solution)/shard_map/all_to_all | solution.py:67
  150.0 1.2 copy.10
Async XLA Ops:
  71.0 1.5 %copy-start = (bf16[8,2,128,640]{3,2,1,0:T(8,128)(2,1)}, bf16[8,2,128,640]{3,2,1,0:T(8,128)(2,1)S(1)}, u32[]{:S(2)}) copy-start(bf16[8,2,128,640]{3,2,1,0:T(8,128)(2,1)S(1)} %all_to_all.15.mine_hbm) | copy-start | bytes 7864324
  71.0 36.8 %collective-permute-start = (bf16[8,2,128,640]{3,2,1,0:T(8,128)(2,1)S(1)}, bf16[8,2,128,640]{3,2,1,0:T(8,128)(2,1)}, u32[]{:S(2)}, u32[]{:S(2)}) collective-permute-start(bf16[8,2,128,640]{3,2,1,0:T(8,128)(2,1)S(1)} %all_to_all.15.mine_hbm), channel_id=1, source_target_pairs={{0,1},{1,0},{2,3},{3,2},{4,5},{5,4},{6,7},{7,6},{8,9},{9,8},{10,11... | collective-permute-start | bytes 7864328 | tf_op jit(solution)/shard_map/ppermute | solution.py:50
  71.0 5.8 %copy-start.2 = (s32[40,16]{0,1:T(8,128)S(1)}, s32[40,16]{0,1:T(8,128)}, u32[]{:S(2)}) copy-start(s32[40,16]{0,1:T(8,128)} %param.9) | copy-start | bytes 7684
  71.0 6.6 %copy-start.1 = (s32[40,16,2]{0,2,1:T(2,128)S(1)}, s32[40,16,2]{0,2,1:T(2,128)}, u32[]{:S(2)}) copy-start(s32[40,16,2]{0,2,1:T(2,128)} %param.8) | copy-start | bytes 15364
  72.6 35.3 %all-to-all-start = ((bf16[8,128,640]{2,1,0:T(8,128)(2,1)}), bf16[8,128,640]{2,1,0:T(8,128)(2,1)}, u32[]{:S(2)}, u32[]{:S(2)}) async-start(bf16[8,128,640]{2,1,0:T(8,128)(2,1)} %get-tuple-element.7), calls=%async_computation | async-start | bytes 2621440 | tf_op jit(solution)/shard_map/all_to_all | solution.py:53

commit v15 on v14

--- a/solution.py
+++ b/solution.py
@@ -181,19 +181,40 @@
 def regroup_in(key_rows, value_rows, queries, group_count, width):
     tok_rows = queries.shape[0]
 
-    def kernel(k_ref, v_ref, q_ref, pair_ref, query_ref):
-        for g in range(group_count):
-            cols = pl.ds(g * width, width)
-            pair_ref[g, 0] = k_ref[:, cols]
-            pair_ref[g, 1] = v_ref[:, cols]
-            query_ref[g] = q_ref[:, cols]
-
+    def kernel(k_hbm, v_hbm, q_hbm, pair_hbm, query_hbm, staged, sems):
+        loads = []
+        for n, src_ref in enumerate((k_hbm, v_hbm, q_hbm)):
+            copy = pltpu.make_async_copy(src_ref, staged.at[n], sems.at[n])
+            copy.start()
+            loads.append(copy)
+        stores = []
+        for n in range(3):
+            loads[n].wait()
+            for g in range(group_count):
+                dst_ref = query_hbm.at[g] if n == 2 else pair_hbm.at[g, n]
+                copy = pltpu.make_async_copy(
+                    staged.at[n, :, pl.ds(g * width, width)],
+                    dst_ref,
+                    sems.at[3 + n * group_count + g],
+                )
+                copy.start()
+                stores.append(copy)
+        for copy in stores:
+            copy.wait()
+
+    anywhere = pl.BlockSpec(memory_space=pl.ANY)
     return pl.pallas_call(
         kernel,
         out_shape=(
             jax.ShapeDtypeStruct((group_count, 2, tok_rows, width), queries.dtype),
             jax.ShapeDtypeStruct((group_count, tok_rows, width), queries.dtype),
         ),
+        in_specs=[anywhere, anywhere, anywhere],
+        out_specs=(anywhere, anywhere),
+        scratch_shapes=[
+            pltpu.VMEM((3,) + queries.shape, queries.dtype),
+            pltpu.SemaphoreType.DMA((3 + 3 * group_count,)),
+        ],
     )(key_rows, value_rows, queries)
 
 

time: 152 us -> 151 us (level)
  no operation moved by 1% of the time
where the time goes in v15:
time: 151 us; the launch traced here: 150 us
  blocking collectives  102 us (68%)
  waiting for transfers between devices  29.2 us (19%)
  Pallas kernels  10.5 us (7%)
  local copies, waits for them, and re-layouts  4.54 us (3%)
  starting transfers between devices  4.29 us (3%)
    all_to_all x1, blocking collectives, body(): pair_mine = lax.all_to_all(pair_groups, GROUP, 0, 0, tiled=True)  66.7 us
    all_to_all x1, blocking collectives, body(): returned = lax.all_to_all(send_back, GROUP, 0, 0, tiled=True)  35.1 us
    all_to_all x1, waiting for transfers between devices, body(): query_own = lax.all_to_all(query_groups, GROUP, 0, 0, tiled=True)  29.2 us
    pallas_call x1, Pallas kernels, attend(): pl.pallas_call(kernel, grid_spec=grid_spec, out_shape=jax.ShapeDtypeStruc...  7.04 us
    all_to_all x1, starting transfers between devices, body(): query_own = lax.all_to_all(query_groups, GROUP, 0, 0, tiled=True)  4.28 us
    pallas_call x1, Pallas kernels, regroup_in(): pl.pallas_call(kernel, out_shape=(jax.ShapeDtypeStruct((group_count, 2, t...  3.46 us
  transfers between devices with their start and end apart: 2, of which 1 were waited for; matrix products, arithmetic and copies ran while one was open for 1% of the time, Pallas kernels for 0%

profile of v15, /device:TPU:0, one launch (start us, length us, event | category | flops | bytes accessed | tf_op | source)
XLA Modules:
  0.0 150.4 jit_solution(3447102064182539014)
XLA Ops:
  0.0 3.5 %shard_map.55 = (bf16[8,2,128,640]{3,2,1,0:T(8,128)(2,1)}, bf16[8,128,640]{2,1,0:T(8,128)(2,1)}) custom-call(bf16[128,5120]{1,0:T(8,128)(2,1)} %k_hbm.1, bf16[128,5120]{1,0:T(8,128)(2,1)} %v_hbm.1, bf16[128,5120]{1,0:T(8,128)(2,1)} %q_hbm.1), custom_call_target="tpu_custom_call" | custom-call | tf_op jit(solution)/shard_map/pallas_call | solution.py:206
  3.5 66.7 %all_to_all.15.mine_hbm = bf16[8,2,128,640]{3,2,1,0:T(8,128)(2,1)S(1)} all-to-all(bf16[8,2,128,640]{3,2,1,0:T(8,128)(2,1)} %get-tuple-element.8), channel_id=1, replica_groups=mesh['clips'=2,'seq'=4,'px'=2,'pc'=2] {'seq','px'}, dimensions={0} | all-to-all | bytes 5242880 | tf_op jit(solution)/shard_map/all_to_all | solution.py:47
  70.2 0.0 copy-start
  70.2 0.0 collective-permute-start
  70.2 0.0 copy-start.2
  70.2 0.0 copy-start.1
  70.2 1.5 %copy-done = bf16[8,2,128,640]{3,2,1,0:T(8,128)(2,1)} copy-done((bf16[8,2,128,640]{3,2,1,0:T(8,128)(2,1)}, bf16[8,2,128,640]{3,2,1,0:T(8,128)(2,1)S(1)}, u32[]{:S(2)}) %copy-start) | copy-done | bytes 2621464
  71.7 4.3 %all-to-all-start = ((bf16[8,128,640]{2,1,0:T(8,128)(2,1)}), bf16[8,128,640]{2,1,0:T(8,128)(2,1)}, u32[]{:S(2)}, u32[]{:S(2)}) async-start(bf16[8,128,640]{2,1,0:T(8,128)(2,1)} %get-tuple-element.7), calls=%async_computation | async-start | bytes 2621440 | tf_op jit(solution)/shard_map/all_to_all | solution.py:53
  76.0 0.0 copy-done.2
  76.0 0.1 copy.8
  76.1 0.7 reshape.16.counts_ref
  76.8 0.0 copy-done.1
  76.8 0.2 copy.7
  77.0 0.8 reshape.15.lists_ref
  77.8 29.2 %all-to-all-done = bf16[8,128,640]{2,1,0:T(8,128)(2,1)} async-done(((bf16[8,128,640]{2,1,0:T(8,128)(2,1)}), bf16[8,128,640]{2,1,0:T(8,128)(2,1)}, u32[]{:S(2)}, u32[]{:S(2)}) %all-to-all-start) | async-done | bytes 1310752 | tf_op jit(solution)/shard_map/all_to_all | solution.py:53
  107.0 0.0 collective-permute-done.other_hbm
  107.0 7.0 %shard_map.56 = bf16[1024,640]{1,0:T(8,128)(2,1)} custom-call(s32[1280]{0:T(1024)} %reshape.15.lists_ref, s32[640]{0:T(1024)} %reshape.16.counts_ref, bf16[1024,640]{1,0:T(8,128)(2,1)} %bitcast.q_hbm, bf16[8,2,128,640]{3,2,1,0:T(8,128)(2,1)} %copy-done, bf16[8,2,128,640]{3,2,1,0:T(8,128)(2,1)} %collective-permute-done.other_hbm), custom_call_target="tpu_custom_call" | custom-call | tf_op jit(solution)/shard_map/pallas_call | solution.py:174
  114.0 35.1 %all_to_all.16 = bf16[8,128,640]{2,1,0:T(8,128)(2,1)S(1)} all-to-all(bf16[8,128,640]{2,1,0:T(8,128)(2,1)} %bitcast.6), channel_id=1, replica_groups=mesh['clips'=2,'seq'=4,'px'=2,'pc'=2] {'seq','px'}, dimensions={0} | all-to-all | bytes 2621440 | tf_op jit(solution)/shard_map/all_to_all | solution.py:67
  149.1 1.2 copy.10
Async XLA Ops:
  70.2 1.5 %copy-start = (bf16[8,2,128,640]{3,2,1,0:T(8,128)(2,1)}, bf16[8,2,128,640]{3,2,1,0:T(8,128)(2,1)S(1)}, u32[]{:S(2)}) copy-start(bf16[8,2,128,640]{3,2,1,0:T(8,128)(2,1)S(1)} %all_to_all.15.mine_hbm) | copy-start | bytes 7864324
  70.2 36.8 %collective-permute-start = (bf16[8,2,128,640]{3,2,1,0:T(8,128)(2,1)S(1)}, bf16[8,2,128,640]{3,2,1,0:T(8,128)(2,1)}, u32[]{:S(2)}, u32[]{:S(2)}) collective-permute-start(bf16[8,2,128,640]{3,2,1,0:T(8,128)(2,1)S(1)} %all_to_all.15.mine_hbm), channel_id=1, source_target_pairs={{0,1},{1,0},{2,3},{3,2},{4,5},{5,4},{6,7},{7,6},{8,9},{9,8},{10,11... | collective-permute-start | bytes 7864328 | tf_op jit(solution)/shard_map/ppermute | solution.py:50
  70.2 5.8 %copy-start.2 = (s32[40,16]{0,1:T(8,128)S(1)}, s32[40,16]{0,1:T(8,128)}, u32[]{:S(2)}) copy-start(s32[40,16]{0,1:T(8,128)} %param.9) | copy-start | bytes 7684
  70.2 6.6 %copy-start.1 = (s32[40,16,2]{0,2,1:T(2,128)S(1)}, s32[40,16,2]{0,2,1:T(2,128)}, u32[]{:S(2)}) copy-start(s32[40,16,2]{0,2,1:T(2,128)} %param.8) | copy-start | bytes 15364
  71.7 35.3 %all-to-all-start = ((bf16[8,128,640]{2,1,0:T(8,128)(2,1)}), bf16[8,128,640]{2,1,0:T(8,128)(2,1)}, u32[]{:S(2)}, u32[]{:S(2)}) async-start(bf16[8,128,640]{2,1,0:T(8,128)(2,1)} %get-tuple-element.7), calls=%async_computation | async-start | bytes 2621440 | tf_op jit(solution)/shard_map/all_to_all | solution.py:53

commit v16 on v15

--- a/solution.py
+++ b/solution.py
@@ -76,7 +76,9 @@
     group_count, _, tok_rows, _ = pair_mine.shape
     local_blocks = tok_rows // BLOCK
 
-    def kernel(lists_ref, counts_ref, q_hbm, mine_hbm, other_hbm, o_ref, q_buf, mine_buf, other_buf, sems):
+    def kernel(
+        lists_ref, counts_ref, q_hbm, mine_hbm, other_hbm, o_hbm, q_buf, mine_buf, other_buf, o_buf, sems
+    ):
         px_count = lax.axis_size("px")
         pc_count = lax.axis_size("pc")
         group_place = lax.axis_index("seq") * px_count + lax.axis_index("px")
@@ -96,10 +98,12 @@
                 head_loads.append(copy)
             loads.append(head_loads)
 
+        stores = []
         for head_local in range(heads_per):
             for copy in loads[head_local]:
                 copy.wait()
             cols = pl.ds(head_local * HD, HD)
+            o_ref = o_buf.at[head_local]
             q_ref = q_buf.at[head_local]
             mine_ref = mine_buf.at[head_local]
             other_ref = other_buf.at[head_local]
@@ -153,22 +157,30 @@
                     preferred_element_type=jnp.float32,
                 )
                 total = jnp.where(total > 0.0, total, 1.0)
-                o_ref[pl.ds(row, BLOCK), cols] = (acc / total).astype(o_ref.dtype)
+                o_ref[pl.ds(row, BLOCK), :] = (acc / total).astype(o_ref.dtype)
                 return carry
 
             lax.fori_loop(0, own_count, per_block, 0, unroll=min(own_count, 8))
+            store = pltpu.make_async_copy(
+                o_buf.at[head_local], o_hbm.at[:, cols], sems.at[3 * heads_per + head_local]
+            )
+            store.start()
+            stores.append(store)
+        for store in stores:
+            store.wait()
 
     anywhere = pl.BlockSpec(memory_space=pl.ANY)
     grid_spec = pltpu.PrefetchScalarGridSpec(
         num_scalar_prefetch=2,
         grid=(1,),
         in_specs=[anywhere, anywhere, anywhere],
-        out_specs=pl.BlockSpec(query_rows.shape, lambda h, *_: (0, 0)),
+        out_specs=anywhere,
         scratch_shapes=[
             pltpu.VMEM((heads_per, own_rows, HD), query_rows.dtype),
             pltpu.VMEM((heads_per, group_count, 2, tok_rows, HD), pair_mine.dtype),
             pltpu.VMEM((heads_per, group_count, 2, tok_rows, HD), pair_mine.dtype),
-            pltpu.SemaphoreType.DMA((3 * heads_per,)),
+            pltpu.VMEM((heads_per, own_rows, HD), query_rows.dtype),
+            pltpu.SemaphoreType.DMA((4 * heads_per,)),
         ],
     )
     return pl.pallas_call(

time: 151 us -> 150 us (level)
  no operation moved by 1% of the time
where the time goes in v16:
time: 150 us
  blocking collectives  102 us (68%)
  waiting for transfers between devices  29.2 us (19%)
  Pallas kernels  10.2 us (7%)
  local copies, waits for them, and re-layouts  4.54 us (3%)
  starting transfers between devices  4.29 us (3%)
    all_to_all x1, blocking collectives, body(): pair_mine = lax.all_to_all(pair_groups, GROUP, 0, 0, tiled=True)  66.7 us
    all_to_all x1, blocking collectives, body(): returned = lax.all_to_all(send_back, GROUP, 0, 0, tiled=True)  35.1 us
    all_to_all x1, waiting for transfers between devices, body(): query_own = lax.all_to_all(query_groups, GROUP, 0, 0, tiled=True)  29.2 us
    pallas_call x1, Pallas kernels, attend(): pl.pallas_call(kernel, grid_spec=grid_spec, out_shape=jax.ShapeDtypeStruc...  6.72 us
    all_to_all x1, starting transfers between devices, body(): query_own = lax.all_to_all(query_groups, GROUP, 0, 0, tiled=True)  4.28 us
    pallas_call x1, Pallas kernels, regroup_in(): pl.pallas_call(kernel, out_shape=(jax.ShapeDtypeStruct((group_count, 2, t...  3.46 us
  transfers between devices with their start and end apart: 2, of which 1 were waited for; matrix products, arithmetic and copies ran while one was open for 1% of the time, Pallas kernels for 0%

profile of v16, /device:TPU:0, one launch (start us, length us, event | category | flops | bytes accessed | tf_op | source)
XLA Modules:
  0.0 150.0 jit_solution(1677979259169636135)
XLA Ops:
  0.0 3.5 %shard_map.55 = (bf16[8,2,128,640]{3,2,1,0:T(8,128)(2,1)}, bf16[8,128,640]{2,1,0:T(8,128)(2,1)}) custom-call(bf16[128,5120]{1,0:T(8,128)(2,1)} %k_hbm.1, bf16[128,5120]{1,0:T(8,128)(2,1)} %v_hbm.1, bf16[128,5120]{1,0:T(8,128)(2,1)} %q_hbm.1), custom_call_target="tpu_custom_call" | custom-call | tf_op jit(solution)/shard_map/pallas_call | solution.py:218
  3.5 66.7 %all_to_all.15.mine_hbm = bf16[8,2,128,640]{3,2,1,0:T(8,128)(2,1)S(1)} all-to-all(bf16[8,2,128,640]{3,2,1,0:T(8,128)(2,1)} %get-tuple-element.8), channel_id=1, replica_groups=mesh['clips'=2,'seq'=4,'px'=2,'pc'=2] {'seq','px'}, dimensions={0} | all-to-all | bytes 5242880 | tf_op jit(solution)/shard_map/all_to_all | solution.py:47
  70.2 0.0 copy-start
  70.2 0.0 collective-permute-start
  70.2 0.0 copy-start.2
  70.2 0.0 copy-start.1
  70.2 1.5 %copy-done = bf16[8,2,128,640]{3,2,1,0:T(8,128)(2,1)} copy-done((bf16[8,2,128,640]{3,2,1,0:T(8,128)(2,1)}, bf16[8,2,128,640]{3,2,1,0:T(8,128)(2,1)S(1)}, u32[]{:S(2)}) %copy-start) | copy-done | bytes 2621464
  71.7 4.3 %all-to-all-start = ((bf16[8,128,640]{2,1,0:T(8,128)(2,1)}), bf16[8,128,640]{2,1,0:T(8,128)(2,1)}, u32[]{:S(2)}, u32[]{:S(2)}) async-start(bf16[8,128,640]{2,1,0:T(8,128)(2,1)} %get-tuple-element.7), calls=%async_computation | async-start | bytes 2621440 | tf_op jit(solution)/shard_map/all_to_all | solution.py:53
  76.0 0.0 copy-done.2
  76.0 0.1 copy.8
  76.1 0.7 reshape.16.counts_ref
  76.8 0.0 copy-done.1
  76.8 0.2 copy.7
  77.0 0.8 reshape.15.lists_ref
  77.8 29.2 %all-to-all-done = bf16[8,128,640]{2,1,0:T(8,128)(2,1)} async-done(((bf16[8,128,640]{2,1,0:T(8,128)(2,1)}), bf16[8,128,640]{2,1,0:T(8,128)(2,1)}, u32[]{:S(2)}, u32[]{:S(2)}) %all-to-all-start) | async-done | bytes 1310752 | tf_op jit(solution)/shard_map/all_to_all | solution.py:53
  107.0 0.0 collective-permute-done.other_hbm
  107.0 6.7 %shard_map.56 = bf16[1024,640]{1,0:T(8,128)(2,1)} custom-call(s32[1280]{0:T(1024)} %reshape.15.lists_ref, s32[640]{0:T(1024)} %reshape.16.counts_ref, bf16[1024,640]{1,0:T(8,128)(2,1)} %bitcast.q_hbm, bf16[8,2,128,640]{3,2,1,0:T(8,128)(2,1)} %copy-done, bf16[8,2,128,640]{3,2,1,0:T(8,128)(2,1)} %collective-permute-done.other_hbm), custom_call_target="tpu_custom_call" | custom-call | tf_op jit(solution)/shard_map/pallas_call | solution.py:186
  113.7 35.1 %all_to_all.16 = bf16[8,128,640]{2,1,0:T(8,128)(2,1)S(1)} all-to-all(bf16[8,128,640]{2,1,0:T(8,128)(2,1)} %bitcast.6), channel_id=1, replica_groups=mesh['clips'=2,'seq'=4,'px'=2,'pc'=2] {'seq','px'}, dimensions={0} | all-to-all | bytes 2621440 | tf_op jit(solution)/shard_map/all_to_all | solution.py:67
  148.8 1.2 copy.10
Async XLA Ops:
  70.2 1.5 %copy-start = (bf16[8,2,128,640]{3,2,1,0:T(8,128)(2,1)}, bf16[8,2,128,640]{3,2,1,0:T(8,128)(2,1)S(1)}, u32[]{:S(2)}) copy-start(bf16[8,2,128,640]{3,2,1,0:T(8,128)(2,1)S(1)} %all_to_all.15.mine_hbm) | copy-start | bytes 7864324
  70.2 36.8 %collective-permute-start = (bf16[8,2,128,640]{3,2,1,0:T(8,128)(2,1)S(1)}, bf16[8,2,128,640]{3,2,1,0:T(8,128)(2,1)}, u32[]{:S(2)}, u32[]{:S(2)}) collective-permute-start(bf16[8,2,128,640]{3,2,1,0:T(8,128)(2,1)S(1)} %all_to_all.15.mine_hbm), channel_id=1, source_target_pairs={{0,1},{1,0},{2,3},{3,2},{4,5},{5,4},{6,7},{7,6},{8,9},{9,8},{10,11... | collective-permute-start | bytes 7864328 | tf_op jit(solution)/shard_map/ppermute | solution.py:50
  70.2 5.8 %copy-start.2 = (s32[40,16]{0,1:T(8,128)S(1)}, s32[40,16]{0,1:T(8,128)}, u32[]{:S(2)}) copy-start(s32[40,16]{0,1:T(8,128)} %param.9) | copy-start | bytes 7684
  70.2 6.6 %copy-start.1 = (s32[40,16,2]{0,2,1:T(2,128)S(1)}, s32[40,16,2]{0,2,1:T(2,128)}, u32[]{:S(2)}) copy-start(s32[40,16,2]{0,2,1:T(2,128)} %param.8) | copy-start | bytes 15364
  71.7 35.3 %all-to-all-start = ((bf16[8,128,640]{2,1,0:T(8,128)(2,1)}), bf16[8,128,640]{2,1,0:T(8,128)(2,1)}, u32[]{:S(2)}, u32[]{:S(2)}) async-start(bf16[8,128,640]{2,1,0:T(8,128)(2,1)} %get-tuple-element.7), calls=%async_computation | async-start | bytes 2621440 | tf_op jit(solution)/shard_map/all_to_all | solution.py:53
